TPU v7x, 128 devices: a whole 4x4x4 slice. The times are simulated.
128 devices in a mesh: scan: 8 (over z, x_lo), det: 16 (over y, x_hi, core).
Axes of the slice: x: 4 (x_hi: 2, x_lo: 2; x = x_hi * 2 + x_lo), y: 4, z: 4, core: 2. Of those that a mesh axis runs over, the one named last changes fastest.
Arguments:
- frames: bfloat16 [16, 1024, 16384], P('det', 'scan'), may hold values from -6 to 6
- offsets: int32 [16384, 2], P(('scan', 'det')), may hold values from -32 to 32
- bright: int32 [16384], P(('scan', 'det')), may hold values from 0 to 1, as said below
- aberration: float32 [2], replicated, may hold values from 0.5 to 2
Outputs:
- tiles: float32 [16, 8, 160], P('det', 'scan')
Inputs may be any that keep to these rules, and one draw needn't show every extreme that they name: bright[k] is 1 exactly where (k // 128 - a)^2 + (k % 128 - b)^2 <= R^2 and 0 elsewhere, for one centre with whole a in 62 .. 66 and whole b in 62 .. 66, and one whole radius R in 40 .. 56, all ranges inclusive; so at least one pixel is 1.
All inputs are finite; a program needn't handle non-finite values.
Results may differ from a plain program's by a relative error of at most 0.0023.
Values may be sent and summed in bfloat16 or wider, within the bound.
No kernel may reach another device: no remote copies, remote signals or barrier semaphores. Data moves between devices by JAX's collectives and lax.ppermute only.
A program may use at most 128 MiB of HBM per device.

v0:
```python
import math

import jax
import jax.numpy as jnp
from jax import lax
from jax.sharding import PartitionSpec as P
from jax.experimental import pallas as pl

SR = 16
SC = 1024
DROWS = 128
DCOLS = 128
HALO = 16


TWO_PI = 2.0 * math.pi
EXACT_PRECISION = lax.Precision.HIGHEST


def phase_angles(first, second_operand, modulus):
    product = jnp.mod(first[:, None] * second_operand[None, :], modulus)
    return TWO_PI / modulus * product.astype(jnp.float32)


def signed_frequency(length):
    position = jnp.arange(length, dtype=jnp.int32)
    folded = jnp.where(position < length // 2, position, position - length)
    return 2.0 * folded.astype(jnp.float32) / length


def pixel_phase(pixel_index, shifts, aberration):
    freq_rows = signed_frequency(SR)[:, None, None]
    freq_cols = signed_frequency(SC)[None, :, None]
    half_rows = DROWS // 2
    half_cols = DCOLS // 2
    tilt_x = ((pixel_index // DCOLS - half_rows).astype(jnp.float32) / half_rows)[None, None, :]
    tilt_y = ((pixel_index % DCOLS - half_cols).astype(jnp.float32) / half_cols)[None, None, :]
    ramp_rows = jnp.mod(jnp.arange(SR, dtype=jnp.int32)[:, None] * shifts[:, 0][None, :], SR)
    ramp_cols = jnp.mod(jnp.arange(SC, dtype=jnp.int32)[:, None] * shifts[:, 1][None, :], SC)
    shift_phase = (
        TWO_PI / SR * ramp_rows.astype(jnp.float32)[:, None, :]
        + TWO_PI / SC * ramp_cols.astype(jnp.float32)[None, :, :]
    )
    tilt_sq = tilt_x * tilt_x + tilt_y * tilt_y
    tilt_dot = tilt_x * freq_rows + tilt_y * freq_cols
    moved_x = freq_rows + tilt_x
    moved_y = freq_cols + tilt_y
    moved_sq = moved_x * moved_x + moved_y * moved_y
    lens_phase = math.pi * (
        aberration[0] * (freq_rows * freq_rows + freq_cols * freq_cols)
        + aberration[1] * (moved_sq * moved_sq - tilt_sq * tilt_sq - 4.0 * tilt_sq * tilt_dot)
    )
    return shift_phase - lens_phase


def window_weights(width):
    position = jnp.arange(width, dtype=jnp.int32)
    nearest = jnp.minimum(position, width - 1 - position)
    ramped = 0.3 + 0.35 * (
        1.0 - jnp.cos(math.pi * (nearest.astype(jnp.float32) + 0.5) / (2 * HALO))
    )
    return jnp.where(nearest < 2 * HALO, ramped, jnp.float32(1.0))


def inverse_transform(spec_real, spec_imag, columns, rows):
    real_piece = jnp.dot(spec_real, cos_cols, precision=EXACT_PRECISION) - jnp.dot(
        spec_imag, sin_cols, precision=EXACT_PRECISION
    )
    imaginary_piece = jnp.dot(spec_real, sin_cols, precision=EXACT_PRECISION) + jnp.dot(
        spec_imag, cos_cols, precision=EXACT_PRECISION
    )
    angles_by_row = phase_angles(jnp.arange(SR, dtype=jnp.int32), rows, SR)
    row_cosines = jnp.cos(angles_by_row)
    row_sines = jnp.sin(angles_by_row)
    return jnp.dot(row_cosines.T, real_piece, precision=EXACT_PRECISION) - jnp.dot(
        row_sines.T, imaginary_piece, precision=EXACT_PRECISION
    )


def sincos_reduced(rest, quadrant):
    square = rest * rest
    sine = rest + rest * square * (
        -1.6666654611e-1 + square * (8.3321608736e-3 + square * -1.9515295891e-4)
    )
    cosine = 1.0 - 0.5 * square + square * square * (
        4.166664568298827e-2 + square * (-1.388731625493765e-3 + square * 2.443315711809948e-5)
    )
    swap = (quadrant & 1) == 1
    sin_out = jnp.where(swap, cosine, sine)
    cos_out = jnp.where(swap, sine, cosine)
    sin_out = jnp.where(quadrant >= 2, -sin_out, sin_out)
    cos_out = jnp.where((quadrant == 1) | (quadrant == 2), -cos_out, cos_out)
    return sin_out, cos_out


def sincos(angle):
    turns = jnp.round(angle * (2.0 / math.pi))
    quadrant = turns.astype(jnp.int32) & 3
    rest = angle - turns * 1.5703125
    rest = rest - turns * 4.837512969970703125e-4
    rest = rest - turns * 7.54978995489188216e-8
    return sincos_reduced(rest, quadrant)


def sincos_of_steps(steps, modulus):
    quarter = modulus // 4
    turns = (steps + quarter // 2) // quarter
    rest = (steps - turns * quarter).astype(jnp.float32) * (TWO_PI / modulus)
    return sincos_reduced(rest, turns & 3)


def exchange(values, axes, count, low, bits, rows):
    digit = (lax.axis_index(axes) >> low) & ((1 << bits) - 1)
    kept = lax.dynamic_index_in_dim(rows(values), digit, axis=1, keepdims=False)
    for d in range(1, 1 << bits):
        sent = lax.dynamic_index_in_dim(rows(values), digit ^ d, axis=1, keepdims=False)
        kept = kept + lax.ppermute(sent, axes, [(i, i ^ (d << low)) for i in range(count)])
    return kept


def phase_parts(pixel_index, shifts, aberration):
    freq_rows = signed_frequency(SR)[:, None]
    freq_cols = signed_frequency(SC)[:, None]
    half_rows = DROWS // 2
    half_cols = DCOLS // 2
    tilt_x = ((pixel_index // DCOLS - half_rows).astype(jnp.float32) / half_rows)[None, :]
    tilt_y = ((pixel_index % DCOLS - half_cols).astype(jnp.float32) / half_cols)[None, :]
    ramp_rows = jnp.mod(jnp.arange(SR, dtype=jnp.int32)[:, None] * shifts[:, 0][None, :], SR)
    ramp_cols = jnp.mod(jnp.arange(SC, dtype=jnp.int32)[:, None] * shifts[:, 1][None, :], SC)
    tilt_sq = tilt_x * tilt_x + tilt_y * tilt_y
    defocus = math.pi * aberration[0]
    spherical = math.pi * aberration[1]
    row_part = (
        TWO_PI / SR * ramp_rows.astype(jnp.float32)
        - defocus * freq_rows * freq_rows
        + spherical * (tilt_sq * tilt_sq + 4.0 * tilt_sq * tilt_x * freq_rows)
    )
    col_part = (
        TWO_PI / SC * ramp_cols.astype(jnp.float32)
        - defocus * freq_cols * freq_cols
        + spherical * (4.0 * tilt_sq * tilt_y * freq_cols)
    )
    moved_rows = (freq_rows + tilt_x) * (freq_rows + tilt_x)
    moved_cols = (freq_cols + tilt_y) * (freq_cols + tilt_y)
    return row_part, col_part, moved_rows, moved_cols, spherical


def four_point(points):
    (ar, ai), (br, bi), (cr, ci), (dr, di) = points
    s02r = ar + cr
    s02i = ai + ci
    d02r = ar - cr
    d02i = ai - ci
    s13r = br + dr
    s13i = bi + di
    d13r = br - dr
    d13i = bi - di
    return [
        (s02r + s13r, s02i + s13i),
        (d02r + d13i, d02i - d13r),
        (s02r - s13r, s02i - s13i),
        (d02r - d13i, d02i + d13r),
    ]


def fft16(points):
    twisted = {}
    for b in range(4):
        column = four_point([points[4 * a + b] for a in range(4)])
        for s1, (gr, gi) in enumerate(column):
            k = b * s1
            if k == 0:
                twisted[b, s1] = (gr, gi)
            elif k == 4:
                twisted[b, s1] = (gi, -gr)
            else:
                c = math.cos(TWO_PI * k / 16)
                d = math.sin(TWO_PI * k / 16)
                twisted[b, s1] = (gr * c + gi * d, gi * c - gr * d)
    out = [None] * 16
    for s1 in range(4):
        row = four_point([twisted[b, s1] for b in range(4)])
        for s2 in range(4):
            out[s1 + 4 * s2] = row[s2]
    return out


def spectrum_kernel(re_ref, im_ref, tc_ref, ts_ref, out_ref):
    out_ref[...] = jnp.zeros(out_ref.shape, out_ref.dtype)

    def body(i, carry):
        rows = pl.ds(pl.multiple_of(i * 8, 8), 8)
        full = fft16([(re_ref[r, rows, :], im_ref[r, rows, :]) for r in range(SR)])
        for s in range(SR):
            fr, fi = full[s]
            tc = tc_ref[s, rows, :]
            ts = ts_ref[s, rows, :]
            out_ref[0, s] += fr * tc - fi * ts
            out_ref[1, s] += fr * ts + fi * tc
        return carry

    lax.fori_loop(0, re_ref.shape[1] // 8, body, 0)


def spectrum(both_col, turn_cos, turn_sin):
    pixels = both_col.shape[1]
    block = 128
    steps = SC // block
    spec = pl.pallas_call(
        spectrum_kernel,
        grid=(steps,),
        in_specs=[
            pl.BlockSpec((SR, pixels, block), lambda j: (0, 0, j)),
            pl.BlockSpec((SR, pixels, block), lambda j: (0, 0, j + steps)),
            pl.BlockSpec((SR, pixels, block), lambda j: (0, 0, j)),
            pl.BlockSpec((SR, pixels, block), lambda j: (0, 0, j)),
        ],
        out_specs=pl.BlockSpec((2, SR, 8, block), lambda j: (0, 0, 0, j)),
        out_shape=jax.ShapeDtypeStruct((2, SR, 8, SC), jnp.float32),
    )(both_col, both_col, turn_cos, turn_sin)
    return jnp.sum(spec, axis=2)


def local(frames, offsets, bright, aberration):
    scan_size = lax.axis_size("scan")
    det_size = lax.axis_size("det")
    rows_dev, tile, detector = frames.shape
    owned = offsets.shape[0]
    groups = detector // owned
    owner = lax.axis_index("scan") * det_size + lax.axis_index("det")
    blocks = jnp.transpose(frames.reshape(rows_dev * tile, groups, owned), (1, 0, 2))
    arrived = lax.all_to_all(blocks, ("scan", "det"), split_axis=0, concat_axis=0, tiled=True)
    images = arrived.reshape(scan_size, det_size, rows_dev, tile, owned)
    full_cols = jnp.arange(SC, dtype=jnp.int32)
    col_sin, col_cos = sincos_of_steps(jnp.mod(full_cols[:, None] * full_cols[None, :], SC), SC)
    col_cos = col_cos.astype(jnp.bfloat16)
    col_sin = col_sin.astype(jnp.bfloat16)
    table = jnp.concatenate([col_cos, -col_sin], axis=1).reshape(scan_size, tile, 2 * SC)
    both_col = jnp.einsum(
        "abrcp,acq->brpq", images, table, preferred_element_type=jnp.float32
    ).reshape(SR, owned, 2 * SC)
    full_rows = jnp.arange(SR, dtype=jnp.int32)
    angles_by_row = phase_angles(full_rows, full_rows, SR)
    row_cos = jnp.cos(angles_by_row)
    row_sin = jnp.sin(angles_by_row)
    pixel_index = owner * owned + jnp.arange(owned, dtype=jnp.int32)
    row_part, col_part, moved_rows, moved_cols, spherical = phase_parts(
        pixel_index, offsets, aberration
    )
    moved_sq = moved_rows[:, :, None] + moved_cols.T[None, :, :]
    phase = row_part[:, :, None] + col_part.T[None, :, :] - spherical * (moved_sq * moved_sq)
    weights = bright.astype(jnp.float32)
    turn_sin, turn_cos = sincos(phase)
    turn_cos, turn_sin = lax.optimization_barrier(
        (turn_cos * weights[None, :, None], turn_sin * weights[None, :, None])
    )
    spec_real, spec_imag = spectrum(both_col, turn_cos, turn_sin)
    row_cos_t = row_cos.T
    row_sin_t = row_sin.T
    rows_real = jnp.dot(row_cos_t, spec_real, precision=EXACT_PRECISION) - jnp.dot(
        row_sin_t, spec_imag, precision=EXACT_PRECISION
    )
    rows_imag = jnp.dot(row_sin_t, spec_real, precision=EXACT_PRECISION) + jnp.dot(
        row_cos_t, spec_imag, precision=EXACT_PRECISION
    )
    packed = jnp.concatenate(
        [rows_real, rows_imag, jnp.broadcast_to(jnp.sum(weights), (SR, 128))], axis=1
    )
    width = tile + 2 * HALO
    columns = jnp.mod(
        lax.axis_index("scan") * tile - HALO + jnp.arange(width, dtype=jnp.int32), SC
    )
    col_angles = phase_angles(jnp.arange(SC, dtype=jnp.int32), columns, SC)
    cos_cols, sin_cols = lax.optimization_barrier((jnp.cos(col_angles), jnp.sin(col_angles)))
    axes = ("scan", "det")
    count = scan_size * det_size
    quarters = packed.reshape(4, 4, packed.shape[1])
    partial = exchange(quarters, axes, count, 0, 2, lambda x: x)
    own = exchange(partial, axes, count, 2, 2, lambda x: x.reshape(1, 4, x.shape[1]))
    own = own.reshape(-1)
    partners = [own] + [
        lax.ppermute(own, axes, [(i, i ^ (d << 4)) for i in range(count)]) for d in range(1, 8)
    ]
    while len(partners) > 1:
        partners = [partners[e] + partners[e + 1] for e in range(0, len(partners), 2)]
    total = partners[0]
    line_real = total[:SC]
    line_imag = total[SC : 2 * SC]
    bright_sum = total[2 * SC]
    picture = jnp.dot(line_real, cos_cols, precision=EXACT_PRECISION) - jnp.dot(
        line_imag, sin_cols, precision=EXACT_PRECISION
    )
    return (
        (picture * (1.0 / (SR * SC)) / jnp.sqrt(bright_sum) * window_weights(width))
        .reshape(rows_dev, 1, width)
    )


def solution(mesh):
    placed = (P("det", "scan", None), P(("scan", "det"), None), P(("scan", "det")), P())
    return jax.shard_map(
        local, mesh=mesh, in_specs=placed, out_specs=P("det", "scan", None), check_vma=False
    )
```

profile of v0, /device:TPU:0, one launch (start us, length us, event | category | flops | bytes accessed | tf_op | source)
XLA Modules:
  0.0 134.3 jit_solution(11767085908386271901)
XLA Ops:
  0.0 6.4 %copy.8 = bf16[1,128,16384]{1,2,0:T(8,128)(2,1)} copy(bf16[1,128,16384]{2,1,0:T(8,128)(2,1)} %param.4) | data formatting | bytes 8388608 | tf_op args[0]
  6.4 11.7 %all-to-all-start = ((bf16[128,128,128]{1,2,0:T(8,128)(2,1)}), bf16[128,128,128]{1,2,0:T(8,128)(2,1)}, u32[]{:S(2)}, u32[]{:S(2)}) async-start(bf16[128,128,128]{1,2,0:T(8,128)(2,1)} %bitcast.56), calls=%async_computation | async-start | bytes 8388608 | tf_op jit(solution)/shard_map/all_to_all | solution.py:232
  18.2 0.7 fusion.103
  21.4 14.2 %fusion.10 = (f32[16,128,1024]{2,1,0:T(8,128)}, f32[16,128,1024]{2,1,0:T(8,128)}) fusion(f32[128]{0:T(128)S(1)} %convert_element_type.126, f32[128,1024]{1,0:T(8,128)S(1)} %get-tuple-element.25, f32[16,128]{1,0:T(8,128)S(1)} %get-tuple-element.31, f32[]{:T(128)} %bitcast.8, f32[128,1024]{1,0:T(8,128)S(1)} %get-tuple-element.24, ...), kind=kLoop, calls=%fused_computation.19 | loop fusion | flops 96468992 | bytes 17842692 | tf_op jit(solution)/shard_map/mul | solution.py:255
  36.9 8.3 %fusion.36 = bf16[8,128,1024]{1,2,0:T(8,128)(2,1)S(1)} fusion(s32[8,128]{1,0:T(8,128)S(1)} %multiply_add_fusion), kind=kLoop, calls=%fused_computation.70 | loop fusion | flops 62914560 | bytes 2101248 | tf_op jit(solution)/shard_map/neg | solution.py:238
  45.2 9.1 %fusion.26 = bf16[8,128,1024]{1,2,0:T(8,128)(2,1)} fusion(s32[8,128]{1,0:T(8,128)S(1)} %multiply_add_fusion), kind=kLoop, calls=%fused_computation.57 | loop fusion | flops 61865984 | bytes 2101248 | tf_op jit(solution)/shard_map/convert_element_type | solution.py:236
  54.3 15.4 %all-to-all-done = bf16[128,128,128]{1,2,0:T(8,128)(2,1)} async-done(((bf16[128,128,128]{1,2,0:T(8,128)(2,1)}), bf16[128,128,128]{1,2,0:T(8,128)(2,1)}, u32[]{:S(2)}, u32[]{:S(2)}) %all-to-all-start) | async-done | bytes 4194336 | tf_op jit(solution)/shard_map/all_to_all | solution.py:232
  69.7 14.5 %convolution_bitcast_fusion.re_ref.im_ref = f32[16,128,2048]{2,1,0:T(8,128)} fusion(bf16[8,16,128,128]{2,3,1,0:T(8,128)(2,1)} %bitcast.3, bf16[8,128,1024]{1,2,0:T(8,128)(2,1)S(1)} %fusion.36, bf16[8,128,1024]{1,2,0:T(8,128)(2,1)} %fusion.26), kind=kOutput, calls=%fused_computation.29 | convolution fusion | flops 8598323200 | bytes 25165824 | tf_op jit(solution)/shard_map/abrcp,acq->brpq/dot_general | solution.py:239
  84.2 15.3 %shard_map.46 = f32[2,16,8,1024]{3,2,1,0:T(8,128)} custom-call(f32[16,128,2048]{2,1,0:T(8,128)} %convolution_bitcast_fusion.re_ref.im_ref, f32[16,128,2048]{2,1,0:T(8,128)} %convolution_bitcast_fusion.re_ref.im_ref, f32[16,128,1024]{2,1,0:T(8,128)} %get-tuple-element.9.tc_ref, f32[16,128,1024]{2,1,0:T(8,128)} %get-tuple-element.10.ts_ref), custom_call_target="tpu_custom_call" | custom-call | tf_op jit(solution)/shard_map/pallas_call | solution.py:209
  99.6 1.5 %reduce_sum.18 = f32[2,16,1024]{2,1,0:T(8,128)S(1)} reduce(f32[2,16,8,1024]{3,2,1,0:T(8,128)} %shard_map.46, f32[]{:T(128)} %constant.240.clone.1), dimensions={2}, to_apply=%region_0.1 | reduce | flops 229376 | bytes 1179652 | tf_op jit(solution)/shard_map/reduce_sum | solution.py:221
  102.6 1.3 collective-permute-start.2
  103.9 1.8 %collective-permute-start.1 = (f32[4,2176]{1,0:T(4,128)S(1)}, f32[4,2176]{1,0:T(4,128)S(1)}, u32[]{:S(2)}, u32[]{:S(2)}) collective-permute-start(f32[4,2176]{1,0:T(4,128)S(1)} %bitcast.58), channel_id=1, source_target_pairs={{0,2},{1,3},{2,0},{3,1},{4,6},{5,7},{6,4},{7,5},{8,10},{9,11},{10,... | collective-permute-start | bytes 104456 | tf_op jit(solution)/shard_map/ppermute | solution.py:117
  105.7 0.7 collective-permute-start
  106.4 1.3 collective-permute-done.2
  107.7 2.1 %collective-permute-done.1 = f32[4,2176]{1,0:T(4,128)S(1)} collective-permute-done((f32[4,2176]{1,0:T(4,128)S(1)}, f32[4,2176]{1,0:T(4,128)S(1)}, u32[]{:S(2)}, u32[]{:S(2)}) %collective-permute-start.1) | collective-permute-done | bytes 34848 | tf_op jit(solution)/shard_map/ppermute | solution.py:117
  110.3 1.9 %collective-permute-start.4 = (f32[1,2176]{1,0:T(1,128)S(1)}, f32[1,2176]{1,0:T(1,128)S(1)}, u32[]{:S(2)}, u32[]{:S(2)}) collective-permute-start(f32[1,2176]{1,0:T(1,128)S(1)} %get-tuple-element.21), channel_id=1, source_target_pairs={{0,8},{1,9},{2,10},{3,11},{4,12},{5,13},{6,14},{7,15},{8,0},{9,1},... | collective-permute-start | bytes 26120 | tf_op jit(solution)/shard_map/ppermute | solution.py:117
  112.3 1.8 %collective-permute-start.3 = (f32[1,2176]{1,0:T(1,128)S(1)}, f32[1,2176]{1,0:T(1,128)S(1)}, u32[]{:S(2)}, u32[]{:S(2)}) collective-permute-start(f32[1,2176]{1,0:T(1,128)S(1)} %get-tuple-element.19), channel_id=1, source_target_pairs={{0,4},{1,5},{2,6},{3,7},{4,0},{5,1},{6,2},{7,3},{8,12},{9,13},{10,... | collective-permute-start | bytes 26120 | tf_op jit(solution)/shard_map/ppermute | solution.py:117
  114.1 0.8 collective-permute-done.5
  114.8 0.7 collective-permute-done.4
  116.0 1.0 collective-permute-start.11
  116.9 3.4 %collective-permute-start.12 = (f32[2176]{0:T(1024)S(1)}, f32[2176]{0:T(1024)S(1)}, u32[]{:S(2)}, u32[]{:S(2)}) collective-permute-start(f32[2176]{0:T(1024)S(1)} %add_reduce_fusion), channel_id=1, source_target_pairs={{0,112},{1,113},{2,114},{3,115},{4,116},{5,117},{6,118},{7,119},{8... | collective-permute-start | bytes 26120 | tf_op jit(solution)/shard_map/ppermute | solution.py:282
  120.4 3.4 %collective-permute-start.10 = (f32[2176]{0:T(1024)S(1)}, f32[2176]{0:T(1024)S(1)}, u32[]{:S(2)}, u32[]{:S(2)}) collective-permute-start(f32[2176]{0:T(1024)S(1)} %add_reduce_fusion), channel_id=1, source_target_pairs={{0,80},{1,81},{2,82},{3,83},{4,84},{5,85},{6,86},{7,87},{8,88},{9,... | collective-permute-start | bytes 26120 | tf_op jit(solution)/shard_map/ppermute | solution.py:282
  123.7 3.1 %collective-permute-start.8 = (f32[2176]{0:T(1024)S(1)}, f32[2176]{0:T(1024)S(1)}, u32[]{:S(2)}, u32[]{:S(2)}) collective-permute-start(f32[2176]{0:T(1024)S(1)} %add_reduce_fusion), channel_id=1, source_target_pairs={{0,48},{1,49},{2,50},{3,51},{4,52},{5,53},{6,54},{7,55},{8,56},{9,... | collective-permute-start | bytes 26120 | tf_op jit(solution)/shard_map/ppermute | solution.py:282
  127.2 4.1 %fusion.48 = (f32[1024,160]{1,0:T(8,128)S(1)}, f32[1024,160]{1,0:T(8,128)S(1)}) fusion(s32[160]{0:T(256)S(1)} %and_select_fusion), kind=kLoop, calls=%fused_computation.90 | loop fusion | flops 2293760 | bytes 1311360 | tf_op jit(solution)/shard_map/sin | solution.py:274
  (52 shorter events, 6.9 us)
Async XLA Ops:
  6.4 11.8 %copy-start.2 = (s32[128]{0:T(128)S(1)}, s32[128]{0:T(128)}, u32[]{:S(2)}) copy-start(s32[128]{0:T(128)} %param.6) | copy-start | bytes 1540
  6.4 11.8 %copy-start = (f32[2]{0:T(128)S(1)}, f32[2]{0:T(128)}, u32[]{:S(2)}) copy-start(f32[2]{0:T(128)} %param.7) | copy-start | bytes 28
  6.4 13.2 %copy-start.1 = (s32[128,2]{0,1:T(2,128)S(1)}, s32[128,2]{0,1:T(2,128)}, u32[]{:S(2)}) copy-start(s32[128,2]{0,1:T(2,128)} %param.5) | copy-start | bytes 3076
  6.4 63.4 %all-to-all-start = ((bf16[128,128,128]{1,2,0:T(8,128)(2,1)}), bf16[128,128,128]{1,2,0:T(8,128)(2,1)}, u32[]{:S(2)}, u32[]{:S(2)}) async-start(bf16[128,128,128]{1,2,0:T(8,128)(2,1)} %bitcast.56), calls=%async_computation | async-start | bytes 8388608 | tf_op jit(solution)/shard_map/all_to_all | solution.py:232
  102.6 5.1 %collective-permute-start.2 = (f32[4,2176]{1,0:T(4,128)S(1)}, f32[4,2176]{1,0:T(4,128)S(1)}, u32[]{:S(2)}, u32[]{:S(2)}) collective-permute-start(f32[4,2176]{1,0:T(4,128)S(1)} %bitcast.57), channel_id=1, source_target_pairs={{0,3},{1,2},{2,1},{3,0},{4,7},{5,6},{6,5},{7,4},{8,11},{9,10},{10,... | collective-permute-start | bytes 104456 | tf_op jit(solution)/shard_map/ppermute | solution.py:117
  103.9 5.9 %collective-permute-start.1 = (f32[4,2176]{1,0:T(4,128)S(1)}, f32[4,2176]{1,0:T(4,128)S(1)}, u32[]{:S(2)}, u32[]{:S(2)}) collective-permute-start(f32[4,2176]{1,0:T(4,128)S(1)} %bitcast.58), channel_id=1, source_target_pairs={{0,2},{1,3},{2,0},{3,1},{4,6},{5,7},{6,4},{7,5},{8,10},{9,11},{10,... | collective-permute-start | bytes 104456 | tf_op jit(solution)/shard_map/ppermute | solution.py:117
  105.7 4.1 %collective-permute-start = (f32[4,2176]{1,0:T(4,128)S(1)}, f32[4,2176]{1,0:T(4,128)S(1)}, u32[]{:S(2)}, u32[]{:S(2)}) collective-permute-start(f32[4,2176]{1,0:T(4,128)S(1)} %bitcast.59), channel_id=1, source_target_pairs={{0,1},{1,0},{2,3},{3,2},{4,5},{5,4},{6,7},{7,6},{8,9},{9,8},{10,11... | collective-permute-start | bytes 104456 | tf_op jit(solution)/shard_map/ppermute | solution.py:117
  109.9 4.9 %collective-permute-start.5 = (f32[1,2176]{1,0:T(1,128)S(1)}, f32[1,2176]{1,0:T(1,128)S(1)}, u32[]{:S(2)}, u32[]{:S(2)}) collective-permute-start(f32[1,2176]{1,0:T(1,128)S(1)} %get-tuple-element.20), channel_id=1, source_target_pairs={{0,12},{1,13},{2,14},{3,15},{4,8},{5,9},{6,10},{7,11},{8,4},{9,5},... | collective-permute-start | bytes 26120 | tf_op jit(solution)/shard_map/ppermute | solution.py:117
  110.3 5.2 %collective-permute-start.4 = (f32[1,2176]{1,0:T(1,128)S(1)}, f32[1,2176]{1,0:T(1,128)S(1)}, u32[]{:S(2)}, u32[]{:S(2)}) collective-permute-start(f32[1,2176]{1,0:T(1,128)S(1)} %get-tuple-element.21), channel_id=1, source_target_pairs={{0,8},{1,9},{2,10},{3,11},{4,12},{5,13},{6,14},{7,15},{8,0},{9,1},... | collective-permute-start | bytes 26120 | tf_op jit(solution)/shard_map/ppermute | solution.py:117
  112.3 3.7 %collective-permute-start.3 = (f32[1,2176]{1,0:T(1,128)S(1)}, f32[1,2176]{1,0:T(1,128)S(1)}, u32[]{:S(2)}, u32[]{:S(2)}) collective-permute-start(f32[1,2176]{1,0:T(1,128)S(1)} %get-tuple-element.19), channel_id=1, source_target_pairs={{0,4},{1,5},{2,6},{3,7},{4,0},{5,1},{6,2},{7,3},{8,12},{9,13},{10,... | collective-permute-start | bytes 26120 | tf_op jit(solution)/shard_map/ppermute | solution.py:117
  116.0 7.8 %collective-permute-start.11 = (f32[2176]{0:T(1024)S(1)}, f32[2176]{0:T(1024)S(1)}, u32[]{:S(2)}, u32[]{:S(2)}) collective-permute-start(f32[2176]{0:T(1024)S(1)} %add_reduce_fusion), channel_id=1, source_target_pairs={{0,96},{1,97},{2,98},{3,99},{4,100},{5,101},{6,102},{7,103},{8,104... | collective-permute-start | bytes 26120 | tf_op jit(solution)/shard_map/ppermute | solution.py:282
  116.9 9.8 %collective-permute-start.12 = (f32[2176]{0:T(1024)S(1)}, f32[2176]{0:T(1024)S(1)}, u32[]{:S(2)}, u32[]{:S(2)}) collective-permute-start(f32[2176]{0:T(1024)S(1)} %add_reduce_fusion), channel_id=1, source_target_pairs={{0,112},{1,113},{2,114},{3,115},{4,116},{5,117},{6,118},{7,119},{8... | collective-permute-start | bytes 26120 | tf_op jit(solution)/shard_map/ppermute | solution.py:282
  120.3 11.0 %collective-permute-start.9 = (f32[2176]{0:T(1024)S(1)}, f32[2176]{0:T(1024)S(1)}, u32[]{:S(2)}, u32[]{:S(2)}) collective-permute-start(f32[2176]{0:T(1024)S(1)} %add_reduce_fusion), channel_id=1, source_target_pairs={{0,64},{1,65},{2,66},{3,67},{4,68},{5,69},{6,70},{7,71},{8,72},{9,... | collective-permute-start | bytes 26120 | tf_op jit(solution)/shard_map/ppermute | solution.py:282
  120.4 11.0 %collective-permute-start.10 = (f32[2176]{0:T(1024)S(1)}, f32[2176]{0:T(1024)S(1)}, u32[]{:S(2)}, u32[]{:S(2)}) collective-permute-start(f32[2176]{0:T(1024)S(1)} %add_reduce_fusion), channel_id=1, source_target_pairs={{0,80},{1,81},{2,82},{3,83},{4,84},{5,85},{6,86},{7,87},{8,88},{9,... | collective-permute-start | bytes 26120 | tf_op jit(solution)/shard_map/ppermute | solution.py:282
  123.7 7.6 %collective-permute-start.7 = (f32[2176]{0:T(1024)S(1)}, f32[2176]{0:T(1024)S(1)}, u32[]{:S(2)}, u32[]{:S(2)}) collective-permute-start(f32[2176]{0:T(1024)S(1)} %add_reduce_fusion), channel_id=1, source_target_pairs={{0,32},{1,33},{2,34},{3,35},{4,36},{5,37},{6,38},{7,39},{8,40},{9,... | collective-permute-start | bytes 26120 | tf_op jit(solution)/shard_map/ppermute | solution.py:282
  123.7 7.6 %collective-permute-start.8 = (f32[2176]{0:T(1024)S(1)}, f32[2176]{0:T(1024)S(1)}, u32[]{:S(2)}, u32[]{:S(2)}) collective-permute-start(f32[2176]{0:T(1024)S(1)} %add_reduce_fusion), channel_id=1, source_target_pairs={{0,48},{1,49},{2,50},{3,51},{4,52},{5,53},{6,54},{7,55},{8,56},{9,... | collective-permute-start | bytes 26120 | tf_op jit(solution)/shard_map/ppermute | solution.py:282
  126.8 4.6 %collective-permute-start.6 = (f32[2176]{0:T(1024)S(1)}, f32[2176]{0:T(1024)S(1)}, u32[]{:S(2)}, u32[]{:S(2)}) collective-permute-start(f32[2176]{0:T(1024)S(1)} %add_reduce_fusion), channel_id=1, source_target_pairs={{0,16},{1,17},{2,18},{3,19},{4,20},{5,21},{6,22},{7,23},{8,24},{9,... | collective-permute-start | bytes 26120 | tf_op jit(solution)/shard_map/ppermute | solution.py:282
where the time goes:
time: 135 us; the launch traced here: 134 us
  other arithmetic  39.1 us (29%)
  starting transfers between devices  30.9 us (23%)
  waiting for transfers between devices  20.7 us (15%)
  matrix products  16.8 us (12%)
  Pallas kernels  15.3 us (11%)
  local copies, waits for them, and re-layouts  8.43 us (6%)
  between operations  2.98 us (2%)
    all_to_all x1, waiting for transfers between devices, local(): lax.all_to_all(blocks, ('scan', 'det'), split_axis=0, concat_axis=0, tile...  15.4 us
    pallas_call x1, Pallas kernels, spectrum(): pl.pallas_call(spectrum_kernel, grid=(steps,), in_specs=[pl.BlockSpec((SR...  15.3 us
    dot_general x1, matrix products, local(): jnp.einsum('abrcp,acq->brpq', images, table, preferred_element_type=jnp.f...  14.5 us
    mul x1, other arithmetic, local(): turn_sin * weights[None, :, None]  14.2 us
    all_to_all x1, starting transfers between devices, local(): lax.all_to_all(blocks, ('scan', 'det'), split_axis=0, concat_axis=0, tile...  11.7 us
    ppermute x7, starting transfers between devices, local(): lax.ppermute(own, axes, [(i, i ^ d << 4) for i in range(count)])  11.2 us
    convert_element_type x1, other arithmetic, local(): col_cos = col_cos.astype(jnp.bfloat16)  9.08 us
    neg x1, other arithmetic, local(): -col_sin  8.29 us
  transfers between devices with their start and end apart: 14, of which 6 were waited for; matrix products, arithmetic and copies ran while one was open for 28% of the time, Pallas kernels for 0%

commit v1 on v0

--- a/solution.py
+++ b/solution.py
@@ -109,13 +109,13 @@
     return sincos_reduced(rest, turns & 3)
 
 
-def exchange(values, axes, count, low, bits, rows):
-    digit = (lax.axis_index(axes) >> low) & ((1 << bits) - 1)
-    kept = lax.dynamic_index_in_dim(rows(values), digit, axis=1, keepdims=False)
-    for d in range(1, 1 << bits):
-        sent = lax.dynamic_index_in_dim(rows(values), digit ^ d, axis=1, keepdims=False)
-        kept = kept + lax.ppermute(sent, axes, [(i, i ^ (d << low)) for i in range(count)])
-    return kept
+def pairwise_sum(values):
+    while len(values) > 1:
+        values = [
+            values[e] + values[e + 1] if e + 1 < len(values) else values[e]
+            for e in range(0, len(values), 2)
+        ]
+    return values[0]
 
 
 def phase_parts(pixel_index, shifts, aberration):
@@ -272,18 +272,11 @@
     )
     col_angles = phase_angles(jnp.arange(SC, dtype=jnp.int32), columns, SC)
     cos_cols, sin_cols = lax.optimization_barrier((jnp.cos(col_angles), jnp.sin(col_angles)))
-    axes = ("scan", "det")
-    count = scan_size * det_size
-    quarters = packed.reshape(4, 4, packed.shape[1])
-    partial = exchange(quarters, axes, count, 0, 2, lambda x: x)
-    own = exchange(partial, axes, count, 2, 2, lambda x: x.reshape(1, 4, x.shape[1]))
-    own = own.reshape(-1)
-    partners = [own] + [
-        lax.ppermute(own, axes, [(i, i ^ (d << 4)) for i in range(count)]) for d in range(1, 8)
-    ]
-    while len(partners) > 1:
-        partners = [partners[e] + partners[e + 1] for e in range(0, len(partners), 2)]
-    total = partners[0]
+    gathered = lax.all_to_all(packed, "det", 0, 0, tiled=True)
+    own = pairwise_sum([gathered[i] for i in range(det_size)])
+    spread = jnp.broadcast_to(own, (scan_size,) + own.shape)
+    gathered = lax.all_to_all(spread, "scan", 0, 0, tiled=True)
+    total = pairwise_sum([gathered[i] for i in range(scan_size)])
     line_real = total[:SC]
     line_imag = total[SC : 2 * SC]
     bright_sum = total[2 * SC]

time: 135 us -> 131 us (0.970)
  starting transfers between devices: 30.9 us -> 20.4 us
  waiting for transfers between devices: 20.7 us -> 26.1 us
    ppermute x13 -> x0, starting transfers between devices: 19.2 us -> none  [the longest x7 11.2 us: local(): lax.ppermute(own, axes, [(i, i ^ d << 4) for i in range(count)])]
    all_to_all x0 -> x2, waiting for transfers between devices: none -> 10.5 us  [the longest x1 8.26 us: local(): gathered = lax.all_to_all(packed, 'det', 0, 0, tiled=True)]
    all_to_all x0 -> x2, starting transfers between devices: none -> 8.7 us  [the longest x1 4.58 us: local(): gathered = lax.all_to_all(spread, 'scan', 0, 0, tiled=True)]
    ppermute x13 -> x0, waiting for transfers between devices: 5.33 us -> none  [the longest x6 5.31 us: exchange(): lax.ppermute(sent, axes, [(i, i ^ d << low) for i in range(count)])]
    unnamed x10 -> x7, local copies, waits for them, and re-layouts: 6.39 us -> 6.36 us
  transfers between devices with their start and end apart: 14 -> 3, of which waited for: 6 -> 3; matrix products, arithmetic and copies ran while one was open for 28% -> 29% of each run, Pallas kernels for 0% -> 0%
where the time goes in v1:
time: 131 us; the launch traced here: 130 us
  other arithmetic  39 us (30%)
  waiting for transfers between devices  26.1 us (20%)
  starting transfers between devices  20.4 us (16%)
  matrix products  16.8 us (13%)
  Pallas kernels  15.3 us (12%)
  local copies, waits for them, and re-layouts  9.63 us (7%)
  between operations  2.87 us (2%)
    all_to_all x1, waiting for transfers between devices, local(): lax.all_to_all(blocks, ('scan', 'det'), split_axis=0, concat_axis=0, tile...  15.5 us
    pallas_call x1, Pallas kernels, spectrum(): pl.pallas_call(spectrum_kernel, grid=(steps,), in_specs=[pl.BlockSpec((SR...  15.3 us
    dot_general x1, matrix products, local(): jnp.einsum('abrcp,acq->brpq', images, table, preferred_element_type=jnp.f...  14.6 us
    mul x1, other arithmetic, local(): turn_sin * weights[None, :, None]  14.2 us
    all_to_all x1, starting transfers between devices, local(): lax.all_to_all(blocks, ('scan', 'det'), split_axis=0, concat_axis=0, tile...  11.7 us
    convert_element_type x1, other arithmetic, local(): col_cos = col_cos.astype(jnp.bfloat16)  9.05 us
    neg x1, other arithmetic, local(): -col_sin  8.29 us
    all_to_all x1, waiting for transfers between devices, local(): gathered = lax.all_to_all(packed, 'det', 0, 0, tiled=True)  8.26 us
  transfers between devices with their start and end apart: 3, of which 3 were waited for; matrix products, arithmetic and copies ran while one was open for 29% of the time, Pallas kernels for 0%

profile of v1, /device:TPU:0, one launch (start us, length us, event | category | flops | bytes accessed | tf_op | source)
XLA Modules:
  0.0 130.2 jit_solution(15382452662483991348)
XLA Ops:
  0.0 6.4 %copy.12 = bf16[1,128,16384]{1,2,0:T(8,128)(2,1)} copy(bf16[1,128,16384]{2,1,0:T(8,128)(2,1)} %param.4) | data formatting | bytes 8388608 | tf_op args[0]
  6.4 11.7 %all-to-all-start = ((bf16[128,128,128]{1,2,0:T(8,128)(2,1)}), bf16[128,128,128]{1,2,0:T(8,128)(2,1)}, u32[]{:S(2)}, u32[]{:S(2)}) async-start(bf16[128,128,128]{1,2,0:T(8,128)(2,1)} %bitcast.49), calls=%async_computation | async-start | bytes 8388608 | tf_op jit(solution)/shard_map/all_to_all | solution.py:232
  18.2 0.6 fusion.111
  20.8 0.4 fusion.47
  21.4 14.2 %fusion.10 = (f32[16,128,1024]{2,1,0:T(8,128)}, f32[16,128,1024]{2,1,0:T(8,128)}) fusion(f32[128]{0:T(128)S(1)} %convert_element_type.126, f32[128,1024]{1,0:T(8,128)S(1)} %get-tuple-element.16, f32[16,128]{1,0:T(8,128)S(1)} %get-tuple-element.22, f32[]{:T(128)} %bitcast.8, f32[128,1024]{1,0:T(8,128)S(1)} %get-tuple-element.15, ...), kind=kLoop, calls=%fused_computation.19 | loop fusion | flops 96468992 | bytes 17842692 | tf_op jit(solution)/shard_map/mul | solution.py:255
  35.5 0.6 convert_reduce_fusion
  36.1 0.6 broadcast_in_dim.5
  36.8 8.3 %fusion.36 = bf16[8,128,1024]{1,2,0:T(8,128)(2,1)S(1)} fusion(s32[8,128]{1,0:T(8,128)S(1)} %multiply_add_fusion), kind=kLoop, calls=%fused_computation.70 | loop fusion | flops 62914560 | bytes 2101248 | tf_op jit(solution)/shard_map/neg | solution.py:238
  45.1 9.0 %fusion.26 = bf16[8,128,1024]{1,2,0:T(8,128)(2,1)} fusion(s32[8,128]{1,0:T(8,128)S(1)} %multiply_add_fusion), kind=kLoop, calls=%fused_computation.57 | loop fusion | flops 61865984 | bytes 2101248 | tf_op jit(solution)/shard_map/convert_element_type | solution.py:236
  54.2 15.5 %all-to-all-done = bf16[128,128,128]{1,2,0:T(8,128)(2,1)} async-done(((bf16[128,128,128]{1,2,0:T(8,128)(2,1)}), bf16[128,128,128]{1,2,0:T(8,128)(2,1)}, u32[]{:S(2)}, u32[]{:S(2)}) %all-to-all-start) | async-done | bytes 4194336 | tf_op jit(solution)/shard_map/all_to_all | solution.py:232
  69.7 14.6 %convolution_bitcast_fusion.re_ref.im_ref = f32[16,128,2048]{2,1,0:T(8,128)} fusion(bf16[8,16,128,128]{2,3,1,0:T(8,128)(2,1)} %bitcast.3, bf16[8,128,1024]{1,2,0:T(8,128)(2,1)S(1)} %fusion.36, bf16[8,128,1024]{1,2,0:T(8,128)(2,1)} %fusion.26), kind=kOutput, calls=%fused_computation.29 | convolution fusion | flops 8598323200 | bytes 25165824 | tf_op jit(solution)/shard_map/abrcp,acq->brpq/dot_general | solution.py:239
  84.3 15.3 %shard_map.46 = f32[2,16,8,1024]{3,2,1,0:T(8,128)} custom-call(f32[16,128,2048]{2,1,0:T(8,128)} %convolution_bitcast_fusion.re_ref.im_ref, f32[16,128,2048]{2,1,0:T(8,128)} %convolution_bitcast_fusion.re_ref.im_ref, f32[16,128,1024]{2,1,0:T(8,128)} %get-tuple-element.9.tc_ref, f32[16,128,1024]{2,1,0:T(8,128)} %get-tuple-element.10.ts_ref), custom_call_target="tpu_custom_call" | custom-call | tf_op jit(solution)/shard_map/pallas_call | solution.py:209
  99.6 1.5 %reduce_sum.18 = f32[2,16,1024]{2,1,0:T(8,128)S(1)} reduce(f32[2,16,8,1024]{3,2,1,0:T(8,128)} %shard_map.46, f32[]{:T(128)} %constant.216.clone.1), dimensions={2}, to_apply=%region_0.1 | reduce | flops 229376 | bytes 1179652 | tf_op jit(solution)/shard_map/reduce_sum | solution.py:221
  102.4 0.8 copy.16
  103.2 4.1 %all-to-all-start.1 = ((f32[16,1,2176]{2,1,0:T(1,128)}), f32[16,1,2176]{2,1,0:T(1,128)S(1)}, u32[]{:S(2)}, u32[]{:S(2)}) async-start(f32[16,1,2176]{2,1,0:T(1,128)} %copy.16), calls=%async_computation.1 | async-start | bytes 278528 | tf_op jit(solution)/shard_map/all_to_all | solution.py:275
  107.3 8.3 %all-to-all-done.1 = f32[16,1,2176]{2,1,0:T(1,128)S(1)} async-done(((f32[16,1,2176]{2,1,0:T(1,128)}), f32[16,1,2176]{2,1,0:T(1,128)S(1)}, u32[]{:S(2)}, u32[]{:S(2)}) %all-to-all-start.1) | async-done | bytes 139296 | tf_op jit(solution)/shard_map/all_to_all | solution.py:275
  115.7 0.7 broadcast_in_dim.6
  116.3 4.6 %all-to-all-start.2 = ((f32[8,1,2176]{2,1,0:T(1,128)}), f32[8,1,2176]{2,1,0:T(1,128)S(1)}, u32[]{:S(2)}, u32[]{:S(2)}) async-start(f32[8,1,2176]{2,1,0:T(1,128)} %broadcast_in_dim.6), calls=%async_computation.2 | async-start | bytes 139264 | tf_op jit(solution)/shard_map/all_to_all | solution.py:278
  120.9 4.1 %fusion.48 = (f32[1024,160]{1,0:T(8,128)S(1)}, f32[1024,160]{1,0:T(8,128)S(1)}) fusion(s32[160]{0:T(256)S(1)} %and_select_fusion), kind=kLoop, calls=%fused_computation.90 | loop fusion | flops 2293760 | bytes 1311360 | tf_op jit(solution)/shard_map/sin | solution.py:274
  125.0 2.3 %all-to-all-done.2 = f32[8,1,2176]{2,1,0:T(1,128)S(1)} async-done(((f32[8,1,2176]{2,1,0:T(1,128)}), f32[8,1,2176]{2,1,0:T(1,128)S(1)}, u32[]{:S(2)}, u32[]{:S(2)}) %all-to-all-start.2) | async-done | bytes 69664 | tf_op jit(solution)/shard_map/all_to_all | solution.py:278
  127.3 0.5 slice.183
  127.8 0.5 fusion.80
  128.3 0.5 fusion.79
  129.6 0.6 divide_multiply_fusion
  (24 shorter events, 1.5 us)
Async XLA Ops:
  6.4 11.8 %copy-start.2 = (s32[128]{0:T(128)S(1)}, s32[128]{0:T(128)}, u32[]{:S(2)}) copy-start(s32[128]{0:T(128)} %param.6) | copy-start | bytes 1540
  6.4 11.8 %copy-start = (f32[2]{0:T(128)S(1)}, f32[2]{0:T(128)}, u32[]{:S(2)}) copy-start(f32[2]{0:T(128)} %param.7) | copy-start | bytes 28
  6.4 13.1 %copy-start.1 = (s32[128,2]{0,1:T(2,128)S(1)}, s32[128,2]{0,1:T(2,128)}, u32[]{:S(2)}) copy-start(s32[128,2]{0,1:T(2,128)} %param.5) | copy-start | bytes 3076
  6.4 63.4 %all-to-all-start = ((bf16[128,128,128]{1,2,0:T(8,128)(2,1)}), bf16[128,128,128]{1,2,0:T(8,128)(2,1)}, u32[]{:S(2)}, u32[]{:S(2)}) async-start(bf16[128,128,128]{1,2,0:T(8,128)(2,1)} %bitcast.49), calls=%async_computation | async-start | bytes 8388608 | tf_op jit(solution)/shard_map/all_to_all | solution.py:232
  103.2 12.4 %all-to-all-start.1 = ((f32[16,1,2176]{2,1,0:T(1,128)}), f32[16,1,2176]{2,1,0:T(1,128)S(1)}, u32[]{:S(2)}, u32[]{:S(2)}) async-start(f32[16,1,2176]{2,1,0:T(1,128)} %copy.16), calls=%async_computation.1 | async-start | bytes 278528 | tf_op jit(solution)/shard_map/all_to_all | solution.py:275
  116.3 10.9 %all-to-all-start.2 = ((f32[8,1,2176]{2,1,0:T(1,128)}), f32[8,1,2176]{2,1,0:T(1,128)S(1)}, u32[]{:S(2)}, u32[]{:S(2)}) async-start(f32[8,1,2176]{2,1,0:T(1,128)} %broadcast_in_dim.6), calls=%async_computation.2 | async-start | bytes 139264 | tf_op jit(solution)/shard_map/all_to_all | solution.py:278

commit v2 on v1

--- a/solution.py
+++ b/solution.py
@@ -5,6 +5,7 @@
 from jax import lax
 from jax.sharding import PartitionSpec as P
 from jax.experimental import pallas as pl
+from jax.experimental.pallas import tpu as pltpu
 
 SR = 16
 SC = 1024
@@ -185,39 +186,85 @@
     return out
 
 
-def spectrum_kernel(re_ref, im_ref, tc_ref, ts_ref, out_ref):
-    out_ref[...] = jnp.zeros(out_ref.shape, out_ref.dtype)
-
-    def body(i, carry):
-        rows = pl.ds(pl.multiple_of(i * 8, 8), 8)
-        full = fft16([(re_ref[r, rows, :], im_ref[r, rows, :]) for r in range(SR)])
+def fused_kernel(x_ref, t_ref, tc_ref, ts_ref, out_ref, y_ref):
+    step = pl.program_id(0)
+    blocks = pl.num_programs(0) - 1
+    sources = x_ref.shape[0] // SR
+    width = tc_ref.shape[2]
+    slot = step % 2
+
+    def columns(i):
+        acc = jnp.zeros((x_ref.shape[1], 2 * width), jnp.float32)
+        for t in range(sources):
+            acc = acc + jnp.dot(
+                x_ref[t * SR + i],
+                t_ref[pl.ds(t * x_ref.shape[2], x_ref.shape[2]), :],
+                preferred_element_type=jnp.float32,
+            )
+        y_ref[slot, i] = acc
+
+    def rows(i):
+        lines = pl.ds(pl.multiple_of(i * 8, 8), 8)
+        full = fft16(
+            [
+                (y_ref[1 - slot, r, lines, pl.ds(0, width)], y_ref[1 - slot, r, lines, pl.ds(width, width)])
+                for r in range(SR)
+            ]
+        )
         for s in range(SR):
             fr, fi = full[s]
-            tc = tc_ref[s, rows, :]
-            ts = ts_ref[s, rows, :]
+            tc = tc_ref[s, lines, :]
+            ts = ts_ref[s, lines, :]
             out_ref[0, s] += fr * tc - fi * ts
             out_ref[1, s] += fr * ts + fi * tc
+
+    def both(i, carry):
+        columns(i)
+        rows(i)
         return carry
 
-    lax.fori_loop(0, re_ref.shape[1] // 8, body, 0)
-
-
-def spectrum(both_col, turn_cos, turn_sin):
-    pixels = both_col.shape[1]
+    def first(i, carry):
+        columns(i)
+        return carry
+
+    def last(i, carry):
+        rows(i)
+        return carry
+
+    @pl.when(step == 0)
+    def _():
+        lax.fori_loop(0, SR, first, 0)
+
+    @pl.when((step > 0) & (step < blocks))
+    def _():
+        out_ref[...] = jnp.zeros(out_ref.shape, out_ref.dtype)
+        lax.fori_loop(0, SR, both, 0)
+
+    @pl.when(step == blocks)
+    def _():
+        out_ref[...] = jnp.zeros(out_ref.shape, out_ref.dtype)
+        lax.fori_loop(0, x_ref.shape[1] // 8, last, 0)
+
+
+def spectrum(sources, table, turn_cos, turn_sin):
+    pixels = sources.shape[1]
+    chunk = sources.shape[2]
     block = 128
     steps = SC // block
     spec = pl.pallas_call(
-        spectrum_kernel,
-        grid=(steps,),
+        fused_kernel,
+        grid=(steps + 1,),
         in_specs=[
-            pl.BlockSpec((SR, pixels, block), lambda j: (0, 0, j)),
-            pl.BlockSpec((SR, pixels, block), lambda j: (0, 0, j + steps)),
-            pl.BlockSpec((SR, pixels, block), lambda j: (0, 0, j)),
-            pl.BlockSpec((SR, pixels, block), lambda j: (0, 0, j)),
+            pl.BlockSpec(sources.shape, lambda j: (0, 0, 0)),
+            pl.BlockSpec((table.shape[0], 2 * block), lambda j: (0, jnp.minimum(j, steps - 1))),
+            pl.BlockSpec((SR, pixels, block), lambda j: (0, 0, jnp.maximum(j - 1, 0))),
+            pl.BlockSpec((SR, pixels, block), lambda j: (0, 0, jnp.maximum(j - 1, 0))),
         ],
-        out_specs=pl.BlockSpec((2, SR, 8, block), lambda j: (0, 0, 0, j)),
+        out_specs=pl.BlockSpec((2, SR, 8, block), lambda j: (0, 0, 0, jnp.maximum(j - 1, 0))),
         out_shape=jax.ShapeDtypeStruct((2, SR, 8, SC), jnp.float32),
-    )(both_col, both_col, turn_cos, turn_sin)
+        scratch_shapes=[pltpu.VMEM((2, SR, pixels, 2 * block), jnp.float32)],
+        compiler_params=pltpu.CompilerParams(vmem_limit_bytes=48 * 1024 * 1024),
+    )(sources, table, turn_cos, turn_sin)
     return jnp.sum(spec, axis=2)
 
 
@@ -230,15 +277,14 @@
     owner = lax.axis_index("scan") * det_size + lax.axis_index("det")
     blocks = jnp.transpose(frames.reshape(rows_dev * tile, groups, owned), (1, 0, 2))
     arrived = lax.all_to_all(blocks, ("scan", "det"), split_axis=0, concat_axis=0, tiled=True)
-    images = arrived.reshape(scan_size, det_size, rows_dev, tile, owned)
     full_cols = jnp.arange(SC, dtype=jnp.int32)
     col_sin, col_cos = sincos_of_steps(jnp.mod(full_cols[:, None] * full_cols[None, :], SC), SC)
     col_cos = col_cos.astype(jnp.bfloat16)
     col_sin = col_sin.astype(jnp.bfloat16)
-    table = jnp.concatenate([col_cos, -col_sin], axis=1).reshape(scan_size, tile, 2 * SC)
-    both_col = jnp.einsum(
-        "abrcp,acq->brpq", images, table, preferred_element_type=jnp.float32
-    ).reshape(SR, owned, 2 * SC)
+    table = jnp.stack(
+        [col_cos.reshape(SC, SC // 128, 128), -col_sin.reshape(SC, SC // 128, 128)], axis=2
+    ).reshape(SC, 2 * SC)
+    sources = jnp.swapaxes(arrived, 1, 2)
     full_rows = jnp.arange(SR, dtype=jnp.int32)
     angles_by_row = phase_angles(full_rows, full_rows, SR)
     row_cos = jnp.cos(angles_by_row)
@@ -254,7 +300,7 @@
     turn_cos, turn_sin = lax.optimization_barrier(
         (turn_cos * weights[None, :, None], turn_sin * weights[None, :, None])
     )
-    spec_real, spec_imag = spectrum(both_col, turn_cos, turn_sin)
+    spec_real, spec_imag = spectrum(sources, table, turn_cos, turn_sin)
     row_cos_t = row_cos.T
     row_sin_t = row_sin.T
     rows_real = jnp.dot(row_cos_t, spec_real, precision=EXACT_PRECISION) - jnp.dot(

time: 131 us -> 151 us (1.15)
  Pallas kernels: 15.3 us -> 46.3 us
  local copies, waits for them, and re-layouts: 9.63 us -> 26 us
  waiting for transfers between devices: 26.1 us -> 10.5 us
  matrix products: 16.8 us -> 2.29 us
  starting transfers between devices: 20.4 us -> 22.7 us
    pallas_call x1, Pallas kernels: 15.3 us -> 46.3 us  [spectrum(): pl.pallas_call(fused_kernel, grid=(steps + 1,), in_specs=[pl.BlockSpec(so...]
    all_to_all x1, waiting for transfers between devices: 15.5 us -> 0.01 us  [local(): lax.all_to_all(blocks, ('scan', 'det'), split_axis=0, concat_axis=0, tile...]
    dot_general x1 -> x0, matrix products: 14.6 us -> none  [local(): jnp.einsum('abrcp,acq->brpq', images, table, preferred_element_type=jnp.f...]
    another operation x0 -> x1, local copies, waits for them, and re-layouts: none -> 8.45 us  [local(): jnp.stack([col_cos.reshape(SC, SC // 128, 128), -col_sin.reshape(SC, SC /...]
    reshape x0 -> x1, local copies, waits for them, and re-layouts: none -> 7.89 us  [local(): table = jnp.stack([col_cos.reshape(SC, SC // 128, 128), -col_sin.reshape(...]
    another operation x0 -> x1, other arithmetic: none -> 2.65 us  [local(): jnp.stack([col_cos.reshape(SC, SC // 128, 128), -col_sin.reshape(SC, SC /...]
    all_to_all x1, starting transfers between devices: 4.12 us -> 6.19 us  [local(): gathered = lax.all_to_all(packed, 'det', 0, 0, tiled=True)]
  transfers between devices with their start and end apart: 3 -> 3, of which waited for: 3 -> 2; matrix products, arithmetic and copies ran while one was open for 29% -> 38% of each run, Pallas kernels for 0% -> 0%
where the time goes in v2:
time: 151 us
  Pallas kernels  46.3 us (31%)
  other arithmetic  40 us (26%)
  local copies, waits for them, and re-layouts  26 us (17%)
  starting transfers between devices  22.7 us (15%)
  waiting for transfers between devices  10.5 us (7%)
  between operations  2.82 us (2%)
  matrix products  2.29 us (2%)
    pallas_call x1, Pallas kernels, spectrum(): pl.pallas_call(fused_kernel, grid=(steps + 1,), in_specs=[pl.BlockSpec(so...  46.3 us
    mul x1, other arithmetic, local(): turn_sin * weights[None, :, None]  14.4 us
    all_to_all x1, starting transfers between devices, local(): lax.all_to_all(blocks, ('scan', 'det'), split_axis=0, concat_axis=0, tile...  11.7 us
    another operation x1, local copies, waits for them, and re-layouts, local(): jnp.stack([col_cos.reshape(SC, SC // 128, 128), -col_sin.reshape(SC, SC /...  8.45 us
    neg x1, other arithmetic, local(): -col_sin.reshape(SC, SC // 128, 128)  8.33 us
    convert_element_type x1, other arithmetic, local(): col_cos = col_cos.astype(jnp.bfloat16)  8.31 us
    all_to_all x1, waiting for transfers between devices, local(): gathered = lax.all_to_all(packed, 'det', 0, 0, tiled=True)  8.26 us
    reshape x1, local copies, waits for them, and re-layouts, local(): table = jnp.stack([col_cos.reshape(SC, SC // 128, 128), -col_sin.reshape(...  7.89 us
  transfers between devices with their start and end apart: 3, of which 2 were waited for; matrix products, arithmetic and copies ran while one was open for 38% of the time, Pallas kernels for 0%

profile of v2, /device:TPU:0, one launch (start us, length us, event | category | flops | bytes accessed | tf_op | source)
XLA Modules:
  0.0 150.6 jit_solution(15804222644227408171)
XLA Ops:
  0.0 6.4 %copy.8 = bf16[1,128,16384]{1,2,0:T(8,128)(2,1)} copy(bf16[1,128,16384]{2,1,0:T(8,128)(2,1)} %param.4) | data formatting | bytes 8388608 | tf_op args[0]
  6.4 11.7 %all-to-all-start = ((bf16[128,128,128]{1,2,0:T(8,128)(2,1)}), bf16[128,128,128]{1,2,0:T(8,128)(2,1)}, u32[]{:S(2)}, u32[]{:S(2)}) async-start(bf16[128,128,128]{1,2,0:T(8,128)(2,1)} %bitcast.37), calls=%async_computation | async-start | bytes 8388608 | tf_op jit(solution)/shard_map/all_to_all | solution.py:279
  18.2 8.3 %fusion.32 = bf16[1024,8,1,128]{3,1,2,0:T(8,128)(2,1)S(1)} fusion(s32[8,128]{1,0:T(8,128)S(1)} %multiply_add_fusion), kind=kLoop, calls=%fused_computation.66 | loop fusion | flops 62914560 | bytes 2101248 | tf_op jit(solution)/shard_map/neg | solution.py:285
  26.5 8.3 %fusion.26 = bf16[1024,8,1,128]{3,1,2,0:T(8,128)(2,1)S(1)} fusion(s32[8,128]{1,0:T(8,128)S(1)} %multiply_add_fusion), kind=kLoop, calls=%fused_computation.56 | loop fusion | flops 61865984 | bytes 2101248 | tf_op jit(solution)/shard_map/convert_element_type | solution.py:282
  34.8 2.6 %pad_maximum_fusion = bf16[1024,8,2,128]{3,1,2,0:T(8,128)(2,1)} fusion(bf16[1024,8,1,128]{3,1,2,0:T(8,128)(2,1)S(1)} %fusion.32, bf16[1024,8,1,128]{3,1,2,0:T(8,128)(2,1)S(1)} %fusion.26), kind=kLoop, calls=%fused_computation.58 | loop fusion | flops 2097152 | bytes 8388608 | tf_op jit(solution)/shard_map/stack | solution.py:284
  37.5 8.4 %copy.9 = bf16[1024,8,2,128]{3,2,1,0:T(2,128)(2,1)} copy(bf16[1024,8,2,128]{3,1,2,0:T(8,128)(2,1)} %pad_maximum_fusion) | data formatting | bytes 8388608 | tf_op jit(solution)/shard_map/stack | solution.py:284
  45.9 7.9 %reshape.705.t_ref = bf16[1024,2048]{1,0:T(8,128)(2,1)} reshape(bf16[1024,8,2,128]{3,2,1,0:T(2,128)(2,1)} %copy.9) | data formatting | bytes 8388608 | tf_op jit(solution)/shard_map/reshape | solution.py:286
  53.8 0.6 fusion.106
  56.6 0.4 fusion.43
  57.0 14.4 %fusion.10 = (f32[16,128,1024]{2,1,0:T(8,128)}, f32[16,128,1024]{2,1,0:T(8,128)}) fusion(f32[128]{0:T(128)S(1)} %convert_element_type.150, f32[128,1024]{1,0:T(8,128)S(1)} %get-tuple-element.16, f32[16,128]{1,0:T(8,128)S(1)} %get-tuple-element.22, f32[]{:T(128)} %bitcast.5, f32[128,1024]{1,0:T(8,128)S(1)} %get-tuple-element.15, ...), kind=kLoop, calls=%fused_computation.19 | loop fusion | flops 96468992 | bytes 17842692 | tf_op jit(solution)/shard_map/mul | solution.py:301
  71.4 0.6 convert_reduce_fusion
  72.0 0.6 broadcast_in_dim.5
  72.7 46.3 %shard_map.46 = f32[2,16,8,1024]{3,2,1,0:T(8,128)S(1)} custom-call(bf16[128,128,128]{2,1,0:T(8,128)(2,1)} %bitcast.2.x_ref, bf16[1024,2048]{1,0:T(8,128)(2,1)} %reshape.705.t_ref, f32[16,128,1024]{2,1,0:T(8,128)} %get-tuple-element.9.tc_ref, f32[16,128,1024]{2,1,0:T(8,128)} %get-tuple-element.10.ts_ref), custom_call_target="tpu_custom_call" | custom-call | tf_op jit(solution)/shard_map/pallas_call | solution.py:254
  120.6 0.8 copy.10
  121.3 6.2 %all-to-all-start.1 = ((f32[16,1,2176]{2,1,0:T(1,128)}), f32[16,1,2176]{2,1,0:T(1,128)S(1)}, u32[]{:S(2)}, u32[]{:S(2)}) async-start(f32[16,1,2176]{2,1,0:T(1,128)} %copy.10), calls=%async_computation.1 | async-start | bytes 278528 | tf_op jit(solution)/shard_map/all_to_all | solution.py:321
  127.6 8.3 %all-to-all-done.1 = f32[16,1,2176]{2,1,0:T(1,128)S(1)} async-done(((f32[16,1,2176]{2,1,0:T(1,128)}), f32[16,1,2176]{2,1,0:T(1,128)S(1)}, u32[]{:S(2)}, u32[]{:S(2)}) %all-to-all-start.1) | async-done | bytes 139296 | tf_op jit(solution)/shard_map/all_to_all | solution.py:321
  135.9 0.7 broadcast_in_dim.6
  136.6 4.8 %all-to-all-start.2 = ((f32[8,1,2176]{2,1,0:T(1,128)}), f32[8,1,2176]{2,1,0:T(1,128)S(1)}, u32[]{:S(2)}, u32[]{:S(2)}) async-start(f32[8,1,2176]{2,1,0:T(1,128)} %broadcast_in_dim.6), calls=%async_computation.2 | async-start | bytes 139264 | tf_op jit(solution)/shard_map/all_to_all | solution.py:324
  141.4 4.1 %fusion.44 = (f32[1024,160]{1,0:T(8,128)S(1)}, f32[1024,160]{1,0:T(8,128)S(1)}) fusion(s32[160]{0:T(256)S(1)} %and_select_fusion), kind=kLoop, calls=%fused_computation.86 | loop fusion | flops 2293760 | bytes 1311360 | tf_op jit(solution)/shard_map/sin | solution.py:320
  145.5 2.3 %all-to-all-done.2 = f32[8,1,2176]{2,1,0:T(1,128)S(1)} async-done(((f32[8,1,2176]{2,1,0:T(1,128)}), f32[8,1,2176]{2,1,0:T(1,128)S(1)}, u32[]{:S(2)}, u32[]{:S(2)}) %all-to-all-start.2) | async-done | bytes 69664 | tf_op jit(solution)/shard_map/all_to_all | solution.py:324
  147.8 0.5 slice.183
  148.3 0.5 fusion.76
  148.8 0.5 fusion.75
  150.0 0.6 divide_multiply_fusion
  (26 shorter events, 1.8 us)
Async XLA Ops:
  6.4 66.2 %all-to-all-start = ((bf16[128,128,128]{1,2,0:T(8,128)(2,1)}), bf16[128,128,128]{1,2,0:T(8,128)(2,1)}, u32[]{:S(2)}, u32[]{:S(2)}) async-start(bf16[128,128,128]{1,2,0:T(8,128)(2,1)} %bitcast.37), calls=%async_computation | async-start | bytes 8388608 | tf_op jit(solution)/shard_map/all_to_all | solution.py:279
  45.9 7.9 %copy-start.2 = (s32[128]{0:T(128)S(1)}, s32[128]{0:T(128)}, u32[]{:S(2)}) copy-start(s32[128]{0:T(128)} %param.6) | copy-start | bytes 1540
  45.9 7.9 %copy-start = (f32[2]{0:T(128)S(1)}, f32[2]{0:T(128)}, u32[]{:S(2)}) copy-start(f32[2]{0:T(128)} %param.7) | copy-start | bytes 28
  45.9 10.6 %copy-start.1 = (s32[128,2]{0,1:T(2,128)S(1)}, s32[128,2]{0,1:T(2,128)}, u32[]{:S(2)}) copy-start(s32[128,2]{0,1:T(2,128)} %param.5) | copy-start | bytes 3076
  121.3 14.5 %all-to-all-start.1 = ((f32[16,1,2176]{2,1,0:T(1,128)}), f32[16,1,2176]{2,1,0:T(1,128)S(1)}, u32[]{:S(2)}, u32[]{:S(2)}) async-start(f32[16,1,2176]{2,1,0:T(1,128)} %copy.10), calls=%async_computation.1 | async-start | bytes 278528 | tf_op jit(solution)/shard_map/all_to_all | solution.py:321
  136.6 11.2 %all-to-all-start.2 = ((f32[8,1,2176]{2,1,0:T(1,128)}), f32[8,1,2176]{2,1,0:T(1,128)S(1)}, u32[]{:S(2)}, u32[]{:S(2)}) async-start(f32[8,1,2176]{2,1,0:T(1,128)} %broadcast_in_dim.6), calls=%async_computation.2 | async-start | bytes 139264 | tf_op jit(solution)/shard_map/all_to_all | solution.py:324

commit v3 on v1

--- a/solution.py
+++ b/solution.py
@@ -118,15 +118,15 @@
     return values[0]
 
 
-def phase_parts(pixel_index, shifts, aberration):
+def phase_parts(pixel_index, shifts, aberration, col_index):
     freq_rows = signed_frequency(SR)[:, None]
-    freq_cols = signed_frequency(SC)[:, None]
+    freq_cols = jnp.take(signed_frequency(SC), col_index)[:, None]
     half_rows = DROWS // 2
     half_cols = DCOLS // 2
     tilt_x = ((pixel_index // DCOLS - half_rows).astype(jnp.float32) / half_rows)[None, :]
     tilt_y = ((pixel_index % DCOLS - half_cols).astype(jnp.float32) / half_cols)[None, :]
     ramp_rows = jnp.mod(jnp.arange(SR, dtype=jnp.int32)[:, None] * shifts[:, 0][None, :], SR)
-    ramp_cols = jnp.mod(jnp.arange(SC, dtype=jnp.int32)[:, None] * shifts[:, 1][None, :], SC)
+    ramp_cols = jnp.mod(col_index[:, None] * shifts[:, 1][None, :], SC)
     tilt_sq = tilt_x * tilt_x + tilt_y * tilt_y
     defocus = math.pi * aberration[0]
     spherical = math.pi * aberration[1]
@@ -185,7 +185,7 @@
     return out
 
 
-def spectrum_kernel(re_ref, im_ref, tc_ref, ts_ref, out_ref):
+def spectrum_kernel(re_ref, im_ref, lc_ref, ls_ref, uc_ref, us_ref, out_ref):
     out_ref[...] = jnp.zeros(out_ref.shape, out_ref.dtype)
 
     def body(i, carry):
@@ -193,10 +193,15 @@
         full = fft16([(re_ref[r, rows, :], im_ref[r, rows, :]) for r in range(SR)])
         for s in range(SR):
             fr, fi = full[s]
-            tc = tc_ref[s, rows, :]
-            ts = ts_ref[s, rows, :]
-            out_ref[0, s] += fr * tc - fi * ts
-            out_ref[1, s] += fr * ts + fi * tc
+            tc = lc_ref[s, rows, :]
+            ts = ls_ref[s, rows, :]
+            out_ref[0, 0, s] += fr * tc - fi * ts
+            out_ref[0, 1, s] += fr * ts + fi * tc
+            gr, gi = full[(SR - s) % SR]
+            tc = uc_ref[s, rows, :]
+            ts = us_ref[s, rows, :]
+            out_ref[1, 0, s] += gr * tc + gi * ts
+            out_ref[1, 1, s] += gr * ts - gi * tc
         return carry
 
     lax.fori_loop(0, re_ref.shape[1] // 8, body, 0)
@@ -204,21 +209,26 @@
 
 def spectrum(both_col, turn_cos, turn_sin):
     pixels = both_col.shape[1]
+    half = SC // 2
     block = 128
-    steps = SC // block
+    steps = half // block
+    lower = lambda j: (0, 0, j)
+    upper = lambda j: (0, 0, j + steps)
     spec = pl.pallas_call(
         spectrum_kernel,
         grid=(steps,),
         in_specs=[
-            pl.BlockSpec((SR, pixels, block), lambda j: (0, 0, j)),
-            pl.BlockSpec((SR, pixels, block), lambda j: (0, 0, j + steps)),
-            pl.BlockSpec((SR, pixels, block), lambda j: (0, 0, j)),
-            pl.BlockSpec((SR, pixels, block), lambda j: (0, 0, j)),
+            pl.BlockSpec((SR, pixels, block), lower),
+            pl.BlockSpec((SR, pixels, block), upper),
+            pl.BlockSpec((SR, pixels, block), lower),
+            pl.BlockSpec((SR, pixels, block), lower),
+            pl.BlockSpec((SR, pixels, block), upper),
+            pl.BlockSpec((SR, pixels, block), upper),
         ],
-        out_specs=pl.BlockSpec((2, SR, 8, block), lambda j: (0, 0, 0, j)),
-        out_shape=jax.ShapeDtypeStruct((2, SR, 8, SC), jnp.float32),
-    )(both_col, both_col, turn_cos, turn_sin)
-    return jnp.sum(spec, axis=2)
+        out_specs=pl.BlockSpec((2, 2, SR, 8, block), lambda j: (0, 0, 0, 0, j)),
+        out_shape=jax.ShapeDtypeStruct((2, 2, SR, 8, half), jnp.float32),
+    )(both_col, both_col, turn_cos, turn_sin, turn_cos, turn_sin)
+    return jnp.sum(spec, axis=3)
 
 
 def local(frames, offsets, bright, aberration):
@@ -235,26 +245,50 @@
     col_sin, col_cos = sincos_of_steps(jnp.mod(full_cols[:, None] * full_cols[None, :], SC), SC)
     col_cos = col_cos.astype(jnp.bfloat16)
     col_sin = col_sin.astype(jnp.bfloat16)
-    table = jnp.concatenate([col_cos, -col_sin], axis=1).reshape(scan_size, tile, 2 * SC)
+    half = SC // 2
+    nyquist = jnp.zeros((SC, 128), jnp.bfloat16).at[:, 0].set(col_cos[:, half])
+    table = jnp.concatenate([col_cos[:, :half], -col_sin[:, :half], nyquist], axis=1)
     both_col = jnp.einsum(
-        "abrcp,acq->brpq", images, table, preferred_element_type=jnp.float32
-    ).reshape(SR, owned, 2 * SC)
+        "abrcp,acq->brpq",
+        images,
+        table.reshape(scan_size, tile, table.shape[1]),
+        preferred_element_type=jnp.float32,
+    ).reshape(SR, owned, table.shape[1])
     full_rows = jnp.arange(SR, dtype=jnp.int32)
     angles_by_row = phase_angles(full_rows, full_rows, SR)
     row_cos = jnp.cos(angles_by_row)
     row_sin = jnp.sin(angles_by_row)
     pixel_index = owner * owned + jnp.arange(owned, dtype=jnp.int32)
+    steps = jnp.arange(half, dtype=jnp.int32)
+    col_index = jnp.concatenate([steps, jnp.mod(SC - steps, SC), jnp.full((1,), half, jnp.int32)])
     row_part, col_part, moved_rows, moved_cols, spherical = phase_parts(
-        pixel_index, offsets, aberration
+        pixel_index, offsets, aberration, col_index
     )
     moved_sq = moved_rows[:, :, None] + moved_cols.T[None, :, :]
     phase = row_part[:, :, None] + col_part.T[None, :, :] - spherical * (moved_sq * moved_sq)
     weights = bright.astype(jnp.float32)
+    keep = (jnp.arange(SC + 1) != half).astype(jnp.float32)
     turn_sin, turn_cos = sincos(phase)
     turn_cos, turn_sin = lax.optimization_barrier(
-        (turn_cos * weights[None, :, None], turn_sin * weights[None, :, None])
-    )
-    spec_real, spec_imag = spectrum(both_col, turn_cos, turn_sin)
+        (
+            turn_cos * weights[None, :, None] * keep[None, None, :],
+            turn_sin * weights[None, :, None] * keep[None, None, :],
+        )
+    )
+    parts = spectrum(both_col, turn_cos, turn_sin)
+    nyquist_col = both_col[:, :, SC]
+    nyquist_real = jnp.dot(row_cos.T, nyquist_col, precision=EXACT_PRECISION)
+    nyquist_imag = -jnp.dot(row_sin.T, nyquist_col, precision=EXACT_PRECISION)
+    last_cos = turn_cos[:, :, SC]
+    last_sin = turn_sin[:, :, SC]
+    nyquist_spec_real = jnp.sum(nyquist_real * last_cos - nyquist_imag * last_sin, axis=1)
+    nyquist_spec_imag = jnp.sum(nyquist_real * last_sin + nyquist_imag * last_cos, axis=1)
+    spec_real = jnp.concatenate(
+        [parts[0, 0], nyquist_spec_real[:, None], parts[1, 0, :, :0:-1]], axis=1
+    )
+    spec_imag = jnp.concatenate(
+        [parts[0, 1], nyquist_spec_imag[:, None], parts[1, 1, :, :0:-1]], axis=1
+    )
     row_cos_t = row_cos.T
     row_sin_t = row_sin.T
     rows_real = jnp.dot(row_cos_t, spec_real, precision=EXACT_PRECISION) - jnp.dot(

time: 131 us -> 128 us (0.977)
  waiting for transfers between devices: 26.1 us -> 10.5 us
  other arithmetic: 39 us -> 49.7 us
  local copies, waits for them, and re-layouts: 9.63 us -> 17.6 us
  matrix products: 16.8 us -> 12.7 us
  Pallas kernels: 15.3 us -> 11.3 us
  starting transfers between devices: 20.4 us -> 22.7 us
    all_to_all x1, waiting for transfers between devices: 15.5 us -> 0.01 us  [local(): lax.all_to_all(blocks, ('scan', 'det'), split_axis=0, concat_axis=0, tile...]
    neg x1, other arithmetic: 8.29 us -> 0.91 us  [local(): -col_sin[:, :half]]
    add x0 -> x1, other arithmetic: none -> 7.22 us  [sincos_reduced(): rest + rest * square * (-0.16666654611 + square * (0.0083321608736 + squa...]
    eq x0 -> x1, other arithmetic: none -> 4.96 us  [sincos_reduced(): swap = quadrant & 1 == 1]
    gather x0 -> x1, local copies, waits for them, and re-layouts: none -> 4.36 us  [phase_parts(): freq_cols = jnp.take(signed_frequency(SC), col_index)[:, None]]
    and x0 -> x1, other arithmetic: none -> 4.3 us  [sincos_of_steps(): return sincos_reduced(rest, turns & 3)]
    dot_general x1 -> x3, matrix products: 14.6 us -> 10.4 us  [the longest x1 9.72 us: local(): jnp.einsum('abrcp,acq->brpq', images, table.reshape(scan_size, tile, tabl...]
    pallas_call x1, Pallas kernels: 15.3 us -> 11.3 us  [spectrum(): pl.pallas_call(spectrum_kernel, grid=(steps,), in_specs=[pl.BlockSpec((SR...]
  transfers between devices with their start and end apart: 3 -> 3, of which waited for: 3 -> 2; matrix products, arithmetic and copies ran while one was open for 29% -> 42% of each run, Pallas kernels for 0% -> 0%
where the time goes in v3:
time: 128 us
  other arithmetic  49.7 us (39%)
  starting transfers between devices  22.7 us (18%)
  local copies, waits for them, and re-layouts  17.6 us (14%)
  matrix products  12.7 us (10%)
  Pallas kernels  11.3 us (9%)
  waiting for transfers between devices  10.5 us (8%)
  between operations  2.99 us (2%)
    mul x1, other arithmetic, local(): turn_sin * weights[None, :, None] * keep[None, None, :]  14.8 us
    all_to_all x1, starting transfers between devices, local(): lax.all_to_all(blocks, ('scan', 'det'), split_axis=0, concat_axis=0, tile...  11.7 us
    pallas_call x1, Pallas kernels, spectrum(): pl.pallas_call(spectrum_kernel, grid=(steps,), in_specs=[pl.BlockSpec((SR...  11.3 us
    dot_general x1, matrix products, local(): jnp.einsum('abrcp,acq->brpq', images, table.reshape(scan_size, tile, tabl...  9.72 us
    all_to_all x1, waiting for transfers between devices, local(): gathered = lax.all_to_all(packed, 'det', 0, 0, tiled=True)  8.26 us
    convert_element_type x1, other arithmetic, local(): col_cos = col_cos.astype(jnp.bfloat16)  8.25 us
    add x1, other arithmetic, sincos_reduced(): rest + rest * square * (-0.16666654611 + square * (0.0083321608736 + squa...  7.22 us
    unnamed x15, local copies, waits for them, and re-layouts  7.04 us
  transfers between devices with their start and end apart: 3, of which 2 were waited for; matrix products, arithmetic and copies ran while one was open for 42% of the time, Pallas kernels for 0%

profile of v3, /device:TPU:0, one launch (start us, length us, event | category | flops | bytes accessed | tf_op | source)
XLA Modules:
  0.0 127.6 jit_solution(6328757276987581597)
XLA Ops:
  0.0 6.4 %copy.24 = bf16[1,128,16384]{1,2,0:T(8,128)(2,1)} copy(bf16[1,128,16384]{2,1,0:T(8,128)(2,1)} %param.6) | data formatting | bytes 8388608 | tf_op args[0]
  6.4 11.7 %all-to-all-start = ((bf16[128,128,128]{1,2,0:T(8,128)(2,1)}), bf16[128,128,128]{1,2,0:T(8,128)(2,1)}, u32[]{:S(2)}, u32[]{:S(2)}) async-start(bf16[128,128,128]{1,2,0:T(8,128)(2,1)} %bitcast.57), calls=%async_computation | async-start | bytes 8388608 | tf_op jit(solution)/shard_map/all_to_all | solution.py:242
  18.1 8.3 %fusion.29 = bf16[1024,1024]{1,0:T(8,128)(2,1)S(1)} fusion(), kind=kLoop, calls=%fused_computation.61 | loop fusion | flops 61865984 | bytes 2097152 | tf_op jit(solution)/shard_map/convert_element_type | solution.py:246
  26.4 0.8 compare_reduce_fusion
  27.9 0.7 slice_select_fusion.1
  31.2 4.4 %gather_fusion = f32[1025]{0:T(1024)S(1)} fusion(f32[1024]{0:T(1024)S(1)} %fusion.78, s32[2048]{0:T(1024)S(1)} %pad_clamp_fusion), kind=kCustom, calls=%fused_computation | custom fusion | bytes 12300 | tf_op jit(solution)/shard_map/jit(_take)/gather | solution.py:123
  36.2 14.8 %fusion.12 = (f32[16,128,1025]{2,1,0:T(8,128)S(1)}, f32[16,128,1025]{2,1,0:T(8,128)S(1)}) fusion(f32[1025]{0:T(1024)S(1)} %fusion.75, f32[128]{0:T(128)S(1)} %convert_element_type.126, f32[128,1025]{1,0:T(8,128)S(1)} %get-tuple-element.36, f32[16,128]{1,0:T(8,128)S(1)} %get-tuple-element.42, f32[]{:T(128)} %bitcast.9, f32[128,1025]{1,0:T(8,128)S(1)} %get-tuple-element.35, ...), kind=kLoop, calls=%fused_computation.22 | loop fusion | flops 100761600 | bytes 17864200 | tf_op jit(solution)/shard_map/mul | solution.py:275
  51.7 0.7 broadcast_in_dim.18
  52.4 4.3 %broadcast_and_fusion = s32[1024,1024]{1,0:T(8,128)S(1)} fusion(), kind=kLoop, calls=%fused_computation.74 | loop fusion | flops 30408704 | bytes 4194304 | tf_op jit(solution)/shard_map/and | solution.py:109
  56.7 5.0 %and_compare_fusion.1 = pred[1024,1024]{1,0:T(8,128)(4,1)S(1)} fusion(), kind=kLoop, calls=%fused_computation.63 | loop fusion | flops 32505856 | bytes 1048576 | tf_op jit(solution)/shard_map/eq | solution.py:88
  61.7 7.2 %fusion.19 = (f32[1024,1024]{1,0:T(8,128)S(1)}, f32[1024,1024]{1,0:T(8,128)S(1)}) fusion(), kind=kLoop, calls=%fused_computation.51 | loop fusion | flops 51380224 | bytes 8388608 | tf_op jit(solution)/shard_map/add | solution.py:82
  68.9 0.9 fusion.39
  70.3 9.7 %convolution_bitcast_fusion.re_ref.im_ref = f32[16,128,1152]{2,1,0:T(8,128)} fusion(bf16[8,128,1152,1]{2,1,3,0:T(8,128)(2,1)S(1)} %bitcast.58, bf16[8,16,128,128]{2,3,1,0:T(8,128)(2,1)} %bitcast.4), kind=kOutput, calls=%fused_computation.32 | convolution fusion | flops 4831838208 | bytes 15990784 | tf_op jit(solution)/shard_map/abrcp,acq->brpq/dot_general | solution.py:251
  80.1 11.3 %shard_map.46 = f32[2,2,16,8,512]{4,3,2,1,0:T(8,128)} custom-call(f32[16,128,1152]{2,1,0:T(8,128)} %convolution_bitcast_fusion.re_ref.im_ref, f32[16,128,1152]{2,1,0:T(8,128)} %convolution_bitcast_fusion.re_ref.im_ref, f32[16,128,1025]{2,1,0:T(8,128)} %copy-done.1, f32[16,128,1025]{2,1,0:T(8,128)} %copy-done, f32[16,128,1025]{2,1,0:T(8,128)} %copy-done.1, ...), custom_call_target="tpu_custom_call" | custom-call | tf_op jit(solution)/shard_map/pallas_call | solution.py:217
  91.4 1.6 %slice_reduce_fusion = f32[16,128]{1,0:T(8,128)S(1)} fusion(f32[16,128,1152]{2,1,0:T(8,128)} %convolution_bitcast_fusion.re_ref.im_ref), kind=kLoop, calls=%fused_computation.88 | loop fusion | bytes 16384 | tf_op jit(solution)/shard_map/slice | solution.py:279
  93.0 1.5 %reduce_sum.36 = f32[2,2,16,512]{3,2,1,0:T(8,128)S(1)} reduce(f32[2,2,16,8,512]{4,3,2,1,0:T(8,128)} %shard_map.46, f32[]{:T(128)} %constant.275.clone.1), dimensions={3}, to_apply=%region_1.2 | reduce | flops 229376 | bytes 1179652 | tf_op jit(solution)/shard_map/reduce_sum | solution.py:231
  97.5 0.8 copy.31
  98.3 6.2 %all-to-all-start.1 = ((f32[16,1,2176]{2,1,0:T(1,128)}), f32[16,1,2176]{2,1,0:T(1,128)S(1)}, u32[]{:S(2)}, u32[]{:S(2)}) async-start(f32[16,1,2176]{2,1,0:T(1,128)} %copy.31), calls=%async_computation.1 | async-start | bytes 278528 | tf_op jit(solution)/shard_map/all_to_all | solution.py:309
  104.5 8.3 %all-to-all-done.1 = f32[16,1,2176]{2,1,0:T(1,128)S(1)} async-done(((f32[16,1,2176]{2,1,0:T(1,128)}), f32[16,1,2176]{2,1,0:T(1,128)S(1)}, u32[]{:S(2)}, u32[]{:S(2)}) %all-to-all-start.1) | async-done | bytes 139296 | tf_op jit(solution)/shard_map/all_to_all | solution.py:309
  112.8 0.7 broadcast_in_dim.19
  113.5 4.8 %all-to-all-start.2 = ((f32[8,1,2176]{2,1,0:T(1,128)}), f32[8,1,2176]{2,1,0:T(1,128)S(1)}, u32[]{:S(2)}, u32[]{:S(2)}) async-start(f32[8,1,2176]{2,1,0:T(1,128)} %broadcast_in_dim.19), calls=%async_computation.2 | async-start | bytes 139264 | tf_op jit(solution)/shard_map/all_to_all | solution.py:312
  118.3 4.1 %fusion.48 = (f32[1024,160]{1,0:T(8,128)S(1)}, f32[1024,160]{1,0:T(8,128)S(1)}) fusion(s32[160]{0:T(256)S(1)} %and_select_fusion.1), kind=kLoop, calls=%fused_computation.102 | loop fusion | flops 2293760 | bytes 1311360 | tf_op jit(solution)/shard_map/sin | solution.py:308
  122.4 2.3 %all-to-all-done.2 = f32[8,1,2176]{2,1,0:T(1,128)S(1)} async-done(((f32[8,1,2176]{2,1,0:T(1,128)}), f32[8,1,2176]{2,1,0:T(1,128)S(1)}, u32[]{:S(2)}, u32[]{:S(2)}) %all-to-all-start.2) | async-done | bytes 69664 | tf_op jit(solution)/shard_map/all_to_all | solution.py:312
  126.9 0.6 divide_multiply_fusion
  (59 shorter events, 7.7 us)
Async XLA Ops:
  6.4 20.9 %copy-start.5 = (s32[128]{0:T(128)S(1)}, s32[128]{0:T(128)}, u32[]{:S(2)}) copy-start(s32[128]{0:T(128)} %param.8) | copy-start | bytes 1540
  6.4 63.9 %all-to-all-start = ((bf16[128,128,128]{1,2,0:T(8,128)(2,1)}), bf16[128,128,128]{1,2,0:T(8,128)(2,1)}, u32[]{:S(2)}, u32[]{:S(2)}) async-start(bf16[128,128,128]{1,2,0:T(8,128)(2,1)} %bitcast.57), calls=%async_computation | async-start | bytes 8388608 | tf_op jit(solution)/shard_map/all_to_all | solution.py:242
  18.1 10.5 %copy-start.3 = (f32[2]{0:T(128)S(1)}, f32[2]{0:T(128)}, u32[]{:S(2)}) copy-start(f32[2]{0:T(128)} %param.9) | copy-start | bytes 28
  18.1 12.4 %copy-start.4 = (s32[128,2]{0,1:T(2,128)S(1)}, s32[128,2]{0,1:T(2,128)}, u32[]{:S(2)}) copy-start(s32[128,2]{0,1:T(2,128)} %param.7) | copy-start | bytes 3076
  26.4 9.2 %copy-start.2 = (bf16[1024,1024]{1,0:T(8,128)(2,1)}, bf16[1024,1024]{1,0:T(8,128)(2,1)S(1)}, u32[]{:S(2)}) copy-start(bf16[1024,1024]{1,0:T(8,128)(2,1)S(1)} %fusion.29) | copy-start | bytes 6291460
  51.0 17.9 %copy-start = (f32[16,128,1025]{2,1,0:T(8,128)}, f32[16,128,1025]{2,1,0:T(8,128)S(1)}, u32[]{:S(2)}) copy-start(f32[16,128,1025]{2,1,0:T(8,128)S(1)} %get-tuple-element.22.ls_ref.us_ref) | copy-start | bytes 25190404
  51.0 17.9 %copy-start.1 = (f32[16,128,1025]{2,1,0:T(8,128)}, f32[16,128,1025]{2,1,0:T(8,128)S(1)}, u32[]{:S(2)}) copy-start(f32[16,128,1025]{2,1,0:T(8,128)S(1)} %get-tuple-element.21.lc_ref.uc_ref) | copy-start | bytes 25190404
  68.9 1.2 slice-start
  98.3 14.5 %all-to-all-start.1 = ((f32[16,1,2176]{2,1,0:T(1,128)}), f32[16,1,2176]{2,1,0:T(1,128)S(1)}, u32[]{:S(2)}, u32[]{:S(2)}) async-start(f32[16,1,2176]{2,1,0:T(1,128)} %copy.31), calls=%async_computation.1 | async-start | bytes 278528 | tf_op jit(solution)/shard_map/all_to_all | solution.py:309
  113.5 11.2 %all-to-all-start.2 = ((f32[8,1,2176]{2,1,0:T(1,128)}), f32[8,1,2176]{2,1,0:T(1,128)S(1)}, u32[]{:S(2)}, u32[]{:S(2)}) async-start(f32[8,1,2176]{2,1,0:T(1,128)} %broadcast_in_dim.19), calls=%async_computation.2 | async-start | bytes 139264 | tf_op jit(solution)/shard_map/all_to_all | solution.py:312

commit v4 on v3

--- a/solution.py
+++ b/solution.py
@@ -5,6 +5,7 @@
 from jax import lax
 from jax.sharding import PartitionSpec as P
 from jax.experimental import pallas as pl
+from jax.experimental.pallas import tpu as pltpu
 
 SR = 16
 SC = 1024
@@ -120,7 +121,7 @@
 
 def phase_parts(pixel_index, shifts, aberration, col_index):
     freq_rows = signed_frequency(SR)[:, None]
-    freq_cols = jnp.take(signed_frequency(SC), col_index)[:, None]
+    freq_cols = (2.0 * jnp.where(col_index < SC // 2, col_index, col_index - SC).astype(jnp.float32) / SC)[:, None]
     half_rows = DROWS // 2
     half_cols = DCOLS // 2
     tilt_x = ((pixel_index // DCOLS - half_rows).astype(jnp.float32) / half_rows)[None, :]
@@ -185,8 +186,8 @@
     return out
 
 
-def spectrum_kernel(re_ref, im_ref, lc_ref, ls_ref, uc_ref, us_ref, out_ref):
-    out_ref[...] = jnp.zeros(out_ref.shape, out_ref.dtype)
+def spectrum_kernel(re_ref, im_ref, lc_ref, ls_ref, uc_ref, us_ref, out_ref, acc_ref):
+    acc_ref[...] = jnp.zeros(acc_ref.shape, acc_ref.dtype)
 
     def body(i, carry):
         rows = pl.ds(pl.multiple_of(i * 8, 8), 8)
@@ -195,16 +196,19 @@
             fr, fi = full[s]
             tc = lc_ref[s, rows, :]
             ts = ls_ref[s, rows, :]
-            out_ref[0, 0, s] += fr * tc - fi * ts
-            out_ref[0, 1, s] += fr * ts + fi * tc
+            acc_ref[0, 0, s] += fr * tc - fi * ts
+            acc_ref[0, 1, s] += fr * ts + fi * tc
             gr, gi = full[(SR - s) % SR]
             tc = uc_ref[s, rows, :]
             ts = us_ref[s, rows, :]
-            out_ref[1, 0, s] += gr * tc + gi * ts
-            out_ref[1, 1, s] += gr * ts - gi * tc
+            acc_ref[1, 0, s] += gr * tc + gi * ts
+            acc_ref[1, 1, s] += gr * ts - gi * tc
         return carry
 
     lax.fori_loop(0, re_ref.shape[1] // 8, body, 0)
+    for a in range(2):
+        for b in range(2):
+            out_ref[a, b] = jnp.sum(acc_ref[a, b], axis=1)
 
 
 def spectrum(both_col, turn_cos, turn_sin):
@@ -225,10 +229,11 @@
             pl.BlockSpec((SR, pixels, block), upper),
             pl.BlockSpec((SR, pixels, block), upper),
         ],
-        out_specs=pl.BlockSpec((2, 2, SR, 8, block), lambda j: (0, 0, 0, 0, j)),
-        out_shape=jax.ShapeDtypeStruct((2, 2, SR, 8, half), jnp.float32),
+        out_specs=pl.BlockSpec((2, 2, SR, block), lambda j: (0, 0, 0, j)),
+        out_shape=jax.ShapeDtypeStruct((2, 2, SR, half), jnp.float32),
+        scratch_shapes=[pltpu.VMEM((2, 2, SR, 8, block), jnp.float32)],
     )(both_col, both_col, turn_cos, turn_sin, turn_cos, turn_sin)
-    return jnp.sum(spec, axis=3)
+    return spec
 
 
 def local(frames, offsets, bright, aberration):
@@ -241,13 +246,14 @@
     blocks = jnp.transpose(frames.reshape(rows_dev * tile, groups, owned), (1, 0, 2))
     arrived = lax.all_to_all(blocks, ("scan", "det"), split_axis=0, concat_axis=0, tiled=True)
     images = arrived.reshape(scan_size, det_size, rows_dev, tile, owned)
+    half = SC // 2
     full_cols = jnp.arange(SC, dtype=jnp.int32)
-    col_sin, col_cos = sincos_of_steps(jnp.mod(full_cols[:, None] * full_cols[None, :], SC), SC)
-    col_cos = col_cos.astype(jnp.bfloat16)
-    col_sin = col_sin.astype(jnp.bfloat16)
-    half = SC // 2
-    nyquist = jnp.zeros((SC, 128), jnp.bfloat16).at[:, 0].set(col_cos[:, half])
-    table = jnp.concatenate([col_cos[:, :half], -col_sin[:, :half], nyquist], axis=1)
+    col_sin, col_cos = sincos_of_steps(
+        jnp.mod(full_cols[:, None] * full_cols[None, :half], SC), SC
+    )
+    alternating = jnp.where(full_cols % 2 == 0, 1.0, -1.0)
+    nyquist = jnp.where(jnp.arange(128)[None, :] == 0, alternating[:, None], 0.0)
+    table = jnp.concatenate([col_cos, -col_sin, nyquist], axis=1).astype(jnp.bfloat16)
     both_col = jnp.einsum(
         "abrcp,acq->brpq",
         images,

time: 128 us -> 125 us (0.977)
  other arithmetic: 49.7 us -> 25.6 us
  waiting for transfers between devices: 10.5 us -> 33.1 us
  starting transfers between devices: 22.7 us -> 20.2 us
    all_to_all x1, waiting for transfers between devices: 0.01 us -> 22.6 us  [local(): lax.all_to_all(blocks, ('scan', 'det'), split_axis=0, concat_axis=0, tile...]
    convert_element_type x1 -> x0, other arithmetic: 8.25 us -> none  [local(): col_cos = col_cos.astype(jnp.bfloat16)]
    add x1 -> x0, other arithmetic: 7.22 us -> none  [sincos_reduced(): rest + rest * square * (-0.16666654611 + square * (0.0083321608736 + squa...]
    eq x1, other arithmetic: 4.96 us -> 0.01 us  [local(): jnp.arange(128)[None, :] == 0]
    gather x1 -> x0, local copies, waits for them, and re-layouts: 4.36 us -> none  [phase_parts(): freq_cols = jnp.take(signed_frequency(SC), col_index)[:, None]]
    and x1 -> x0, other arithmetic: 4.3 us -> none  [sincos_of_steps(): return sincos_reduced(rest, turns & 3)]
    unnamed x15 -> x13, local copies, waits for them, and re-layouts: 7.04 us -> 11.3 us
    another operation x2, other arithmetic: 1.48 us -> 4.75 us
  transfers between devices with their start and end apart: 3 -> 3, of which waited for: 2 -> 3; matrix products, arithmetic and copies ran while one was open for 42% -> 22% of each run, Pallas kernels for 0% -> 0%
where the time goes in v4:
time: 125 us; the launch traced here: 124 us
  waiting for transfers between devices  33.1 us (26%)
  other arithmetic  25.6 us (20%)
  starting transfers between devices  20.2 us (16%)
  local copies, waits for them, and re-layouts  18.7 us (15%)
  matrix products  12.7 us (10%)
  Pallas kernels  11.3 us (9%)
  between operations  2.86 us (2%)
    all_to_all x1, waiting for transfers between devices, local(): lax.all_to_all(blocks, ('scan', 'det'), split_axis=0, concat_axis=0, tile...  22.6 us
    mul x1, other arithmetic, local(): turn_sin * weights[None, :, None] * keep[None, None, :]  14.7 us
    all_to_all x1, starting transfers between devices, local(): lax.all_to_all(blocks, ('scan', 'det'), split_axis=0, concat_axis=0, tile...  11.7 us
    unnamed x13, local copies, waits for them, and re-layouts  11.3 us
    pallas_call x1, Pallas kernels, spectrum(): pl.pallas_call(spectrum_kernel, grid=(steps,), in_specs=[pl.BlockSpec((SR...  11.3 us
    dot_general x1, matrix products, local(): jnp.einsum('abrcp,acq->brpq', images, table.reshape(scan_size, tile, tabl...  9.7 us
    all_to_all x1, waiting for transfers between devices, local(): gathered = lax.all_to_all(packed, 'det', 0, 0, tiled=True)  8.26 us
    another operation x2, other arithmetic  4.75 us
  transfers between devices with their start and end apart: 3, of which 3 were waited for; matrix products, arithmetic and copies ran while one was open for 22% of the time, Pallas kernels for 0%

profile of v4, /device:TPU:0, one launch (start us, length us, event | category | flops | bytes accessed | tf_op | source)
XLA Modules:
  0.0 124.4 jit_solution(8879318117352862356)
XLA Ops:
  0.0 6.4 %copy.22 = bf16[1,128,16384]{1,2,0:T(8,128)(2,1)} copy(bf16[1,128,16384]{2,1,0:T(8,128)(2,1)} %param.4) | data formatting | bytes 8388608 | tf_op args[0]
  6.4 11.7 %all-to-all-start = ((bf16[128,128,128]{1,2,0:T(8,128)(2,1)}), bf16[128,128,128]{1,2,0:T(8,128)(2,1)}, u32[]{:S(2)}, u32[]{:S(2)}) async-start(bf16[128,128,128]{1,2,0:T(8,128)(2,1)} %bitcast.55), calls=%async_computation | async-start | bytes 8388608 | tf_op jit(solution)/shard_map/all_to_all | solution.py:247
  18.2 0.6 fusion.129
  21.3 14.7 %fusion.12 = (f32[16,128,1025]{2,1,0:T(8,128)S(1)}, f32[16,128,1025]{2,1,0:T(8,128)S(1)}) fusion(f32[1025]{0:T(1024)S(1)} %fusion.77, f32[128]{0:T(128)S(1)} %convert_element_type.125, f32[128,1025]{1,0:T(8,128)S(1)} %get-tuple-element.22, f32[16,128]{1,0:T(8,128)S(1)} %get-tuple-element.32, f32[]{:T(128)} %bitcast.8, f32[128,1025]{1,0:T(8,128)S(1)} %get-tuple-element.21, ...), kind=kLoop, calls=%fused_computation.21 | loop fusion | flops 100761600 | bytes 17864200 | tf_op jit(solution)/shard_map/mul | solution.py:281
  36.0 0.7 convert_reduce_fusion
  36.7 0.7 broadcast_in_dim.44
  37.8 1.8 %copy-done = f32[16,128,1025]{2,1,0:T(8,128)} copy-done((f32[16,128,1025]{2,1,0:T(8,128)}, f32[16,128,1025]{2,1,0:T(8,128)S(1)}, u32[]{:S(2)}) %copy-start) | copy-done | bytes 8396824
  39.9 2.5 %copy-done.1 = f32[16,128,1025]{2,1,0:T(8,128)} copy-done((f32[16,128,1025]{2,1,0:T(8,128)}, f32[16,128,1025]{2,1,0:T(8,128)S(1)}, u32[]{:S(2)}) %copy-start.1) | copy-done | bytes 8396824
  42.5 4.6 %fusion.33 = (bf16[8,128,512]{1,2,0:T(8,128)(2,1)S(1)}, bf16[8,128,512]{1,2,0:T(8,128)(2,1)S(1)}) fusion(s32[512]{0:T(512)S(1)} %slice.150, s32[8,128]{1,0:T(8,128)S(1)} %multiply_add_fusion), kind=kLoop, calls=%fused_computation.66 | loop fusion | flops 34078720 | bytes 2103296 | tf_op jit(solution)/shard_map/convert
  47.2 22.6 %all-to-all-done = bf16[128,128,128]{1,2,0:T(8,128)(2,1)} async-done(((bf16[128,128,128]{1,2,0:T(8,128)(2,1)}), bf16[128,128,128]{1,2,0:T(8,128)(2,1)}, u32[]{:S(2)}, u32[]{:S(2)}) %all-to-all-start) | async-done | bytes 4194336 | tf_op jit(solution)/shard_map/all_to_all | solution.py:247
  69.7 9.7 %convolution_bitcast_fusion.re_ref.im_ref = f32[16,128,1152]{2,1,0:T(8,128)} fusion(bf16[8,16,128,128]{2,3,1,0:T(8,128)(2,1)} %bitcast.3, bf16[8,128,128]{1,2,0:T(8,128)(2,1)S(1)} %select_convert_fusion, bf16[8,128,512]{1,2,0:T(8,128)(2,1)S(1)} %get-tuple-element.24, bf16[8,128,512]{1,2,0:T(8,128)(2,1)S(1)} %get-tuple-element.23), kind=kOutput, calls=%fused_computation.31 | convolution fusion | flops 4838916096 | bytes 15990784 | tf_op jit(solution)/shard_map/abrcp,acq->brpq/dot_general | solution.py:257
  79.4 11.3 %shard_map.46 = f32[2,2,16,512]{3,2,1,0:T(8,128)} custom-call(f32[16,128,1152]{2,1,0:T(8,128)} %convolution_bitcast_fusion.re_ref.im_ref, f32[16,128,1152]{2,1,0:T(8,128)} %convolution_bitcast_fusion.re_ref.im_ref, f32[16,128,1025]{2,1,0:T(8,128)} %copy-done.1, f32[16,128,1025]{2,1,0:T(8,128)} %copy-done, f32[16,128,1025]{2,1,0:T(8,128)} %copy-done.1, ...), custom_call_target="tpu_custom_call" | custom-call | tf_op jit(solution)/shard_map/pallas_call | solution.py:221
  90.7 1.6 %slice_reduce_fusion = f32[16,128]{1,0:T(8,128)S(1)} fusion(f32[16,128,1152]{2,1,0:T(8,128)} %convolution_bitcast_fusion.re_ref.im_ref), kind=kLoop, calls=%fused_computation.86 | loop fusion | bytes 16384 | tf_op jit(solution)/shard_map/slice | solution.py:285
  92.3 0.9 fusion.128
  93.1 0.8 slice_bitcast_fusion
  96.8 0.8 copy.28
  97.6 4.1 %all-to-all-start.1 = ((f32[16,1,2176]{2,1,0:T(1,128)}), f32[16,1,2176]{2,1,0:T(1,128)S(1)}, u32[]{:S(2)}, u32[]{:S(2)}) async-start(f32[16,1,2176]{2,1,0:T(1,128)} %copy.28), calls=%async_computation.1 | async-start | bytes 278528 | tf_op jit(solution)/shard_map/all_to_all | solution.py:315
  101.8 8.3 %all-to-all-done.1 = f32[16,1,2176]{2,1,0:T(1,128)S(1)} async-done(((f32[16,1,2176]{2,1,0:T(1,128)}), f32[16,1,2176]{2,1,0:T(1,128)S(1)}, u32[]{:S(2)}, u32[]{:S(2)}) %all-to-all-start.1) | async-done | bytes 139296 | tf_op jit(solution)/shard_map/all_to_all | solution.py:315
  110.1 0.7 broadcast_in_dim.72
  110.8 4.4 %all-to-all-start.2 = ((f32[8,1,2176]{2,1,0:T(1,128)}), f32[8,1,2176]{2,1,0:T(1,128)S(1)}, u32[]{:S(2)}, u32[]{:S(2)}) async-start(f32[8,1,2176]{2,1,0:T(1,128)} %broadcast_in_dim.72), calls=%async_computation.2 | async-start | bytes 139264 | tf_op jit(solution)/shard_map/all_to_all | solution.py:318
  115.2 4.1 %fusion.49 = (f32[1024,160]{1,0:T(8,128)S(1)}, f32[1024,160]{1,0:T(8,128)S(1)}) fusion(s32[160]{0:T(256)S(1)} %and_select_fusion), kind=kLoop, calls=%fused_computation.100 | loop fusion | flops 2293760 | bytes 1311360 | tf_op jit(solution)/shard_map/sin | solution.py:314
  119.3 2.3 %all-to-all-done.2 = f32[8,1,2176]{2,1,0:T(1,128)S(1)} async-done(((f32[8,1,2176]{2,1,0:T(1,128)}), f32[8,1,2176]{2,1,0:T(1,128)S(1)}, u32[]{:S(2)}, u32[]{:S(2)}) %all-to-all-start.2) | async-done | bytes 69664 | tf_op jit(solution)/shard_map/all_to_all | solution.py:318
  122.1 0.5 fusion.81
  123.8 0.6 divide_multiply_fusion
  (48 shorter events, 5.5 us)
Async XLA Ops:
  6.4 11.8 %copy-start.4 = (s32[128]{0:T(128)S(1)}, s32[128]{0:T(128)}, u32[]{:S(2)}) copy-start(s32[128]{0:T(128)} %param.6) | copy-start | bytes 1540
  6.4 11.8 %copy-start.2 = (f32[2]{0:T(128)S(1)}, f32[2]{0:T(128)}, u32[]{:S(2)}) copy-start(f32[2]{0:T(128)} %param.7) | copy-start | bytes 28
  6.4 13.1 %copy-start.3 = (s32[128,2]{0,1:T(2,128)S(1)}, s32[128,2]{0,1:T(2,128)}, u32[]{:S(2)}) copy-start(s32[128,2]{0,1:T(2,128)} %param.5) | copy-start | bytes 3076
  6.4 63.4 %all-to-all-start = ((bf16[128,128,128]{1,2,0:T(8,128)(2,1)}), bf16[128,128,128]{1,2,0:T(8,128)(2,1)}, u32[]{:S(2)}, u32[]{:S(2)}) async-start(bf16[128,128,128]{1,2,0:T(8,128)(2,1)} %bitcast.55), calls=%async_computation | async-start | bytes 8388608 | tf_op jit(solution)/shard_map/all_to_all | solution.py:247
  36.0 3.6 %copy-start = (f32[16,128,1025]{2,1,0:T(8,128)}, f32[16,128,1025]{2,1,0:T(8,128)S(1)}, u32[]{:S(2)}) copy-start(f32[16,128,1025]{2,1,0:T(8,128)S(1)} %get-tuple-element.10.ls_ref.us_ref) | copy-start | bytes 25190404
  36.0 6.4 %copy-start.1 = (f32[16,128,1025]{2,1,0:T(8,128)}, f32[16,128,1025]{2,1,0:T(8,128)S(1)}, u32[]{:S(2)}) copy-start(f32[16,128,1025]{2,1,0:T(8,128)S(1)} %get-tuple-element.9.lc_ref.uc_ref) | copy-start | bytes 25190404
  97.6 12.4 %all-to-all-start.1 = ((f32[16,1,2176]{2,1,0:T(1,128)}), f32[16,1,2176]{2,1,0:T(1,128)S(1)}, u32[]{:S(2)}, u32[]{:S(2)}) async-start(f32[16,1,2176]{2,1,0:T(1,128)} %copy.28), calls=%async_computation.1 | async-start | bytes 278528 | tf_op jit(solution)/shard_map/all_to_all | solution.py:315
  110.8 10.8 %all-to-all-start.2 = ((f32[8,1,2176]{2,1,0:T(1,128)}), f32[8,1,2176]{2,1,0:T(1,128)S(1)}, u32[]{:S(2)}, u32[]{:S(2)}) async-start(f32[8,1,2176]{2,1,0:T(1,128)} %broadcast_in_dim.72), calls=%async_computation.2 | async-start | bytes 139264 | tf_op jit(solution)/shard_map/all_to_all | solution.py:318

commit v5 on v4

--- a/solution.py
+++ b/solution.py
@@ -289,12 +289,8 @@
     last_sin = turn_sin[:, :, SC]
     nyquist_spec_real = jnp.sum(nyquist_real * last_cos - nyquist_imag * last_sin, axis=1)
     nyquist_spec_imag = jnp.sum(nyquist_real * last_sin + nyquist_imag * last_cos, axis=1)
-    spec_real = jnp.concatenate(
-        [parts[0, 0], nyquist_spec_real[:, None], parts[1, 0, :, :0:-1]], axis=1
-    )
-    spec_imag = jnp.concatenate(
-        [parts[0, 1], nyquist_spec_imag[:, None], parts[1, 1, :, :0:-1]], axis=1
-    )
+    spec_real = jnp.concatenate([parts[0, 0], parts[1, 0], nyquist_spec_real[:, None]], axis=1)
+    spec_imag = jnp.concatenate([parts[0, 1], parts[1, 1], nyquist_spec_imag[:, None]], axis=1)
     row_cos_t = row_cos.T
     row_sin_t = row_sin.T
     rows_real = jnp.dot(row_cos_t, spec_real, precision=EXACT_PRECISION) - jnp.dot(
@@ -303,23 +299,25 @@
     rows_imag = jnp.dot(row_sin_t, spec_real, precision=EXACT_PRECISION) + jnp.dot(
         row_cos_t, spec_imag, precision=EXACT_PRECISION
     )
+    lanes = 2 * (SC + 1)
     packed = jnp.concatenate(
-        [rows_real, rows_imag, jnp.broadcast_to(jnp.sum(weights), (SR, 128))], axis=1
+        [rows_real, rows_imag, jnp.broadcast_to(jnp.sum(weights), (SR, (-lanes) % 128 or 128))],
+        axis=1,
     )
     width = tile + 2 * HALO
     columns = jnp.mod(
         lax.axis_index("scan") * tile - HALO + jnp.arange(width, dtype=jnp.int32), SC
     )
-    col_angles = phase_angles(jnp.arange(SC, dtype=jnp.int32), columns, SC)
+    col_angles = phase_angles(col_index, columns, SC)
     cos_cols, sin_cols = lax.optimization_barrier((jnp.cos(col_angles), jnp.sin(col_angles)))
     gathered = lax.all_to_all(packed, "det", 0, 0, tiled=True)
     own = pairwise_sum([gathered[i] for i in range(det_size)])
     spread = jnp.broadcast_to(own, (scan_size,) + own.shape)
     gathered = lax.all_to_all(spread, "scan", 0, 0, tiled=True)
     total = pairwise_sum([gathered[i] for i in range(scan_size)])
-    line_real = total[:SC]
-    line_imag = total[SC : 2 * SC]
-    bright_sum = total[2 * SC]
+    line_real = total[: SC + 1]
+    line_imag = total[SC + 1 : lanes]
+    bright_sum = total[lanes]
     picture = jnp.dot(line_real, cos_cols, precision=EXACT_PRECISION) - jnp.dot(
         line_imag, sin_cols, precision=EXACT_PRECISION
     )

time: 125 us -> 125 us (level)
  matrix products: 12.7 us -> 10.5 us
  local copies, waits for them, and re-layouts: 18.7 us -> 20.8 us
    unnamed x13, local copies, waits for them, and re-layouts: 11.3 us -> 15.4 us
    dot_general x1, matrix products: 9.7 us -> 7.45 us  [local(): jnp.einsum('abrcp,acq->brpq', images, table.reshape(scan_size, tile, tabl...]
  transfers between devices with their start and end apart: 3 -> 3, of which waited for: 3 -> 3; matrix products, arithmetic and copies ran while one was open for 22% -> 21% of each run, Pallas kernels for 0% -> 0%
where the time goes in v5:
time: 125 us; the launch traced here: 124 us
  waiting for transfers between devices  32.6 us (26%)
  other arithmetic  25.7 us (21%)
  local copies, waits for them, and re-layouts  20.8 us (17%)
  starting transfers between devices  20.4 us (16%)
  Pallas kernels  11.3 us (9%)
  matrix products  10.5 us (8%)
  between operations  2.91 us (2%)
    all_to_all x1, waiting for transfers between devices, local(): lax.all_to_all(blocks, ('scan', 'det'), split_axis=0, concat_axis=0, tile...  22.1 us
    unnamed x13, local copies, waits for them, and re-layouts  15.4 us
    mul x1, other arithmetic, local(): turn_sin * weights[None, :, None] * keep[None, None, :]  14.7 us
    all_to_all x1, starting transfers between devices, local(): lax.all_to_all(blocks, ('scan', 'det'), split_axis=0, concat_axis=0, tile...  11.7 us
    pallas_call x1, Pallas kernels, spectrum(): pl.pallas_call(spectrum_kernel, grid=(steps,), in_specs=[pl.BlockSpec((SR...  11.3 us
    all_to_all x1, waiting for transfers between devices, local(): gathered = lax.all_to_all(packed, 'det', 0, 0, tiled=True)  8.26 us
    dot_general x1, matrix products, local(): jnp.einsum('abrcp,acq->brpq', images, table.reshape(scan_size, tile, tabl...  7.45 us
    another operation x2, other arithmetic  4.76 us
  transfers between devices with their start and end apart: 3, of which 3 were waited for; matrix products, arithmetic and copies ran while one was open for 21% of the time, Pallas kernels for 0%

profile of v5, /device:TPU:0, one launch (start us, length us, event | category | flops | bytes accessed | tf_op | source)
XLA Modules:
  0.0 124.2 jit_solution(13602758302951033174)
XLA Ops:
  0.0 6.4 %copy.22 = bf16[1,128,16384]{1,2,0:T(8,128)(2,1)} copy(bf16[1,128,16384]{2,1,0:T(8,128)(2,1)} %param.4) | data formatting | bytes 8388608 | tf_op args[0]
  6.4 11.7 %all-to-all-start = ((bf16[128,128,128]{1,2,0:T(8,128)(2,1)}), bf16[128,128,128]{1,2,0:T(8,128)(2,1)}, u32[]{:S(2)}, u32[]{:S(2)}) async-start(bf16[128,128,128]{1,2,0:T(8,128)(2,1)} %bitcast.48), calls=%async_computation | async-start | bytes 8388608 | tf_op jit(solution)/shard_map/all_to_all | solution.py:247
  18.3 0.6 fusion.125
  21.4 14.7 %fusion.12 = (f32[16,128,1025]{2,1,0:T(8,128)S(1)}, f32[16,128,1025]{2,1,0:T(8,128)S(1)}) fusion(f32[1025]{0:T(1024)S(1)} %fusion.74, f32[128]{0:T(128)S(1)} %convert_element_type.125, f32[128,1025]{1,0:T(8,128)S(1)} %get-tuple-element.24, f32[16,128]{1,0:T(8,128)S(1)} %get-tuple-element.32, f32[]{:T(128)} %bitcast.8, f32[128,1025]{1,0:T(8,128)S(1)} %get-tuple-element.23, ...), kind=kLoop, calls=%fused_computation.21 | loop fusion | flops 100761600 | bytes 17864200 | tf_op jit(solution)/shard_map/mul | solution.py:281
  36.1 0.7 convert_reduce_fusion
  36.9 2.8 %copy-done = f32[16,128,1025]{2,1,0:T(8,128)} copy-done((f32[16,128,1025]{2,1,0:T(8,128)}, f32[16,128,1025]{2,1,0:T(8,128)S(1)}, u32[]{:S(2)}) %copy-start) | copy-done | bytes 8396824
  40.0 2.5 %copy-done.1 = f32[16,128,1025]{2,1,0:T(8,128)} copy-done((f32[16,128,1025]{2,1,0:T(8,128)}, f32[16,128,1025]{2,1,0:T(8,128)S(1)}, u32[]{:S(2)}) %copy-start.1) | copy-done | bytes 8396824
  43.0 4.6 %fusion.33 = (bf16[8,128,512]{1,2,0:T(8,128)(2,1)S(1)}, bf16[8,128,512]{1,2,0:T(8,128)(2,1)S(1)}) fusion(s32[512]{0:T(512)S(1)} %slice.150, s32[8,128]{1,0:T(8,128)S(1)} %multiply_add_fusion), kind=kLoop, calls=%fused_computation.68 | loop fusion | flops 34078720 | bytes 2103296 | tf_op jit(solution)/shard_map/convert
  47.6 22.1 %all-to-all-done = bf16[128,128,128]{1,2,0:T(8,128)(2,1)} async-done(((bf16[128,128,128]{1,2,0:T(8,128)(2,1)}), bf16[128,128,128]{1,2,0:T(8,128)(2,1)}, u32[]{:S(2)}, u32[]{:S(2)}) %all-to-all-start) | async-done | bytes 4194336 | tf_op jit(solution)/shard_map/all_to_all | solution.py:247
  69.8 7.4 %convolution_bitcast_fusion.re_ref.im_ref = f32[16,128,1152]{2,1,0:T(8,128)S(1)} fusion(bf16[8,16,128,128]{2,3,1,0:T(8,128)(2,1)} %bitcast.3, bf16[8,128,128]{1,2,0:T(8,128)(2,1)S(1)} %select_convert_fusion, bf16[8,128,512]{1,2,0:T(8,128)(2,1)S(1)} %get-tuple-element.26, bf16[8,128,512]{1,2,0:T(8,128)(2,1)S(1)} %get-tuple-element.25), kind=kOutput, calls=%fused_computation.31 | convolution fusion | flops 4838916096 | bytes 15990784 | tf_op jit(solution)/shard_map/abrcp,acq->brpq/dot_general | solution.py:257
  77.2 3.7 %copy-done.2 = f32[16,128,1152]{2,1,0:T(8,128)} copy-done((f32[16,128,1152]{2,1,0:T(8,128)}, f32[16,128,1152]{2,1,0:T(8,128)S(1)}, u32[]{:S(2)}) %copy-start.2) | copy-done | bytes 9437208
  81.3 11.3 %shard_map.46 = f32[2,2,16,512]{3,2,1,0:T(8,128)} custom-call(f32[16,128,1152]{2,1,0:T(8,128)} %copy-done.2, f32[16,128,1152]{2,1,0:T(8,128)} %copy-done.2, f32[16,128,1025]{2,1,0:T(8,128)} %copy-done.1, f32[16,128,1025]{2,1,0:T(8,128)} %copy-done, f32[16,128,1025]{2,1,0:T(8,128)} %copy-done.1, f32[16,128,1025]{2,1,0:T(8,128)} %copy-done), custom_call_target="tpu_custom_call" | custom-call | tf_op jit(solution)/shard_map/pallas_call | solution.py:221
  92.8 0.8 slice_bitcast_fusion.1
  95.5 0.6 broadcast_in_dim.44
  96.2 0.8 copy.28
  97.0 4.3 %all-to-all-start.1 = ((f32[16,1,2176]{2,1,0:T(1,128)}), f32[16,1,2176]{2,1,0:T(1,128)S(1)}, u32[]{:S(2)}, u32[]{:S(2)}) async-start(f32[16,1,2176]{2,1,0:T(1,128)} %copy.28), calls=%async_computation.1 | async-start | bytes 278528 | tf_op jit(solution)/shard_map/all_to_all | solution.py:313
  101.3 8.3 %all-to-all-done.1 = f32[16,1,2176]{2,1,0:T(1,128)S(1)} async-done(((f32[16,1,2176]{2,1,0:T(1,128)}), f32[16,1,2176]{2,1,0:T(1,128)S(1)}, u32[]{:S(2)}, u32[]{:S(2)}) %all-to-all-start.1) | async-done | bytes 139296 | tf_op jit(solution)/shard_map/all_to_all | solution.py:313
  109.7 0.7 broadcast_in_dim.72
  110.3 4.4 %all-to-all-start.2 = ((f32[8,1,2176]{2,1,0:T(1,128)}), f32[8,1,2176]{2,1,0:T(1,128)S(1)}, u32[]{:S(2)}, u32[]{:S(2)}) async-start(f32[8,1,2176]{2,1,0:T(1,128)} %broadcast_in_dim.72), calls=%async_computation.2 | async-start | bytes 139264 | tf_op jit(solution)/shard_map/all_to_all | solution.py:316
  114.7 4.2 %fusion.46 = (f32[1025,160]{1,0:T(8,128)S(1)}, f32[1025,160]{1,0:T(8,128)S(1)}) fusion(s32[160]{0:T(256)S(1)} %and_select_fusion, s32[1025]{0:T(1024)S(1)} %pad_add_fusion), kind=kLoop, calls=%fused_computation.99 | loop fusion | flops 2296000 | bytes 1316740 | tf_op jit(solution)/shard_map/sin | solution.py:312
  118.9 2.2 %all-to-all-done.2 = f32[8,1,2176]{2,1,0:T(1,128)S(1)} async-done(((f32[8,1,2176]{2,1,0:T(1,128)}), f32[8,1,2176]{2,1,0:T(1,128)S(1)}, u32[]{:S(2)}, u32[]{:S(2)}) %all-to-all-start.2) | async-done | bytes 69664 | tf_op jit(solution)/shard_map/all_to_all | solution.py:316
  121.1 0.6 slice.222
  122.4 0.6 fusion.76
  123.5 0.6 divide_multiply_fusion
  (44 shorter events, 4.6 us)
Async XLA Ops:
  6.4 11.8 %copy-start.5 = (s32[128]{0:T(128)S(1)}, s32[128]{0:T(128)}, u32[]{:S(2)}) copy-start(s32[128]{0:T(128)} %param.6) | copy-start | bytes 1540
  6.4 11.8 %copy-start.4 = (s32[128,2]{0,1:T(2,128)S(1)}, s32[128,2]{0,1:T(2,128)}, u32[]{:S(2)}) copy-start(s32[128,2]{0,1:T(2,128)} %param.5) | copy-start | bytes 3076
  6.4 11.9 %copy-start.3 = (f32[2]{0:T(128)S(1)}, f32[2]{0:T(128)}, u32[]{:S(2)}) copy-start(f32[2]{0:T(128)} %param.7) | copy-start | bytes 28
  6.4 63.4 %all-to-all-start = ((bf16[128,128,128]{1,2,0:T(8,128)(2,1)}), bf16[128,128,128]{1,2,0:T(8,128)(2,1)}, u32[]{:S(2)}, u32[]{:S(2)}) async-start(bf16[128,128,128]{1,2,0:T(8,128)(2,1)} %bitcast.48), calls=%async_computation | async-start | bytes 8388608 | tf_op jit(solution)/shard_map/all_to_all | solution.py:247
  36.1 3.6 %copy-start = (f32[16,128,1025]{2,1,0:T(8,128)}, f32[16,128,1025]{2,1,0:T(8,128)S(1)}, u32[]{:S(2)}) copy-start(f32[16,128,1025]{2,1,0:T(8,128)S(1)} %get-tuple-element.10.ls_ref.us_ref) | copy-start | bytes 25190404
  36.1 6.4 %copy-start.1 = (f32[16,128,1025]{2,1,0:T(8,128)}, f32[16,128,1025]{2,1,0:T(8,128)S(1)}, u32[]{:S(2)}) copy-start(f32[16,128,1025]{2,1,0:T(8,128)S(1)} %get-tuple-element.9.lc_ref.uc_ref) | copy-start | bytes 25190404
  77.2 3.7 %copy-start.2 = (f32[16,128,1152]{2,1,0:T(8,128)}, f32[16,128,1152]{2,1,0:T(8,128)S(1)}, u32[]{:S(2)}) copy-start(f32[16,128,1152]{2,1,0:T(8,128)S(1)} %convolution_bitcast_fusion.re_ref.im_ref) | copy-start | bytes 28311556
  97.0 12.6 %all-to-all-start.1 = ((f32[16,1,2176]{2,1,0:T(1,128)}), f32[16,1,2176]{2,1,0:T(1,128)S(1)}, u32[]{:S(2)}, u32[]{:S(2)}) async-start(f32[16,1,2176]{2,1,0:T(1,128)} %copy.28), calls=%async_computation.1 | async-start | bytes 278528 | tf_op jit(solution)/shard_map/all_to_all | solution.py:313
  110.3 10.8 %all-to-all-start.2 = ((f32[8,1,2176]{2,1,0:T(1,128)}), f32[8,1,2176]{2,1,0:T(1,128)S(1)}, u32[]{:S(2)}, u32[]{:S(2)}) async-start(f32[8,1,2176]{2,1,0:T(1,128)} %broadcast_in_dim.72), calls=%async_computation.2 | async-start | bytes 139264 | tf_op jit(solution)/shard_map/all_to_all | solution.py:316

commit v6 on v5

--- a/solution.py
+++ b/solution.py
@@ -186,12 +186,17 @@
     return out
 
 
-def spectrum_kernel(re_ref, im_ref, lc_ref, ls_ref, uc_ref, us_ref, out_ref, acc_ref):
+def spectrum_kernel(y_ref, lc_ref, ls_ref, uc_ref, us_ref, out_ref, acc_ref):
     acc_ref[...] = jnp.zeros(acc_ref.shape, acc_ref.dtype)
+    width = lc_ref.shape[2]
+    low = pl.multiple_of(pl.program_id(0) * width, width)
+    high = pl.multiple_of(pl.program_id(0) * width + SC // 2, width)
 
     def body(i, carry):
         rows = pl.ds(pl.multiple_of(i * 8, 8), 8)
-        full = fft16([(re_ref[r, rows, :], im_ref[r, rows, :]) for r in range(SR)])
+        full = fft16(
+            [(y_ref[r, rows, pl.ds(low, width)], y_ref[r, rows, pl.ds(high, width)]) for r in range(SR)]
+        )
         for s in range(SR):
             fr, fi = full[s]
             tc = lc_ref[s, rows, :]
@@ -205,7 +210,7 @@
             acc_ref[1, 1, s] += gr * ts - gi * tc
         return carry
 
-    lax.fori_loop(0, re_ref.shape[1] // 8, body, 0)
+    lax.fori_loop(0, lc_ref.shape[1] // 8, body, 0)
     for a in range(2):
         for b in range(2):
             out_ref[a, b] = jnp.sum(acc_ref[a, b], axis=1)
@@ -222,8 +227,7 @@
         spectrum_kernel,
         grid=(steps,),
         in_specs=[
-            pl.BlockSpec((SR, pixels, block), lower),
-            pl.BlockSpec((SR, pixels, block), upper),
+            pl.BlockSpec(memory_space=pltpu.VMEM),
             pl.BlockSpec((SR, pixels, block), lower),
             pl.BlockSpec((SR, pixels, block), lower),
             pl.BlockSpec((SR, pixels, block), upper),
@@ -232,7 +236,8 @@
         out_specs=pl.BlockSpec((2, 2, SR, block), lambda j: (0, 0, 0, j)),
         out_shape=jax.ShapeDtypeStruct((2, 2, SR, half), jnp.float32),
         scratch_shapes=[pltpu.VMEM((2, 2, SR, 8, block), jnp.float32)],
-    )(both_col, both_col, turn_cos, turn_sin, turn_cos, turn_sin)
+        compiler_params=pltpu.CompilerParams(vmem_limit_bytes=40 * 1024 * 1024),
+    )(both_col, turn_cos, turn_sin, turn_cos, turn_sin)
     return spec
 
 

time: 125 us -> 118 us (0.944)
  local copies, waits for them, and re-layouts: 20.8 us -> 16.3 us
  Pallas kernels: 11.3 us -> 8.87 us
    unnamed x13 -> x11, local copies, waits for them, and re-layouts: 15.4 us -> 11.7 us
    pallas_call x1, Pallas kernels: 11.3 us -> 8.87 us  [spectrum(): pl.pallas_call(spectrum_kernel, grid=(steps,), in_specs=[pl.BlockSpec(mem...]
  transfers between devices with their start and end apart: 3 -> 3, of which waited for: 3 -> 3; matrix products, arithmetic and copies ran while one was open for 21% -> 22% of each run, Pallas kernels for 0% -> 0%
where the time goes in v6:
time: 118 us; the launch traced here: 117 us
  waiting for transfers between devices  32.6 us (28%)
  other arithmetic  25.7 us (22%)
  starting transfers between devices  20.4 us (17%)
  local copies, waits for them, and re-layouts  16.3 us (14%)
  matrix products  10.5 us (9%)
  Pallas kernels  8.87 us (8%)
  between operations  2.9 us (2%)
    all_to_all x1, waiting for transfers between devices, local(): lax.all_to_all(blocks, ('scan', 'det'), split_axis=0, concat_axis=0, tile...  22.1 us
    mul x1, other arithmetic, local(): turn_sin * weights[None, :, None] * keep[None, None, :]  14.7 us
    all_to_all x1, starting transfers between devices, local(): lax.all_to_all(blocks, ('scan', 'det'), split_axis=0, concat_axis=0, tile...  11.7 us
    unnamed x11, local copies, waits for them, and re-layouts  11.7 us
    pallas_call x1, Pallas kernels, spectrum(): pl.pallas_call(spectrum_kernel, grid=(steps,), in_specs=[pl.BlockSpec(mem...  8.87 us
    all_to_all x1, waiting for transfers between devices, local(): gathered = lax.all_to_all(packed, 'det', 0, 0, tiled=True)  8.26 us
    dot_general x1, matrix products, local(): jnp.einsum('abrcp,acq->brpq', images, table.reshape(scan_size, tile, tabl...  7.45 us
    another operation x2, other arithmetic  4.76 us
  transfers between devices with their start and end apart: 3, of which 3 were waited for; matrix products, arithmetic and copies ran while one was open for 22% of the time, Pallas kernels for 0%

profile of v6, /device:TPU:0, one launch (start us, length us, event | category | flops | bytes accessed | tf_op | source)
XLA Modules:
  0.0 117.2 jit_solution(2517983404500657668)
XLA Ops:
  0.0 6.4 %copy.22 = bf16[1,128,16384]{1,2,0:T(8,128)(2,1)} copy(bf16[1,128,16384]{2,1,0:T(8,128)(2,1)} %param.4) | data formatting | bytes 8388608 | tf_op args[0]
  6.4 11.7 %all-to-all-start = ((bf16[128,128,128]{1,2,0:T(8,128)(2,1)}), bf16[128,128,128]{1,2,0:T(8,128)(2,1)}, u32[]{:S(2)}, u32[]{:S(2)}) async-start(bf16[128,128,128]{1,2,0:T(8,128)(2,1)} %bitcast.48), calls=%async_computation | async-start | bytes 8388608 | tf_op jit(solution)/shard_map/all_to_all | solution.py:252
  18.3 0.6 fusion.125
  20.9 0.5 fusion.44
  21.4 14.7 %fusion.12 = (f32[16,128,1025]{2,1,0:T(8,128)S(1)}, f32[16,128,1025]{2,1,0:T(8,128)S(1)}) fusion(f32[1025]{0:T(1024)S(1)} %fusion.74, f32[128]{0:T(128)S(1)} %convert_element_type.125, f32[128,1025]{1,0:T(8,128)S(1)} %get-tuple-element.24, f32[16,128]{1,0:T(8,128)S(1)} %get-tuple-element.32, f32[]{:T(128)} %bitcast.8, f32[128,1025]{1,0:T(8,128)S(1)} %get-tuple-element.23, ...), kind=kLoop, calls=%fused_computation.21 | loop fusion | flops 100761600 | bytes 17864200 | tf_op jit(solution)/shard_map/mul | solution.py:286
  36.1 0.7 convert_reduce_fusion
  36.9 2.8 %copy-done = f32[16,128,1025]{2,1,0:T(8,128)} copy-done((f32[16,128,1025]{2,1,0:T(8,128)}, f32[16,128,1025]{2,1,0:T(8,128)S(1)}, u32[]{:S(2)}) %copy-start) | copy-done | bytes 8396824
  40.0 2.5 %copy-done.1 = f32[16,128,1025]{2,1,0:T(8,128)} copy-done((f32[16,128,1025]{2,1,0:T(8,128)}, f32[16,128,1025]{2,1,0:T(8,128)S(1)}, u32[]{:S(2)}) %copy-start.1) | copy-done | bytes 8396824
  43.0 4.6 %fusion.33 = (bf16[8,128,512]{1,2,0:T(8,128)(2,1)S(1)}, bf16[8,128,512]{1,2,0:T(8,128)(2,1)S(1)}) fusion(s32[512]{0:T(512)S(1)} %slice.150, s32[8,128]{1,0:T(8,128)S(1)} %multiply_add_fusion), kind=kLoop, calls=%fused_computation.68 | loop fusion | flops 34078720 | bytes 2103296 | tf_op jit(solution)/shard_map/convert
  47.6 22.1 %all-to-all-done = bf16[128,128,128]{1,2,0:T(8,128)(2,1)} async-done(((bf16[128,128,128]{1,2,0:T(8,128)(2,1)}), bf16[128,128,128]{1,2,0:T(8,128)(2,1)}, u32[]{:S(2)}, u32[]{:S(2)}) %all-to-all-start) | async-done | bytes 4194336 | tf_op jit(solution)/shard_map/all_to_all | solution.py:252
  69.7 7.4 %convolution_bitcast_fusion.y_ref = f32[16,128,1152]{2,1,0:T(8,128)S(1)} fusion(bf16[8,16,128,128]{2,3,1,0:T(8,128)(2,1)} %bitcast.3, bf16[8,128,128]{1,2,0:T(8,128)(2,1)S(1)} %select_convert_fusion, bf16[8,128,512]{1,2,0:T(8,128)(2,1)S(1)} %get-tuple-element.26, bf16[8,128,512]{1,2,0:T(8,128)(2,1)S(1)} %get-tuple-element.25), kind=kOutput, calls=%fused_computation.31 | convolution fusion | flops 4838916096 | bytes 15990784 | tf_op jit(solution)/shard_map/abrcp,acq->brpq/dot_general | solution.py:262
  77.5 8.9 %shard_map.46 = f32[2,2,16,512]{3,2,1,0:T(8,128)S(1)} custom-call(f32[16,128,1152]{2,1,0:T(8,128)S(1)} %convolution_bitcast_fusion.y_ref, f32[16,128,1025]{2,1,0:T(8,128)} %copy-done.1, f32[16,128,1025]{2,1,0:T(8,128)} %copy-done, f32[16,128,1025]{2,1,0:T(8,128)} %copy-done.1, f32[16,128,1025]{2,1,0:T(8,128)} %copy-done), custom_call_target="tpu_custom_call" | custom-call | tf_op jit(solution)/shard_map/pallas_call | solution.py:226
  88.5 0.6 broadcast_in_dim.44
  89.3 0.8 copy.28
  90.1 4.3 %all-to-all-start.1 = ((f32[16,1,2176]{2,1,0:T(1,128)}), f32[16,1,2176]{2,1,0:T(1,128)S(1)}, u32[]{:S(2)}, u32[]{:S(2)}) async-start(f32[16,1,2176]{2,1,0:T(1,128)} %copy.28), calls=%async_computation.1 | async-start | bytes 278528 | tf_op jit(solution)/shard_map/all_to_all | solution.py:318
  94.4 8.3 %all-to-all-done.1 = f32[16,1,2176]{2,1,0:T(1,128)S(1)} async-done(((f32[16,1,2176]{2,1,0:T(1,128)}), f32[16,1,2176]{2,1,0:T(1,128)S(1)}, u32[]{:S(2)}, u32[]{:S(2)}) %all-to-all-start.1) | async-done | bytes 139296 | tf_op jit(solution)/shard_map/all_to_all | solution.py:318
  102.7 0.7 broadcast_in_dim.72
  103.4 4.4 %all-to-all-start.2 = ((f32[8,1,2176]{2,1,0:T(1,128)}), f32[8,1,2176]{2,1,0:T(1,128)S(1)}, u32[]{:S(2)}, u32[]{:S(2)}) async-start(f32[8,1,2176]{2,1,0:T(1,128)} %broadcast_in_dim.72), calls=%async_computation.2 | async-start | bytes 139264 | tf_op jit(solution)/shard_map/all_to_all | solution.py:321
  107.8 4.2 %fusion.46 = (f32[1025,160]{1,0:T(8,128)S(1)}, f32[1025,160]{1,0:T(8,128)S(1)}) fusion(s32[160]{0:T(256)S(1)} %and_select_fusion, s32[1025]{0:T(1024)S(1)} %pad_add_fusion), kind=kLoop, calls=%fused_computation.99 | loop fusion | flops 2296000 | bytes 1316740 | tf_op jit(solution)/shard_map/sin | solution.py:317
  112.0 2.2 %all-to-all-done.2 = f32[8,1,2176]{2,1,0:T(1,128)S(1)} async-done(((f32[8,1,2176]{2,1,0:T(1,128)}), f32[8,1,2176]{2,1,0:T(1,128)S(1)}, u32[]{:S(2)}, u32[]{:S(2)}) %all-to-all-start.2) | async-done | bytes 69664 | tf_op jit(solution)/shard_map/all_to_all | solution.py:321
  114.2 0.6 slice.222
  115.5 0.6 fusion.76
  116.0 0.5 fusion.77
  116.6 0.6 divide_multiply_fusion
  (42 shorter events, 3.6 us)
Async XLA Ops:
  6.4 11.8 %copy-start.4 = (s32[128]{0:T(128)S(1)}, s32[128]{0:T(128)}, u32[]{:S(2)}) copy-start(s32[128]{0:T(128)} %param.6) | copy-start | bytes 1540
  6.4 11.8 %copy-start.3 = (s32[128,2]{0,1:T(2,128)S(1)}, s32[128,2]{0,1:T(2,128)}, u32[]{:S(2)}) copy-start(s32[128,2]{0,1:T(2,128)} %param.5) | copy-start | bytes 3076
  6.4 11.9 %copy-start.2 = (f32[2]{0:T(128)S(1)}, f32[2]{0:T(128)}, u32[]{:S(2)}) copy-start(f32[2]{0:T(128)} %param.7) | copy-start | bytes 28
  6.4 63.4 %all-to-all-start = ((bf16[128,128,128]{1,2,0:T(8,128)(2,1)}), bf16[128,128,128]{1,2,0:T(8,128)(2,1)}, u32[]{:S(2)}, u32[]{:S(2)}) async-start(bf16[128,128,128]{1,2,0:T(8,128)(2,1)} %bitcast.48), calls=%async_computation | async-start | bytes 8388608 | tf_op jit(solution)/shard_map/all_to_all | solution.py:252
  36.1 3.6 %copy-start = (f32[16,128,1025]{2,1,0:T(8,128)}, f32[16,128,1025]{2,1,0:T(8,128)S(1)}, u32[]{:S(2)}) copy-start(f32[16,128,1025]{2,1,0:T(8,128)S(1)} %get-tuple-element.10.ls_ref.us_ref) | copy-start | bytes 25190404
  36.1 6.4 %copy-start.1 = (f32[16,128,1025]{2,1,0:T(8,128)}, f32[16,128,1025]{2,1,0:T(8,128)S(1)}, u32[]{:S(2)}) copy-start(f32[16,128,1025]{2,1,0:T(8,128)S(1)} %get-tuple-element.9.lc_ref.uc_ref) | copy-start | bytes 25190404
  90.1 12.6 %all-to-all-start.1 = ((f32[16,1,2176]{2,1,0:T(1,128)}), f32[16,1,2176]{2,1,0:T(1,128)S(1)}, u32[]{:S(2)}, u32[]{:S(2)}) async-start(f32[16,1,2176]{2,1,0:T(1,128)} %copy.28), calls=%async_computation.1 | async-start | bytes 278528 | tf_op jit(solution)/shard_map/all_to_all | solution.py:318
  103.4 10.7 %all-to-all-start.2 = ((f32[8,1,2176]{2,1,0:T(1,128)}), f32[8,1,2176]{2,1,0:T(1,128)S(1)}, u32[]{:S(2)}, u32[]{:S(2)}) async-start(f32[8,1,2176]{2,1,0:T(1,128)} %broadcast_in_dim.72), calls=%async_computation.2 | async-start | bytes 139264 | tf_op jit(solution)/shard_map/all_to_all | solution.py:321

commit v7 on v6

--- a/solution.py
+++ b/solution.py
@@ -294,16 +294,21 @@
     last_sin = turn_sin[:, :, SC]
     nyquist_spec_real = jnp.sum(nyquist_real * last_cos - nyquist_imag * last_sin, axis=1)
     nyquist_spec_imag = jnp.sum(nyquist_real * last_sin + nyquist_imag * last_cos, axis=1)
-    spec_real = jnp.concatenate([parts[0, 0], parts[1, 0], nyquist_spec_real[:, None]], axis=1)
-    spec_imag = jnp.concatenate([parts[0, 1], parts[1, 1], nyquist_spec_imag[:, None]], axis=1)
-    row_cos_t = row_cos.T
-    row_sin_t = row_sin.T
-    rows_real = jnp.dot(row_cos_t, spec_real, precision=EXACT_PRECISION) - jnp.dot(
-        row_sin_t, spec_imag, precision=EXACT_PRECISION
-    )
-    rows_imag = jnp.dot(row_sin_t, spec_real, precision=EXACT_PRECISION) + jnp.dot(
-        row_cos_t, spec_imag, precision=EXACT_PRECISION
-    )
+    spectra = jnp.stack(
+        [
+            jnp.concatenate([parts[0, 0], parts[1, 0], nyquist_spec_real[:, None]], axis=1),
+            jnp.concatenate([parts[0, 1], parts[1, 1], nyquist_spec_imag[:, None]], axis=1),
+        ]
+    )
+    inverse_rows = jnp.stack(
+        [
+            jnp.stack([row_cos.T, -row_sin.T], axis=1),
+            jnp.stack([row_sin.T, row_cos.T], axis=1),
+        ]
+    )
+    rows_both = jnp.einsum("jrks,ksq->jrq", inverse_rows, spectra, precision=EXACT_PRECISION)
+    rows_real = rows_both[0]
+    rows_imag = rows_both[1]
     lanes = 2 * (SC + 1)
     packed = jnp.concatenate(
         [rows_real, rows_imag, jnp.broadcast_to(jnp.sum(weights), (SR, (-lanes) % 128 or 128))],
@@ -314,18 +319,16 @@
         lax.axis_index("scan") * tile - HALO + jnp.arange(width, dtype=jnp.int32), SC
     )
     col_angles = phase_angles(col_index, columns, SC)
-    cos_cols, sin_cols = lax.optimization_barrier((jnp.cos(col_angles), jnp.sin(col_angles)))
+    final_table = lax.optimization_barrier(
+        jnp.concatenate([jnp.cos(col_angles), -jnp.sin(col_angles)], axis=0)
+    )
     gathered = lax.all_to_all(packed, "det", 0, 0, tiled=True)
     own = pairwise_sum([gathered[i] for i in range(det_size)])
     spread = jnp.broadcast_to(own, (scan_size,) + own.shape)
     gathered = lax.all_to_all(spread, "scan", 0, 0, tiled=True)
     total = pairwise_sum([gathered[i] for i in range(scan_size)])
-    line_real = total[: SC + 1]
-    line_imag = total[SC + 1 : lanes]
     bright_sum = total[lanes]
-    picture = jnp.dot(line_real, cos_cols, precision=EXACT_PRECISION) - jnp.dot(
-        line_imag, sin_cols, precision=EXACT_PRECISION
-    )
+    picture = jnp.dot(total[:lanes], final_table, precision=EXACT_PRECISION)
     return (
         (picture * (1.0 / (SR * SC)) / jnp.sqrt(bright_sum) * window_weights(width))
         .reshape(rows_dev, 1, width)

time: 118 us -> 117 us (level)
  other arithmetic: 25.7 us -> 30 us
  local copies, waits for them, and re-layouts: 16.3 us -> 13.5 us
  waiting for transfers between devices: 32.6 us -> 31.2 us
    unnamed x11 -> x7, local copies, waits for them, and re-layouts: 11.7 us -> 6.41 us
    cos x0 -> x1, other arithmetic: none -> 5.25 us  [local(): jnp.cos(col_angles)]
    all_to_all x1, waiting for transfers between devices: 8.26 us -> 3.04 us  [local(): gathered = lax.all_to_all(packed, 'det', 0, 0, tiled=True)]
    sin x1, other arithmetic: 4.18 us -> 0.06 us  [local(): row_sin = jnp.sin(angles_by_row)]
    all_to_all x1, waiting for transfers between devices: 2.17 us -> 4.97 us  [local(): gathered = lax.all_to_all(spread, 'scan', 0, 0, tiled=True)]
    mul x1, other arithmetic: 14.7 us -> 16.5 us  [local(): turn_sin * weights[None, :, None] * keep[None, None, :]]
    concatenate x0 -> x1, other arithmetic: none -> 1.38 us  [local(): jnp.concatenate([jnp.cos(col_angles), -jnp.sin(col_angles)], axis=0)]
    slice x1, local copies, waits for them, and re-layouts: 0.34 us -> 1.57 us  [local(): last_cos = turn_cos[:, :, SC]]
  transfers between devices with their start and end apart: 3 -> 3, of which waited for: 3 -> 3; matrix products, arithmetic and copies ran while one was open for 22% -> 28% of each run, Pallas kernels for 0% -> 0%
where the time goes in v7:
time: 117 us; the launch traced here: 116 us
  waiting for transfers between devices  31.2 us (27%)
  other arithmetic  30 us (26%)
  starting transfers between devices  20.2 us (17%)
  local copies, waits for them, and re-layouts  13.5 us (12%)
  matrix products  9.32 us (8%)
  Pallas kernels  8.87 us (8%)
  between operations  2.88 us (2%)
    all_to_all x1, waiting for transfers between devices, local(): lax.all_to_all(blocks, ('scan', 'det'), split_axis=0, concat_axis=0, tile...  23.2 us
    mul x1, other arithmetic, local(): turn_sin * weights[None, :, None] * keep[None, None, :]  16.5 us
    all_to_all x1, starting transfers between devices, local(): lax.all_to_all(blocks, ('scan', 'det'), split_axis=0, concat_axis=0, tile...  11.7 us
    pallas_call x1, Pallas kernels, spectrum(): pl.pallas_call(spectrum_kernel, grid=(steps,), in_specs=[pl.BlockSpec(mem...  8.87 us
    dot_general x1, matrix products, local(): jnp.einsum('abrcp,acq->brpq', images, table.reshape(scan_size, tile, tabl...  7.44 us
    unnamed x7, local copies, waits for them, and re-layouts  6.41 us
    cos x1, other arithmetic, local(): jnp.cos(col_angles)  5.25 us
    all_to_all x1, waiting for transfers between devices, local(): gathered = lax.all_to_all(spread, 'scan', 0, 0, tiled=True)  4.97 us
  transfers between devices with their start and end apart: 3, of which 3 were waited for; matrix products, arithmetic and copies ran while one was open for 28% of the time, Pallas kernels for 0%

profile of v7, /device:TPU:0, one launch (start us, length us, event | category | flops | bytes accessed | tf_op | source)
XLA Modules:
  0.0 116.0 jit_solution(17867944770218853445)
XLA Ops:
  0.0 6.4 %copy.22 = bf16[1,128,16384]{1,2,0:T(8,128)(2,1)} copy(bf16[1,128,16384]{2,1,0:T(8,128)(2,1)} %param.4) | data formatting | bytes 8388608 | tf_op args[0]
  6.4 11.7 %all-to-all-start = ((bf16[128,128,128]{1,2,0:T(8,128)(2,1)}), bf16[128,128,128]{1,2,0:T(8,128)(2,1)}, u32[]{:S(2)}, u32[]{:S(2)}) async-start(bf16[128,128,128]{1,2,0:T(8,128)(2,1)} %bitcast.61), calls=%async_computation | async-start | bytes 8388608 | tf_op jit(solution)/shard_map/all_to_all | solution.py:252
  18.3 0.6 fusion.112
  20.9 0.5 fusion.44
  21.4 16.5 %fusion.12 = (f32[16,128,1025]{2,1,0:T(8,128)}, f32[16,128,1025]{2,1,0:T(8,128)}) fusion(f32[1025]{0:T(1024)S(1)} %fusion.86, f32[128]{0:T(128)S(1)} %convert_element_type.142, f32[128,1025]{1,0:T(8,128)S(1)} %get-tuple-element.24, f32[16,128]{1,0:T(8,128)S(1)} %get-tuple-element.32, f32[]{:T(128)} %bitcast.10, f32[128,1025]{1,0:T(8,128)S(1)} %get-tuple-element.23, ...), kind=kLoop, calls=%fused_computation.21 | loop fusion | flops 100761600 | bytes 17864200 | tf_op jit(solution)/shard_map/mul | solution.py:286
  37.9 0.6 convert_reduce_fusion
  38.7 1.6 %slice_reduce_fusion.1 = f32[16,128]{1,0:T(8,128)S(1)} fusion(f32[16,128,1025]{2,1,0:T(8,128)} %get-tuple-element.8.ls_ref.us_ref), kind=kLoop, calls=%fused_computation.90 | loop fusion | bytes 16384 | tf_op jit(solution)/shard_map/slice | solution.py:294
  40.2 1.6 %slice_reduce_fusion.2 = f32[16,128]{1,0:T(8,128)S(1)} fusion(f32[16,128,1025]{2,1,0:T(8,128)} %get-tuple-element.7.lc_ref.uc_ref), kind=kLoop, calls=%fused_computation.91 | loop fusion | bytes 16384 | tf_op jit(solution)/shard_map/slice | solution.py:293
  41.9 4.6 %fusion.33 = (bf16[8,128,512]{1,2,0:T(8,128)(2,1)S(1)}, bf16[8,128,512]{1,2,0:T(8,128)(2,1)S(1)}) fusion(s32[512]{0:T(512)S(1)} %slice.150, s32[8,128]{1,0:T(8,128)S(1)} %multiply_add_fusion), kind=kLoop, calls=%fused_computation.68 | loop fusion | flops 34078720 | bytes 2103296 | tf_op jit(solution)/shard_map/convert
  46.6 23.2 %all-to-all-done = bf16[128,128,128]{1,2,0:T(8,128)(2,1)} async-done(((bf16[128,128,128]{1,2,0:T(8,128)(2,1)}), bf16[128,128,128]{1,2,0:T(8,128)(2,1)}, u32[]{:S(2)}, u32[]{:S(2)}) %all-to-all-start) | async-done | bytes 4194336 | tf_op jit(solution)/shard_map/all_to_all | solution.py:252
  69.8 7.4 %convolution_bitcast_fusion.y_ref = f32[16,128,1152]{2,1,0:T(8,128)S(1)} fusion(bf16[8,16,128,128]{2,3,1,0:T(8,128)(2,1)} %bitcast.5, bf16[8,128,128]{1,2,0:T(8,128)(2,1)S(1)} %select_convert_fusion, bf16[8,128,512]{1,2,0:T(8,128)(2,1)S(1)} %get-tuple-element.26, bf16[8,128,512]{1,2,0:T(8,128)(2,1)S(1)} %get-tuple-element.25), kind=kOutput, calls=%fused_computation.31 | convolution fusion | flops 4838916096 | bytes 15990784 | tf_op jit(solution)/shard_map/abrcp,acq->brpq/dot_general | solution.py:262
  77.5 8.9 %shard_map.46 = f32[2,2,16,512]{3,2,1,0:T(8,128)S(1)} custom-call(f32[16,128,1152]{2,1,0:T(8,128)S(1)} %convolution_bitcast_fusion.y_ref, f32[16,128,1025]{2,1,0:T(8,128)} %get-tuple-element.7.lc_ref.uc_ref, f32[16,128,1025]{2,1,0:T(8,128)} %get-tuple-element.8.ls_ref.us_ref, f32[16,128,1025]{2,1,0:T(8,128)} %get-tuple-element.7.lc_ref.uc_ref, ...), custom_call_target="tpu_custom_call" | custom-call | tf_op jit(solution)/shard_map/pallas_call | solution.py:226
  87.6 0.6 broadcast_in_dim.44
  88.4 0.8 copy.28
  89.2 4.1 %all-to-all-start.1 = ((f32[16,1,2176]{2,1,0:T(1,128)}), f32[16,1,2176]{2,1,0:T(1,128)S(1)}, u32[]{:S(2)}, u32[]{:S(2)}) async-start(f32[16,1,2176]{2,1,0:T(1,128)} %copy.28), calls=%async_computation.1 | async-start | bytes 278528 | tf_op jit(solution)/shard_map/all_to_all | solution.py:325
  93.3 5.2 %fusion.46 = (f32[1025,160]{1,0:T(8,128)S(1)}, f32[1025,160]{1,0:T(8,128)}) fusion(s32[160]{0:T(256)S(1)} %and_select_fusion, s32[1025]{0:T(1024)S(1)} %pad_add_fusion), kind=kLoop, calls=%fused_computation.100 | loop fusion | flops 2460000 | bytes 1316740 | tf_op jit(solution)/shard_map/cos | solution.py:323
  98.6 3.0 %all-to-all-done.1 = f32[16,1,2176]{2,1,0:T(1,128)S(1)} async-done(((f32[16,1,2176]{2,1,0:T(1,128)}), f32[16,1,2176]{2,1,0:T(1,128)S(1)}, u32[]{:S(2)}, u32[]{:S(2)}) %all-to-all-start.1) | async-done | bytes 139296 | tf_op jit(solution)/shard_map/all_to_all | solution.py:325
  101.7 0.7 broadcast_in_dim.72
  102.3 4.4 %all-to-all-start.2 = ((f32[8,1,2176]{2,1,0:T(1,128)}), f32[8,1,2176]{2,1,0:T(1,128)S(1)}, u32[]{:S(2)}, u32[]{:S(2)}) async-start(f32[8,1,2176]{2,1,0:T(1,128)} %broadcast_in_dim.72), calls=%async_computation.2 | async-start | bytes 139264 | tf_op jit(solution)/shard_map/all_to_all | solution.py:328
  106.7 1.4 %pad_maximum_fusion = f32[2050,160]{1,0:T(8,128)S(1)} fusion(f32[1025,160]{1,0:T(8,128)} %get-tuple-element.20, f32[1025,160]{1,0:T(8,128)S(1)} %get-tuple-element.19), kind=kLoop, calls=%fused_computation.57 | loop fusion | flops 328000 | bytes 2624000 | tf_op jit(solution)/shard_map/concatenate | solution.py:323
  108.1 5.0 %all-to-all-done.2 = f32[8,1,2176]{2,1,0:T(1,128)S(1)} async-done(((f32[8,1,2176]{2,1,0:T(1,128)}), f32[8,1,2176]{2,1,0:T(1,128)S(1)}, u32[]{:S(2)}, u32[]{:S(2)}) %all-to-all-start.2) | async-done | bytes 69664 | tf_op jit(solution)/shard_map/all_to_all | solution.py:328
  113.1 0.6 slice.223
  114.4 0.9 fusion.52
  115.3 0.6 divide_multiply_fusion
  (41 shorter events, 2.2 us)
Async XLA Ops:
  6.4 11.8 %copy-start.2 = (s32[128]{0:T(128)S(1)}, s32[128]{0:T(128)}, u32[]{:S(2)}) copy-start(s32[128]{0:T(128)} %param.6) | copy-start | bytes 1540
  6.4 11.8 %copy-start.1 = (s32[128,2]{0,1:T(2,128)S(1)}, s32[128,2]{0,1:T(2,128)}, u32[]{:S(2)}) copy-start(s32[128,2]{0,1:T(2,128)} %param.5) | copy-start | bytes 3076
  6.4 11.9 %copy-start = (f32[2]{0:T(128)S(1)}, f32[2]{0:T(128)}, u32[]{:S(2)}) copy-start(f32[2]{0:T(128)} %param.7) | copy-start | bytes 28
  6.4 63.4 %all-to-all-start = ((bf16[128,128,128]{1,2,0:T(8,128)(2,1)}), bf16[128,128,128]{1,2,0:T(8,128)(2,1)}, u32[]{:S(2)}, u32[]{:S(2)}) async-start(bf16[128,128,128]{1,2,0:T(8,128)(2,1)} %bitcast.61), calls=%async_computation | async-start | bytes 8388608 | tf_op jit(solution)/shard_map/all_to_all | solution.py:252
  89.2 12.4 %all-to-all-start.1 = ((f32[16,1,2176]{2,1,0:T(1,128)}), f32[16,1,2176]{2,1,0:T(1,128)S(1)}, u32[]{:S(2)}, u32[]{:S(2)}) async-start(f32[16,1,2176]{2,1,0:T(1,128)} %copy.28), calls=%async_computation.1 | async-start | bytes 278528 | tf_op jit(solution)/shard_map/all_to_all | solution.py:325
  102.3 10.7 %all-to-all-start.2 = ((f32[8,1,2176]{2,1,0:T(1,128)}), f32[8,1,2176]{2,1,0:T(1,128)S(1)}, u32[]{:S(2)}, u32[]{:S(2)}) async-start(f32[8,1,2176]{2,1,0:T(1,128)} %broadcast_in_dim.72), calls=%async_computation.2 | async-start | bytes 139264 | tf_op jit(solution)/shard_map/all_to_all | solution.py:328

commit v8 on v7

--- a/solution.py
+++ b/solution.py
@@ -187,15 +187,22 @@
 
 
 def spectrum_kernel(y_ref, lc_ref, ls_ref, uc_ref, us_ref, out_ref, acc_ref):
-    acc_ref[...] = jnp.zeros(acc_ref.shape, acc_ref.dtype)
+    part = pl.program_id(1)
+
+    @pl.when(part == 0)
+    def _():
+        acc_ref[...] = jnp.zeros(acc_ref.shape, acc_ref.dtype)
+
     width = lc_ref.shape[2]
+    span = lc_ref.shape[1]
     low = pl.multiple_of(pl.program_id(0) * width, width)
     high = pl.multiple_of(pl.program_id(0) * width + SC // 2, width)
 
     def body(i, carry):
         rows = pl.ds(pl.multiple_of(i * 8, 8), 8)
+        lines = pl.ds(pl.multiple_of(part * span + i * 8, 8), 8)
         full = fft16(
-            [(y_ref[r, rows, pl.ds(low, width)], y_ref[r, rows, pl.ds(high, width)]) for r in range(SR)]
+            [(y_ref[r, lines, pl.ds(low, width)], y_ref[r, lines, pl.ds(high, width)]) for r in range(SR)]
         )
         for s in range(SR):
             fr, fi = full[s]
@@ -210,10 +217,13 @@
             acc_ref[1, 1, s] += gr * ts - gi * tc
         return carry
 
-    lax.fori_loop(0, lc_ref.shape[1] // 8, body, 0)
-    for a in range(2):
-        for b in range(2):
-            out_ref[a, b] = jnp.sum(acc_ref[a, b], axis=1)
+    lax.fori_loop(0, span // 8, body, 0)
+
+    @pl.when(part == pl.num_programs(1) - 1)
+    def _():
+        for a in range(2):
+            for b in range(2):
+                out_ref[a, b] = jnp.sum(acc_ref[a, b], axis=1)
 
 
 def spectrum(both_col, turn_cos, turn_sin):
@@ -221,19 +231,20 @@
     half = SC // 2
     block = 128
     steps = half // block
-    lower = lambda j: (0, 0, j)
-    upper = lambda j: (0, 0, j + steps)
+    splits = 2
+    lower = lambda j, k: (0, k, j)
+    upper = lambda j, k: (0, k, j + steps)
     spec = pl.pallas_call(
         spectrum_kernel,
-        grid=(steps,),
+        grid=(steps, splits),
         in_specs=[
             pl.BlockSpec(memory_space=pltpu.VMEM),
-            pl.BlockSpec((SR, pixels, block), lower),
-            pl.BlockSpec((SR, pixels, block), lower),
-            pl.BlockSpec((SR, pixels, block), upper),
-            pl.BlockSpec((SR, pixels, block), upper),
+            pl.BlockSpec((SR, pixels // splits, block), lower),
+            pl.BlockSpec((SR, pixels // splits, block), lower),
+            pl.BlockSpec((SR, pixels // splits, block), upper),
+            pl.BlockSpec((SR, pixels // splits, block), upper),
         ],
-        out_specs=pl.BlockSpec((2, 2, SR, block), lambda j: (0, 0, 0, j)),
+        out_specs=pl.BlockSpec((2, 2, SR, block), lambda j, k: (0, 0, 0, j)),
         out_shape=jax.ShapeDtypeStruct((2, 2, SR, half), jnp.float32),
         scratch_shapes=[pltpu.VMEM((2, 2, SR, 8, block), jnp.float32)],
         compiler_params=pltpu.CompilerParams(vmem_limit_bytes=40 * 1024 * 1024),

time: 117 us -> 118 us (level)
  Pallas kernels: 8.87 us -> 10.5 us
    pallas_call x1, Pallas kernels: 8.87 us -> 10.5 us  [spectrum(): pl.pallas_call(spectrum_kernel, grid=(steps, splits), in_specs=[pl.BlockS...]
where the time goes in v8:
time: 118 us
  waiting for transfers between devices  31.2 us (26%)
  other arithmetic  30 us (25%)
  starting transfers between devices  20.2 us (17%)
  local copies, waits for them, and re-layouts  13.5 us (11%)
  Pallas kernels  10.5 us (9%)
  matrix products  9.32 us (8%)
  between operations  2.88 us (2%)
    all_to_all x1, waiting for transfers between devices, local(): lax.all_to_all(blocks, ('scan', 'det'), split_axis=0, concat_axis=0, tile...  23.2 us
    mul x1, other arithmetic, local(): turn_sin * weights[None, :, None] * keep[None, None, :]  16.5 us
    all_to_all x1, starting transfers between devices, local(): lax.all_to_all(blocks, ('scan', 'det'), split_axis=0, concat_axis=0, tile...  11.7 us
    pallas_call x1, Pallas kernels, spectrum(): pl.pallas_call(spectrum_kernel, grid=(steps, splits), in_specs=[pl.BlockS...  10.5 us
    dot_general x1, matrix products, local(): jnp.einsum('abrcp,acq->brpq', images, table.reshape(scan_size, tile, tabl...  7.44 us
    unnamed x7, local copies, waits for them, and re-layouts  6.41 us
    cos x1, other arithmetic, local(): jnp.cos(col_angles)  5.25 us
    all_to_all x1, waiting for transfers between devices, local(): gathered = lax.all_to_all(spread, 'scan', 0, 0, tiled=True)  4.97 us
  transfers between devices with their start and end apart: 3, of which 3 were waited for; matrix products, arithmetic and copies ran while one was open for 28% of the time, Pallas kernels for 0%

profile of v8, /device:TPU:0, one launch (start us, length us, event | category | flops | bytes accessed | tf_op | source)
XLA Modules:
  0.0 117.5 jit_solution(3226956828749328229)
XLA Ops:
  0.0 6.4 %copy.22 = bf16[1,128,16384]{1,2,0:T(8,128)(2,1)} copy(bf16[1,128,16384]{2,1,0:T(8,128)(2,1)} %param.4) | data formatting | bytes 8388608 | tf_op args[0]
  6.4 11.7 %all-to-all-start = ((bf16[128,128,128]{1,2,0:T(8,128)(2,1)}), bf16[128,128,128]{1,2,0:T(8,128)(2,1)}, u32[]{:S(2)}, u32[]{:S(2)}) async-start(bf16[128,128,128]{1,2,0:T(8,128)(2,1)} %bitcast.61), calls=%async_computation | async-start | bytes 8388608 | tf_op jit(solution)/shard_map/all_to_all | solution.py:263
  18.3 0.6 fusion.112
  20.9 0.5 fusion.44
  21.4 16.5 %fusion.12 = (f32[16,128,1025]{2,1,0:T(8,128)}, f32[16,128,1025]{2,1,0:T(8,128)}) fusion(f32[1025]{0:T(1024)S(1)} %fusion.86, f32[128]{0:T(128)S(1)} %convert_element_type.142, f32[128,1025]{1,0:T(8,128)S(1)} %get-tuple-element.24, f32[16,128]{1,0:T(8,128)S(1)} %get-tuple-element.32, f32[]{:T(128)} %bitcast.10, f32[128,1025]{1,0:T(8,128)S(1)} %get-tuple-element.23, ...), kind=kLoop, calls=%fused_computation.21 | loop fusion | flops 100761600 | bytes 17864200 | tf_op jit(solution)/shard_map/mul | solution.py:297
  37.9 0.6 convert_reduce_fusion
  38.7 1.6 %slice_reduce_fusion.1 = f32[16,128]{1,0:T(8,128)S(1)} fusion(f32[16,128,1025]{2,1,0:T(8,128)} %get-tuple-element.8.ls_ref.us_ref), kind=kLoop, calls=%fused_computation.90 | loop fusion | bytes 16384 | tf_op jit(solution)/shard_map/slice | solution.py:305
  40.2 1.6 %slice_reduce_fusion.2 = f32[16,128]{1,0:T(8,128)S(1)} fusion(f32[16,128,1025]{2,1,0:T(8,128)} %get-tuple-element.7.lc_ref.uc_ref), kind=kLoop, calls=%fused_computation.91 | loop fusion | bytes 16384 | tf_op jit(solution)/shard_map/slice | solution.py:304
  41.9 4.6 %fusion.33 = (bf16[8,128,512]{1,2,0:T(8,128)(2,1)S(1)}, bf16[8,128,512]{1,2,0:T(8,128)(2,1)S(1)}) fusion(s32[512]{0:T(512)S(1)} %slice.150, s32[8,128]{1,0:T(8,128)S(1)} %multiply_add_fusion), kind=kLoop, calls=%fused_computation.68 | loop fusion | flops 34078720 | bytes 2103296 | tf_op jit(solution)/shard_map/convert
  46.6 23.2 %all-to-all-done = bf16[128,128,128]{1,2,0:T(8,128)(2,1)} async-done(((bf16[128,128,128]{1,2,0:T(8,128)(2,1)}), bf16[128,128,128]{1,2,0:T(8,128)(2,1)}, u32[]{:S(2)}, u32[]{:S(2)}) %all-to-all-start) | async-done | bytes 4194336 | tf_op jit(solution)/shard_map/all_to_all | solution.py:263
  69.8 7.4 %convolution_bitcast_fusion.y_ref = f32[16,128,1152]{2,1,0:T(8,128)S(1)} fusion(bf16[8,16,128,128]{2,3,1,0:T(8,128)(2,1)} %bitcast.5, bf16[8,128,128]{1,2,0:T(8,128)(2,1)S(1)} %select_convert_fusion, bf16[8,128,512]{1,2,0:T(8,128)(2,1)S(1)} %get-tuple-element.26, bf16[8,128,512]{1,2,0:T(8,128)(2,1)S(1)} %get-tuple-element.25), kind=kOutput, calls=%fused_computation.31 | convolution fusion | flops 4838916096 | bytes 15990784 | tf_op jit(solution)/shard_map/abrcp,acq->brpq/dot_general | solution.py:273
  77.5 10.5 %shard_map.46 = f32[2,2,16,512]{3,2,1,0:T(8,128)S(1)} custom-call(f32[16,128,1152]{2,1,0:T(8,128)S(1)} %convolution_bitcast_fusion.y_ref, f32[16,128,1025]{2,1,0:T(8,128)} %get-tuple-element.7.lc_ref.uc_ref, f32[16,128,1025]{2,1,0:T(8,128)} %get-tuple-element.8.ls_ref.us_ref, f32[16,128,1025]{2,1,0:T(8,128)} %get-tuple-element.7.lc_ref.uc_ref, ...), custom_call_target="tpu_custom_call" | custom-call | tf_op jit(solution)/shard_map/pallas_call | solution.py:237
  89.2 0.6 broadcast_in_dim.44
  90.0 0.8 copy.28
  90.8 4.1 %all-to-all-start.1 = ((f32[16,1,2176]{2,1,0:T(1,128)}), f32[16,1,2176]{2,1,0:T(1,128)S(1)}, u32[]{:S(2)}, u32[]{:S(2)}) async-start(f32[16,1,2176]{2,1,0:T(1,128)} %copy.28), calls=%async_computation.1 | async-start | bytes 278528 | tf_op jit(solution)/shard_map/all_to_all | solution.py:336
  94.9 5.2 %fusion.46 = (f32[1025,160]{1,0:T(8,128)S(1)}, f32[1025,160]{1,0:T(8,128)}) fusion(s32[160]{0:T(256)S(1)} %and_select_fusion, s32[1025]{0:T(1024)S(1)} %pad_add_fusion), kind=kLoop, calls=%fused_computation.100 | loop fusion | flops 2460000 | bytes 1316740 | tf_op jit(solution)/shard_map/cos | solution.py:334
  100.1 3.0 %all-to-all-done.1 = f32[16,1,2176]{2,1,0:T(1,128)S(1)} async-done(((f32[16,1,2176]{2,1,0:T(1,128)}), f32[16,1,2176]{2,1,0:T(1,128)S(1)}, u32[]{:S(2)}, u32[]{:S(2)}) %all-to-all-start.1) | async-done | bytes 139296 | tf_op jit(solution)/shard_map/all_to_all | solution.py:336
  103.3 0.7 broadcast_in_dim.72
  103.9 4.4 %all-to-all-start.2 = ((f32[8,1,2176]{2,1,0:T(1,128)}), f32[8,1,2176]{2,1,0:T(1,128)S(1)}, u32[]{:S(2)}, u32[]{:S(2)}) async-start(f32[8,1,2176]{2,1,0:T(1,128)} %broadcast_in_dim.72), calls=%async_computation.2 | async-start | bytes 139264 | tf_op jit(solution)/shard_map/all_to_all | solution.py:339
  108.3 1.4 %pad_maximum_fusion = f32[2050,160]{1,0:T(8,128)S(1)} fusion(f32[1025,160]{1,0:T(8,128)} %get-tuple-element.20, f32[1025,160]{1,0:T(8,128)S(1)} %get-tuple-element.19), kind=kLoop, calls=%fused_computation.57 | loop fusion | flops 328000 | bytes 2624000 | tf_op jit(solution)/shard_map/concatenate | solution.py:334
  109.7 5.0 %all-to-all-done.2 = f32[8,1,2176]{2,1,0:T(1,128)S(1)} async-done(((f32[8,1,2176]{2,1,0:T(1,128)}), f32[8,1,2176]{2,1,0:T(1,128)S(1)}, u32[]{:S(2)}, u32[]{:S(2)}) %all-to-all-start.2) | async-done | bytes 69664 | tf_op jit(solution)/shard_map/all_to_all | solution.py:339
  114.7 0.6 slice.223
  116.0 0.9 fusion.52
  116.9 0.6 divide_multiply_fusion
  (41 shorter events, 2.2 us)
Async XLA Ops:
  6.4 11.8 %copy-start.2 = (s32[128]{0:T(128)S(1)}, s32[128]{0:T(128)}, u32[]{:S(2)}) copy-start(s32[128]{0:T(128)} %param.6) | copy-start | bytes 1540
  6.4 11.8 %copy-start.1 = (s32[128,2]{0,1:T(2,128)S(1)}, s32[128,2]{0,1:T(2,128)}, u32[]{:S(2)}) copy-start(s32[128,2]{0,1:T(2,128)} %param.5) | copy-start | bytes 3076
  6.4 11.9 %copy-start = (f32[2]{0:T(128)S(1)}, f32[2]{0:T(128)}, u32[]{:S(2)}) copy-start(f32[2]{0:T(128)} %param.7) | copy-start | bytes 28
  6.4 63.4 %all-to-all-start = ((bf16[128,128,128]{1,2,0:T(8,128)(2,1)}), bf16[128,128,128]{1,2,0:T(8,128)(2,1)}, u32[]{:S(2)}, u32[]{:S(2)}) async-start(bf16[128,128,128]{1,2,0:T(8,128)(2,1)} %bitcast.61), calls=%async_computation | async-start | bytes 8388608 | tf_op jit(solution)/shard_map/all_to_all | solution.py:263
  90.8 12.4 %all-to-all-start.1 = ((f32[16,1,2176]{2,1,0:T(1,128)}), f32[16,1,2176]{2,1,0:T(1,128)S(1)}, u32[]{:S(2)}, u32[]{:S(2)}) async-start(f32[16,1,2176]{2,1,0:T(1,128)} %copy.28), calls=%async_computation.1 | async-start | bytes 278528 | tf_op jit(solution)/shard_map/all_to_all | solution.py:336
  103.9 10.7 %all-to-all-start.2 = ((f32[8,1,2176]{2,1,0:T(1,128)}), f32[8,1,2176]{2,1,0:T(1,128)S(1)}, u32[]{:S(2)}, u32[]{:S(2)}) async-start(f32[8,1,2176]{2,1,0:T(1,128)} %broadcast_in_dim.72), calls=%async_computation.2 | async-start | bytes 139264 | tf_op jit(solution)/shard_map/all_to_all | solution.py:339

commit v9 on v7

--- a/solution.py
+++ b/solution.py
@@ -322,11 +322,11 @@
     final_table = lax.optimization_barrier(
         jnp.concatenate([jnp.cos(col_angles), -jnp.sin(col_angles)], axis=0)
     )
-    gathered = lax.all_to_all(packed, "det", 0, 0, tiled=True)
+    gathered = lax.all_to_all(packed.reshape(SR, -1, 128), "det", 0, 0, tiled=True)
     own = pairwise_sum([gathered[i] for i in range(det_size)])
     spread = jnp.broadcast_to(own, (scan_size,) + own.shape)
     gathered = lax.all_to_all(spread, "scan", 0, 0, tiled=True)
-    total = pairwise_sum([gathered[i] for i in range(scan_size)])
+    total = pairwise_sum([gathered[i] for i in range(scan_size)]).reshape(-1)
     bright_sum = total[lanes]
     picture = jnp.dot(total[:lanes], final_table, precision=EXACT_PRECISION)
     return (

time: 117 us -> 117 us (level)
  no operation moved by 1% of the time
where the time goes in v9:
time: 117 us
  waiting for transfers between devices  32 us (27%)
  other arithmetic  29.9 us (26%)
  starting transfers between devices  20.2 us (17%)
  local copies, waits for them, and re-layouts  13.4 us (11%)
  matrix products  9.33 us (8%)
  Pallas kernels  8.9 us (8%)
  between operations  2.82 us (2%)
    all_to_all x1, waiting for transfers between devices, local(): lax.all_to_all(blocks, ('scan', 'det'), split_axis=0, concat_axis=0, tile...  23.3 us
    mul x1, other arithmetic, local(): turn_sin * weights[None, :, None] * keep[None, None, :]  16.5 us
    all_to_all x1, starting transfers between devices, local(): lax.all_to_all(blocks, ('scan', 'det'), split_axis=0, concat_axis=0, tile...  11.7 us
    pallas_call x1, Pallas kernels, spectrum(): pl.pallas_call(spectrum_kernel, grid=(steps,), in_specs=[pl.BlockSpec(mem...  8.9 us
    dot_general x1, matrix products, local(): jnp.einsum('abrcp,acq->brpq', images, table.reshape(scan_size, tile, tabl...  7.45 us
    unnamed x7, local copies, waits for them, and re-layouts  6.41 us
    cos x1, other arithmetic, local(): jnp.cos(col_angles)  5.25 us
    all_to_all x1, waiting for transfers between devices, local(): gathered = lax.all_to_all(spread, 'scan', 0, 0, tiled=True)  5.15 us
  transfers between devices with their start and end apart: 3, of which 3 were waited for; matrix products, arithmetic and copies ran while one was open for 28% of the time, Pallas kernels for 0%

profile of v9, /device:TPU:0, one launch (start us, length us, event | category | flops | bytes accessed | tf_op | source)
XLA Modules:
  0.0 116.6 jit_solution(17771289284451041824)
XLA Ops:
  0.0 6.4 %copy.16 = bf16[1,128,16384]{1,2,0:T(8,128)(2,1)} copy(bf16[1,128,16384]{2,1,0:T(8,128)(2,1)} %param.4) | data formatting | bytes 8388608 | tf_op args[0]
  6.4 11.7 %all-to-all-start = ((bf16[128,128,128]{1,2,0:T(8,128)(2,1)}), bf16[128,128,128]{1,2,0:T(8,128)(2,1)}, u32[]{:S(2)}, u32[]{:S(2)}) async-start(bf16[128,128,128]{1,2,0:T(8,128)(2,1)} %bitcast.63), calls=%async_computation | async-start | bytes 8388608 | tf_op jit(solution)/shard_map/all_to_all | solution.py:252
  18.3 0.6 fusion.114
  20.8 0.5 fusion.44
  21.3 16.5 %fusion.12 = (f32[16,128,1025]{2,1,0:T(8,128)}, f32[16,128,1025]{2,1,0:T(8,128)}) fusion(f32[1025]{0:T(1024)S(1)} %fusion.88, f32[128]{0:T(128)S(1)} %convert_element_type.142, f32[128,1025]{1,0:T(8,128)S(1)} %get-tuple-element.24, f32[16,128]{1,0:T(8,128)S(1)} %get-tuple-element.32, f32[]{:T(128)} %bitcast.10, f32[128,1025]{1,0:T(8,128)S(1)} %get-tuple-element.23, ...), kind=kLoop, calls=%fused_computation.21 | loop fusion | flops 100761600 | bytes 17864200 | tf_op jit(solution)/shard_map/mul | solution.py:286
  37.8 0.6 convert_reduce_fusion
  38.6 1.6 %slice_reduce_fusion.1 = f32[16,128]{1,0:T(8,128)S(1)} fusion(f32[16,128,1025]{2,1,0:T(8,128)} %get-tuple-element.8.ls_ref.us_ref), kind=kLoop, calls=%fused_computation.90 | loop fusion | bytes 16384 | tf_op jit(solution)/shard_map/slice | solution.py:294
  40.1 1.6 %slice_reduce_fusion.2 = f32[16,128]{1,0:T(8,128)S(1)} fusion(f32[16,128,1025]{2,1,0:T(8,128)} %get-tuple-element.7.lc_ref.uc_ref), kind=kLoop, calls=%fused_computation.91 | loop fusion | bytes 16384 | tf_op jit(solution)/shard_map/slice | solution.py:293
  41.8 4.6 %fusion.33 = (bf16[8,128,512]{1,2,0:T(8,128)(2,1)S(1)}, bf16[8,128,512]{1,2,0:T(8,128)(2,1)S(1)}) fusion(s32[512]{0:T(512)S(1)} %slice.122, s32[8,128]{1,0:T(8,128)S(1)} %multiply_add_fusion), kind=kLoop, calls=%fused_computation.68 | loop fusion | flops 34078720 | bytes 2103296 | tf_op jit(solution)/shard_map/convert
  46.5 23.3 %all-to-all-done = bf16[128,128,128]{1,2,0:T(8,128)(2,1)} async-done(((bf16[128,128,128]{1,2,0:T(8,128)(2,1)}), bf16[128,128,128]{1,2,0:T(8,128)(2,1)}, u32[]{:S(2)}, u32[]{:S(2)}) %all-to-all-start) | async-done | bytes 4194336 | tf_op jit(solution)/shard_map/all_to_all | solution.py:252
  69.8 7.4 %convolution_bitcast_fusion.y_ref = f32[16,128,1152]{2,1,0:T(8,128)S(1)} fusion(bf16[8,16,128,128]{2,3,1,0:T(8,128)(2,1)} %bitcast.5, bf16[8,128,128]{1,2,0:T(8,128)(2,1)S(1)} %select_convert_fusion, bf16[8,128,512]{1,2,0:T(8,128)(2,1)S(1)} %get-tuple-element.26, bf16[8,128,512]{1,2,0:T(8,128)(2,1)S(1)} %get-tuple-element.25), kind=kOutput, calls=%fused_computation.31 | convolution fusion | flops 4838916096 | bytes 15990784 | tf_op jit(solution)/shard_map/abrcp,acq->brpq/dot_general | solution.py:262
  77.6 8.9 %shard_map.46 = f32[2,2,16,512]{3,2,1,0:T(8,128)S(1)} custom-call(f32[16,128,1152]{2,1,0:T(8,128)S(1)} %convolution_bitcast_fusion.y_ref, f32[16,128,1025]{2,1,0:T(8,128)} %get-tuple-element.7.lc_ref.uc_ref, f32[16,128,1025]{2,1,0:T(8,128)} %get-tuple-element.8.ls_ref.us_ref, f32[16,128,1025]{2,1,0:T(8,128)} %get-tuple-element.7.lc_ref.uc_ref, ...), custom_call_target="tpu_custom_call" | custom-call | tf_op jit(solution)/shard_map/pallas_call | solution.py:226
  87.7 0.6 broadcast_in_dim.44
  88.4 0.7 reshape.587
  89.1 4.1 %all-to-all-start.1 = ((f32[16,17,128]{2,1,0:T(8,128)}), f32[16,17,128]{2,1,0:T(8,128)S(1)}, u32[]{:S(2)}, u32[]{:S(2)}) async-start(f32[16,17,128]{2,1,0:T(8,128)} %reshape.587), calls=%async_computation.1 | async-start | bytes 393216 | tf_op jit(solution)/shard_map/all_to_all | solution.py:325
  93.2 5.2 %fusion.46 = (f32[1025,160]{1,0:T(8,128)S(1)}, f32[1025,160]{1,0:T(8,128)}) fusion(s32[160]{0:T(256)S(1)} %and_select_fusion, s32[1025]{0:T(1024)S(1)} %pad_add_fusion), kind=kLoop, calls=%fused_computation.100 | loop fusion | flops 2460000 | bytes 1316740 | tf_op jit(solution)/shard_map/cos | solution.py:323
  98.5 3.6 %all-to-all-done.1 = f32[16,17,128]{2,1,0:T(8,128)S(1)} async-done(((f32[16,17,128]{2,1,0:T(8,128)}), f32[16,17,128]{2,1,0:T(8,128)S(1)}, u32[]{:S(2)}, u32[]{:S(2)}) %all-to-all-start.1) | async-done | bytes 139296 | tf_op jit(solution)/shard_map/all_to_all | solution.py:325
  102.1 0.6 broadcast_in_dim.72
  102.8 4.4 %all-to-all-start.2 = ((f32[8,17,128]{2,1,0:T(8,128)}), f32[8,17,128]{2,1,0:T(8,128)S(1)}, u32[]{:S(2)}, u32[]{:S(2)}) async-start(f32[8,17,128]{2,1,0:T(8,128)} %broadcast_in_dim.72), calls=%async_computation.2 | async-start | bytes 196608 | tf_op jit(solution)/shard_map/all_to_all | solution.py:328
  107.2 1.4 %pad_maximum_fusion = f32[2050,160]{1,0:T(8,128)S(1)} fusion(f32[1025,160]{1,0:T(8,128)} %get-tuple-element.20, f32[1025,160]{1,0:T(8,128)S(1)} %get-tuple-element.19), kind=kLoop, calls=%fused_computation.57 | loop fusion | flops 328000 | bytes 2624000 | tf_op jit(solution)/shard_map/concatenate | solution.py:323
  108.6 5.1 %all-to-all-done.2 = f32[8,17,128]{2,1,0:T(8,128)S(1)} async-done(((f32[8,17,128]{2,1,0:T(8,128)}), f32[8,17,128]{2,1,0:T(8,128)S(1)}, u32[]{:S(2)}, u32[]{:S(2)}) %all-to-all-start.2) | async-done | bytes 69664 | tf_op jit(solution)/shard_map/all_to_all | solution.py:328
  113.7 0.6 slice.194
  115.0 0.9 fusion.115
  115.9 0.6 divide_multiply_fusion
  (42 shorter events, 2.1 us)
Async XLA Ops:
  6.4 11.8 %copy-start.2 = (s32[128]{0:T(128)S(1)}, s32[128]{0:T(128)}, u32[]{:S(2)}) copy-start(s32[128]{0:T(128)} %param.6) | copy-start | bytes 1540
  6.4 11.8 %copy-start.1 = (s32[128,2]{0,1:T(2,128)S(1)}, s32[128,2]{0,1:T(2,128)}, u32[]{:S(2)}) copy-start(s32[128,2]{0,1:T(2,128)} %param.5) | copy-start | bytes 3076
  6.4 11.9 %copy-start = (f32[2]{0:T(128)S(1)}, f32[2]{0:T(128)}, u32[]{:S(2)}) copy-start(f32[2]{0:T(128)} %param.7) | copy-start | bytes 28
  6.4 63.4 %all-to-all-start = ((bf16[128,128,128]{1,2,0:T(8,128)(2,1)}), bf16[128,128,128]{1,2,0:T(8,128)(2,1)}, u32[]{:S(2)}, u32[]{:S(2)}) async-start(bf16[128,128,128]{1,2,0:T(8,128)(2,1)} %bitcast.63), calls=%async_computation | async-start | bytes 8388608 | tf_op jit(solution)/shard_map/all_to_all | solution.py:252
  89.1 13.0 %all-to-all-start.1 = ((f32[16,17,128]{2,1,0:T(8,128)}), f32[16,17,128]{2,1,0:T(8,128)S(1)}, u32[]{:S(2)}, u32[]{:S(2)}) async-start(f32[16,17,128]{2,1,0:T(8,128)} %reshape.587), calls=%async_computation.1 | async-start | bytes 393216 | tf_op jit(solution)/shard_map/all_to_all | solution.py:325
  102.8 10.9 %all-to-all-start.2 = ((f32[8,17,128]{2,1,0:T(8,128)}), f32[8,17,128]{2,1,0:T(8,128)S(1)}, u32[]{:S(2)}, u32[]{:S(2)}) async-start(f32[8,17,128]{2,1,0:T(8,128)} %broadcast_in_dim.72), calls=%async_computation.2 | async-start | bytes 196608 | tf_op jit(solution)/shard_map/all_to_all | solution.py:328

commit v10 on v7

--- a/solution.py
+++ b/solution.py
@@ -187,30 +187,40 @@
 
 
 def spectrum_kernel(y_ref, lc_ref, ls_ref, uc_ref, us_ref, out_ref, acc_ref):
-    acc_ref[...] = jnp.zeros(acc_ref.shape, acc_ref.dtype)
     width = lc_ref.shape[2]
     low = pl.multiple_of(pl.program_id(0) * width, width)
     high = pl.multiple_of(pl.program_id(0) * width + SC // 2, width)
 
-    def body(i, carry):
-        rows = pl.ds(pl.multiple_of(i * 8, 8), 8)
-        full = fft16(
-            [(y_ref[r, rows, pl.ds(low, width)], y_ref[r, rows, pl.ds(high, width)]) for r in range(SR)]
-        )
+    def pass_for(upper):
+        def body(i, acc):
+            rows = pl.ds(pl.multiple_of(i * 8, 8), 8)
+            full = fft16(
+                [(y_ref[r, rows, pl.ds(low, width)], y_ref[r, rows, pl.ds(high, width)]) for r in range(SR)]
+            )
+            out = []
+            for s in range(SR):
+                if upper:
+                    fr, fi = full[(SR - s) % SR]
+                    fi = -fi
+                    tc = uc_ref[s, rows, :]
+                    ts = us_ref[s, rows, :]
+                else:
+                    fr, fi = full[s]
+                    tc = lc_ref[s, rows, :]
+                    ts = ls_ref[s, rows, :]
+                out.append(acc[2 * s] + (fr * tc - fi * ts))
+                out.append(acc[2 * s + 1] + (fr * ts + fi * tc))
+            return tuple(out)
+
+        zero = jnp.zeros((8, width), jnp.float32)
+        acc = lax.fori_loop(0, lc_ref.shape[1] // 8, body, (zero,) * (2 * SR))
+        part = 1 if upper else 0
         for s in range(SR):
-            fr, fi = full[s]
-            tc = lc_ref[s, rows, :]
-            ts = ls_ref[s, rows, :]
-            acc_ref[0, 0, s] += fr * tc - fi * ts
-            acc_ref[0, 1, s] += fr * ts + fi * tc
-            gr, gi = full[(SR - s) % SR]
-            tc = uc_ref[s, rows, :]
-            ts = us_ref[s, rows, :]
-            acc_ref[1, 0, s] += gr * tc + gi * ts
-            acc_ref[1, 1, s] += gr * ts - gi * tc
-        return carry
-
-    lax.fori_loop(0, lc_ref.shape[1] // 8, body, 0)
+            acc_ref[part, 0, s] = acc[2 * s]
+            acc_ref[part, 1, s] = acc[2 * s + 1]
+
+    pass_for(False)
+    pass_for(True)
     for a in range(2):
         for b in range(2):
             out_ref[a, b] = jnp.sum(acc_ref[a, b], axis=1)

time: 117 us -> 118 us (level)
  Pallas kernels: 8.87 us -> 10.6 us
    pallas_call x1, Pallas kernels: 8.87 us -> 10.6 us  [spectrum(): pl.pallas_call(spectrum_kernel, grid=(steps,), in_specs=[pl.BlockSpec(mem...]
where the time goes in v10:
time: 118 us
  waiting for transfers between devices  31.2 us (26%)
  other arithmetic  30 us (25%)
  starting transfers between devices  20.2 us (17%)
  local copies, waits for them, and re-layouts  13.5 us (11%)
  Pallas kernels  10.6 us (9%)
  matrix products  9.32 us (8%)
  between operations  2.88 us (2%)
    all_to_all x1, waiting for transfers between devices, local(): lax.all_to_all(blocks, ('scan', 'det'), split_axis=0, concat_axis=0, tile...  23.2 us
    mul x1, other arithmetic, local(): turn_sin * weights[None, :, None] * keep[None, None, :]  16.5 us
    all_to_all x1, starting transfers between devices, local(): lax.all_to_all(blocks, ('scan', 'det'), split_axis=0, concat_axis=0, tile...  11.7 us
    pallas_call x1, Pallas kernels, spectrum(): pl.pallas_call(spectrum_kernel, grid=(steps,), in_specs=[pl.BlockSpec(mem...  10.6 us
    dot_general x1, matrix products, local(): jnp.einsum('abrcp,acq->brpq', images, table.reshape(scan_size, tile, tabl...  7.44 us
    unnamed x7, local copies, waits for them, and re-layouts  6.41 us
    cos x1, other arithmetic, local(): jnp.cos(col_angles)  5.25 us
    all_to_all x1, waiting for transfers between devices, local(): gathered = lax.all_to_all(spread, 'scan', 0, 0, tiled=True)  4.97 us
  transfers between devices with their start and end apart: 3, of which 3 were waited for; matrix products, arithmetic and copies ran while one was open for 28% of the time, Pallas kernels for 0%

profile of v10, /device:TPU:0, one launch (start us, length us, event | category | flops | bytes accessed | tf_op | source)
XLA Modules:
  0.0 117.7 jit_solution(797339395424003165)
XLA Ops:
  0.0 6.4 %copy.22 = bf16[1,128,16384]{1,2,0:T(8,128)(2,1)} copy(bf16[1,128,16384]{2,1,0:T(8,128)(2,1)} %param.4) | data formatting | bytes 8388608 | tf_op args[0]
  6.4 11.7 %all-to-all-start = ((bf16[128,128,128]{1,2,0:T(8,128)(2,1)}), bf16[128,128,128]{1,2,0:T(8,128)(2,1)}, u32[]{:S(2)}, u32[]{:S(2)}) async-start(bf16[128,128,128]{1,2,0:T(8,128)(2,1)} %bitcast.61), calls=%async_computation | async-start | bytes 8388608 | tf_op jit(solution)/shard_map/all_to_all | solution.py:262
  18.3 0.6 fusion.112
  20.9 0.5 fusion.44
  21.4 16.5 %fusion.12 = (f32[16,128,1025]{2,1,0:T(8,128)}, f32[16,128,1025]{2,1,0:T(8,128)}) fusion(f32[1025]{0:T(1024)S(1)} %fusion.86, f32[128]{0:T(128)S(1)} %convert_element_type.142, f32[128,1025]{1,0:T(8,128)S(1)} %get-tuple-element.24, f32[16,128]{1,0:T(8,128)S(1)} %get-tuple-element.32, f32[]{:T(128)} %bitcast.10, f32[128,1025]{1,0:T(8,128)S(1)} %get-tuple-element.23, ...), kind=kLoop, calls=%fused_computation.21 | loop fusion | flops 100761600 | bytes 17864200 | tf_op jit(solution)/shard_map/mul | solution.py:296
  37.9 0.6 convert_reduce_fusion
  38.7 1.6 %slice_reduce_fusion.1 = f32[16,128]{1,0:T(8,128)S(1)} fusion(f32[16,128,1025]{2,1,0:T(8,128)} %get-tuple-element.8.ls_ref.us_ref), kind=kLoop, calls=%fused_computation.90 | loop fusion | bytes 16384 | tf_op jit(solution)/shard_map/slice | solution.py:304
  40.2 1.6 %slice_reduce_fusion.2 = f32[16,128]{1,0:T(8,128)S(1)} fusion(f32[16,128,1025]{2,1,0:T(8,128)} %get-tuple-element.7.lc_ref.uc_ref), kind=kLoop, calls=%fused_computation.91 | loop fusion | bytes 16384 | tf_op jit(solution)/shard_map/slice | solution.py:303
  41.9 4.6 %fusion.33 = (bf16[8,128,512]{1,2,0:T(8,128)(2,1)S(1)}, bf16[8,128,512]{1,2,0:T(8,128)(2,1)S(1)}) fusion(s32[512]{0:T(512)S(1)} %slice.150, s32[8,128]{1,0:T(8,128)S(1)} %multiply_add_fusion), kind=kLoop, calls=%fused_computation.68 | loop fusion | flops 34078720 | bytes 2103296 | tf_op jit(solution)/shard_map/convert
  46.6 23.2 %all-to-all-done = bf16[128,128,128]{1,2,0:T(8,128)(2,1)} async-done(((bf16[128,128,128]{1,2,0:T(8,128)(2,1)}), bf16[128,128,128]{1,2,0:T(8,128)(2,1)}, u32[]{:S(2)}, u32[]{:S(2)}) %all-to-all-start) | async-done | bytes 4194336 | tf_op jit(solution)/shard_map/all_to_all | solution.py:262
  69.8 7.4 %convolution_bitcast_fusion.y_ref = f32[16,128,1152]{2,1,0:T(8,128)S(1)} fusion(bf16[8,16,128,128]{2,3,1,0:T(8,128)(2,1)} %bitcast.5, bf16[8,128,128]{1,2,0:T(8,128)(2,1)S(1)} %select_convert_fusion, bf16[8,128,512]{1,2,0:T(8,128)(2,1)S(1)} %get-tuple-element.26, bf16[8,128,512]{1,2,0:T(8,128)(2,1)S(1)} %get-tuple-element.25), kind=kOutput, calls=%fused_computation.31 | convolution fusion | flops 4838916096 | bytes 15990784 | tf_op jit(solution)/shard_map/abrcp,acq->brpq/dot_general | solution.py:272
  77.5 10.6 %shard_map.46 = f32[2,2,16,512]{3,2,1,0:T(8,128)S(1)} custom-call(f32[16,128,1152]{2,1,0:T(8,128)S(1)} %convolution_bitcast_fusion.y_ref, f32[16,128,1025]{2,1,0:T(8,128)} %get-tuple-element.7.lc_ref.uc_ref, f32[16,128,1025]{2,1,0:T(8,128)} %get-tuple-element.8.ls_ref.us_ref, f32[16,128,1025]{2,1,0:T(8,128)} %get-tuple-element.7.lc_ref.uc_ref, ...), custom_call_target="tpu_custom_call" | custom-call | tf_op jit(solution)/shard_map/pallas_call | solution.py:236
  89.4 0.6 broadcast_in_dim.44
  90.1 0.8 copy.28
  90.9 4.1 %all-to-all-start.1 = ((f32[16,1,2176]{2,1,0:T(1,128)}), f32[16,1,2176]{2,1,0:T(1,128)S(1)}, u32[]{:S(2)}, u32[]{:S(2)}) async-start(f32[16,1,2176]{2,1,0:T(1,128)} %copy.28), calls=%async_computation.1 | async-start | bytes 278528 | tf_op jit(solution)/shard_map/all_to_all | solution.py:335
  95.1 5.2 %fusion.46 = (f32[1025,160]{1,0:T(8,128)S(1)}, f32[1025,160]{1,0:T(8,128)}) fusion(s32[160]{0:T(256)S(1)} %and_select_fusion, s32[1025]{0:T(1024)S(1)} %pad_add_fusion), kind=kLoop, calls=%fused_computation.100 | loop fusion | flops 2460000 | bytes 1316740 | tf_op jit(solution)/shard_map/cos | solution.py:333
  100.3 3.0 %all-to-all-done.1 = f32[16,1,2176]{2,1,0:T(1,128)S(1)} async-done(((f32[16,1,2176]{2,1,0:T(1,128)}), f32[16,1,2176]{2,1,0:T(1,128)S(1)}, u32[]{:S(2)}, u32[]{:S(2)}) %all-to-all-start.1) | async-done | bytes 139296 | tf_op jit(solution)/shard_map/all_to_all | solution.py:335
  103.4 0.7 broadcast_in_dim.72
  104.1 4.4 %all-to-all-start.2 = ((f32[8,1,2176]{2,1,0:T(1,128)}), f32[8,1,2176]{2,1,0:T(1,128)S(1)}, u32[]{:S(2)}, u32[]{:S(2)}) async-start(f32[8,1,2176]{2,1,0:T(1,128)} %broadcast_in_dim.72), calls=%async_computation.2 | async-start | bytes 139264 | tf_op jit(solution)/shard_map/all_to_all | solution.py:338
  108.5 1.4 %pad_maximum_fusion = f32[2050,160]{1,0:T(8,128)S(1)} fusion(f32[1025,160]{1,0:T(8,128)} %get-tuple-element.20, f32[1025,160]{1,0:T(8,128)S(1)} %get-tuple-element.19), kind=kLoop, calls=%fused_computation.57 | loop fusion | flops 328000 | bytes 2624000 | tf_op jit(solution)/shard_map/concatenate | solution.py:333
  109.9 5.0 %all-to-all-done.2 = f32[8,1,2176]{2,1,0:T(1,128)S(1)} async-done(((f32[8,1,2176]{2,1,0:T(1,128)}), f32[8,1,2176]{2,1,0:T(1,128)S(1)}, u32[]{:S(2)}, u32[]{:S(2)}) %all-to-all-start.2) | async-done | bytes 69664 | tf_op jit(solution)/shard_map/all_to_all | solution.py:338
  114.9 0.6 slice.223
  116.1 0.9 fusion.52
  117.1 0.6 divide_multiply_fusion
  (41 shorter events, 2.2 us)
Async XLA Ops:
  6.4 11.8 %copy-start.2 = (s32[128]{0:T(128)S(1)}, s32[128]{0:T(128)}, u32[]{:S(2)}) copy-start(s32[128]{0:T(128)} %param.6) | copy-start | bytes 1540
  6.4 11.8 %copy-start.1 = (s32[128,2]{0,1:T(2,128)S(1)}, s32[128,2]{0,1:T(2,128)}, u32[]{:S(2)}) copy-start(s32[128,2]{0,1:T(2,128)} %param.5) | copy-start | bytes 3076
  6.4 11.9 %copy-start = (f32[2]{0:T(128)S(1)}, f32[2]{0:T(128)}, u32[]{:S(2)}) copy-start(f32[2]{0:T(128)} %param.7) | copy-start | bytes 28
  6.4 63.4 %all-to-all-start = ((bf16[128,128,128]{1,2,0:T(8,128)(2,1)}), bf16[128,128,128]{1,2,0:T(8,128)(2,1)}, u32[]{:S(2)}, u32[]{:S(2)}) async-start(bf16[128,128,128]{1,2,0:T(8,128)(2,1)} %bitcast.61), calls=%async_computation | async-start | bytes 8388608 | tf_op jit(solution)/shard_map/all_to_all | solution.py:262
  90.9 12.4 %all-to-all-start.1 = ((f32[16,1,2176]{2,1,0:T(1,128)}), f32[16,1,2176]{2,1,0:T(1,128)S(1)}, u32[]{:S(2)}, u32[]{:S(2)}) async-start(f32[16,1,2176]{2,1,0:T(1,128)} %copy.28), calls=%async_computation.1 | async-start | bytes 278528 | tf_op jit(solution)/shard_map/all_to_all | solution.py:335
  104.1 10.7 %all-to-all-start.2 = ((f32[8,1,2176]{2,1,0:T(1,128)}), f32[8,1,2176]{2,1,0:T(1,128)S(1)}, u32[]{:S(2)}, u32[]{:S(2)}) async-start(f32[8,1,2176]{2,1,0:T(1,128)} %broadcast_in_dim.72), calls=%async_computation.2 | async-start | bytes 139264 | tf_op jit(solution)/shard_map/all_to_all | solution.py:338

commit v11 on v7

--- a/solution.py
+++ b/solution.py
@@ -210,7 +210,7 @@
             acc_ref[1, 1, s] += gr * ts - gi * tc
         return carry
 
-    lax.fori_loop(0, lc_ref.shape[1] // 8, body, 0)
+    lax.fori_loop(0, lc_ref.shape[1] // 8, body, 0, unroll=2)
     for a in range(2):
         for b in range(2):
             out_ref[a, b] = jnp.sum(acc_ref[a, b], axis=1)

time: 117 us -> 116 us (level)
  transfers between devices with their start and end apart: 3 -> 3, of which waited for: 3 -> 3; matrix products, arithmetic and copies ran while one was open for 28% -> 29% of each run, Pallas kernels for 0% -> 0%
where the time goes in v11:
time: 116 us
  waiting for transfers between devices  31.2 us (27%)
  other arithmetic  30 us (26%)
  starting transfers between devices  20.2 us (17%)
  local copies, waits for them, and re-layouts  13.5 us (12%)
  matrix products  9.32 us (8%)
  Pallas kernels  8.5 us (7%)
  between operations  2.88 us (2%)
    all_to_all x1, waiting for transfers between devices, local(): lax.all_to_all(blocks, ('scan', 'det'), split_axis=0, concat_axis=0, tile...  23.2 us
    mul x1, other arithmetic, local(): turn_sin * weights[None, :, None] * keep[None, None, :]  16.5 us
    all_to_all x1, starting transfers between devices, local(): lax.all_to_all(blocks, ('scan', 'det'), split_axis=0, concat_axis=0, tile...  11.7 us
    pallas_call x1, Pallas kernels, spectrum(): pl.pallas_call(spectrum_kernel, grid=(steps,), in_specs=[pl.BlockSpec(mem...  8.5 us
    dot_general x1, matrix products, local(): jnp.einsum('abrcp,acq->brpq', images, table.reshape(scan_size, tile, tabl...  7.44 us
    unnamed x7, local copies, waits for them, and re-layouts  6.41 us
    cos x1, other arithmetic, local(): jnp.cos(col_angles)  5.25 us
    all_to_all x1, waiting for transfers between devices, local(): gathered = lax.all_to_all(spread, 'scan', 0, 0, tiled=True)  4.97 us
  transfers between devices with their start and end apart: 3, of which 3 were waited for; matrix products, arithmetic and copies ran while one was open for 29% of the time, Pallas kernels for 0%

profile of v11, /device:TPU:0, one launch (start us, length us, event | category | flops | bytes accessed | tf_op | source)
XLA Modules:
  0.0 115.6 jit_solution(3278744300304186281)
XLA Ops:
  0.0 6.4 %copy.22 = bf16[1,128,16384]{1,2,0:T(8,128)(2,1)} copy(bf16[1,128,16384]{2,1,0:T(8,128)(2,1)} %param.4) | data formatting | bytes 8388608 | tf_op args[0]
  6.4 11.7 %all-to-all-start = ((bf16[128,128,128]{1,2,0:T(8,128)(2,1)}), bf16[128,128,128]{1,2,0:T(8,128)(2,1)}, u32[]{:S(2)}, u32[]{:S(2)}) async-start(bf16[128,128,128]{1,2,0:T(8,128)(2,1)} %bitcast.61), calls=%async_computation | async-start | bytes 8388608 | tf_op jit(solution)/shard_map/all_to_all | solution.py:252
  18.3 0.6 fusion.112
  20.9 0.5 fusion.44
  21.4 16.5 %fusion.12 = (f32[16,128,1025]{2,1,0:T(8,128)}, f32[16,128,1025]{2,1,0:T(8,128)}) fusion(f32[1025]{0:T(1024)S(1)} %fusion.86, f32[128]{0:T(128)S(1)} %convert_element_type.142, f32[128,1025]{1,0:T(8,128)S(1)} %get-tuple-element.24, f32[16,128]{1,0:T(8,128)S(1)} %get-tuple-element.32, f32[]{:T(128)} %bitcast.10, f32[128,1025]{1,0:T(8,128)S(1)} %get-tuple-element.23, ...), kind=kLoop, calls=%fused_computation.21 | loop fusion | flops 100761600 | bytes 17864200 | tf_op jit(solution)/shard_map/mul | solution.py:286
  37.9 0.6 convert_reduce_fusion
  38.7 1.6 %slice_reduce_fusion.1 = f32[16,128]{1,0:T(8,128)S(1)} fusion(f32[16,128,1025]{2,1,0:T(8,128)} %get-tuple-element.8.ls_ref.us_ref), kind=kLoop, calls=%fused_computation.90 | loop fusion | bytes 16384 | tf_op jit(solution)/shard_map/slice | solution.py:294
  40.2 1.6 %slice_reduce_fusion.2 = f32[16,128]{1,0:T(8,128)S(1)} fusion(f32[16,128,1025]{2,1,0:T(8,128)} %get-tuple-element.7.lc_ref.uc_ref), kind=kLoop, calls=%fused_computation.91 | loop fusion | bytes 16384 | tf_op jit(solution)/shard_map/slice | solution.py:293
  41.9 4.6 %fusion.33 = (bf16[8,128,512]{1,2,0:T(8,128)(2,1)S(1)}, bf16[8,128,512]{1,2,0:T(8,128)(2,1)S(1)}) fusion(s32[512]{0:T(512)S(1)} %slice.150, s32[8,128]{1,0:T(8,128)S(1)} %multiply_add_fusion), kind=kLoop, calls=%fused_computation.68 | loop fusion | flops 34078720 | bytes 2103296 | tf_op jit(solution)/shard_map/convert
  46.6 23.2 %all-to-all-done = bf16[128,128,128]{1,2,0:T(8,128)(2,1)} async-done(((bf16[128,128,128]{1,2,0:T(8,128)(2,1)}), bf16[128,128,128]{1,2,0:T(8,128)(2,1)}, u32[]{:S(2)}, u32[]{:S(2)}) %all-to-all-start) | async-done | bytes 4194336 | tf_op jit(solution)/shard_map/all_to_all | solution.py:252
  69.8 7.4 %convolution_bitcast_fusion.y_ref = f32[16,128,1152]{2,1,0:T(8,128)S(1)} fusion(bf16[8,16,128,128]{2,3,1,0:T(8,128)(2,1)} %bitcast.5, bf16[8,128,128]{1,2,0:T(8,128)(2,1)S(1)} %select_convert_fusion, bf16[8,128,512]{1,2,0:T(8,128)(2,1)S(1)} %get-tuple-element.26, bf16[8,128,512]{1,2,0:T(8,128)(2,1)S(1)} %get-tuple-element.25), kind=kOutput, calls=%fused_computation.31 | convolution fusion | flops 4838916096 | bytes 15990784 | tf_op jit(solution)/shard_map/abrcp,acq->brpq/dot_general | solution.py:262
  77.5 8.5 %shard_map.46 = f32[2,2,16,512]{3,2,1,0:T(8,128)S(1)} custom-call(f32[16,128,1152]{2,1,0:T(8,128)S(1)} %convolution_bitcast_fusion.y_ref, f32[16,128,1025]{2,1,0:T(8,128)} %get-tuple-element.7.lc_ref.uc_ref, f32[16,128,1025]{2,1,0:T(8,128)} %get-tuple-element.8.ls_ref.us_ref, f32[16,128,1025]{2,1,0:T(8,128)} %get-tuple-element.7.lc_ref.uc_ref, ...), custom_call_target="tpu_custom_call" | custom-call | tf_op jit(solution)/shard_map/pallas_call | solution.py:226
  87.2 0.6 broadcast_in_dim.44
  88.0 0.8 copy.28
  88.8 4.1 %all-to-all-start.1 = ((f32[16,1,2176]{2,1,0:T(1,128)}), f32[16,1,2176]{2,1,0:T(1,128)S(1)}, u32[]{:S(2)}, u32[]{:S(2)}) async-start(f32[16,1,2176]{2,1,0:T(1,128)} %copy.28), calls=%async_computation.1 | async-start | bytes 278528 | tf_op jit(solution)/shard_map/all_to_all | solution.py:325
  92.9 5.2 %fusion.46 = (f32[1025,160]{1,0:T(8,128)S(1)}, f32[1025,160]{1,0:T(8,128)}) fusion(s32[160]{0:T(256)S(1)} %and_select_fusion, s32[1025]{0:T(1024)S(1)} %pad_add_fusion), kind=kLoop, calls=%fused_computation.100 | loop fusion | flops 2460000 | bytes 1316740 | tf_op jit(solution)/shard_map/cos | solution.py:323
  98.2 3.0 %all-to-all-done.1 = f32[16,1,2176]{2,1,0:T(1,128)S(1)} async-done(((f32[16,1,2176]{2,1,0:T(1,128)}), f32[16,1,2176]{2,1,0:T(1,128)S(1)}, u32[]{:S(2)}, u32[]{:S(2)}) %all-to-all-start.1) | async-done | bytes 139296 | tf_op jit(solution)/shard_map/all_to_all | solution.py:325
  101.3 0.7 broadcast_in_dim.72
  102.0 4.4 %all-to-all-start.2 = ((f32[8,1,2176]{2,1,0:T(1,128)}), f32[8,1,2176]{2,1,0:T(1,128)S(1)}, u32[]{:S(2)}, u32[]{:S(2)}) async-start(f32[8,1,2176]{2,1,0:T(1,128)} %broadcast_in_dim.72), calls=%async_computation.2 | async-start | bytes 139264 | tf_op jit(solution)/shard_map/all_to_all | solution.py:328
  106.3 1.4 %pad_maximum_fusion = f32[2050,160]{1,0:T(8,128)S(1)} fusion(f32[1025,160]{1,0:T(8,128)} %get-tuple-element.20, f32[1025,160]{1,0:T(8,128)S(1)} %get-tuple-element.19), kind=kLoop, calls=%fused_computation.57 | loop fusion | flops 328000 | bytes 2624000 | tf_op jit(solution)/shard_map/concatenate | solution.py:323
  107.7 5.0 %all-to-all-done.2 = f32[8,1,2176]{2,1,0:T(1,128)S(1)} async-done(((f32[8,1,2176]{2,1,0:T(1,128)}), f32[8,1,2176]{2,1,0:T(1,128)S(1)}, u32[]{:S(2)}, u32[]{:S(2)}) %all-to-all-start.2) | async-done | bytes 69664 | tf_op jit(solution)/shard_map/all_to_all | solution.py:328
  112.7 0.6 slice.223
  114.0 0.9 fusion.52
  115.0 0.6 divide_multiply_fusion
  (41 shorter events, 2.2 us)
Async XLA Ops:
  6.4 11.8 %copy-start.2 = (s32[128]{0:T(128)S(1)}, s32[128]{0:T(128)}, u32[]{:S(2)}) copy-start(s32[128]{0:T(128)} %param.6) | copy-start | bytes 1540
  6.4 11.8 %copy-start.1 = (s32[128,2]{0,1:T(2,128)S(1)}, s32[128,2]{0,1:T(2,128)}, u32[]{:S(2)}) copy-start(s32[128,2]{0,1:T(2,128)} %param.5) | copy-start | bytes 3076
  6.4 11.9 %copy-start = (f32[2]{0:T(128)S(1)}, f32[2]{0:T(128)}, u32[]{:S(2)}) copy-start(f32[2]{0:T(128)} %param.7) | copy-start | bytes 28
  6.4 63.4 %all-to-all-start = ((bf16[128,128,128]{1,2,0:T(8,128)(2,1)}), bf16[128,128,128]{1,2,0:T(8,128)(2,1)}, u32[]{:S(2)}, u32[]{:S(2)}) async-start(bf16[128,128,128]{1,2,0:T(8,128)(2,1)} %bitcast.61), calls=%async_computation | async-start | bytes 8388608 | tf_op jit(solution)/shard_map/all_to_all | solution.py:252
  88.8 12.4 %all-to-all-start.1 = ((f32[16,1,2176]{2,1,0:T(1,128)}), f32[16,1,2176]{2,1,0:T(1,128)S(1)}, u32[]{:S(2)}, u32[]{:S(2)}) async-start(f32[16,1,2176]{2,1,0:T(1,128)} %copy.28), calls=%async_computation.1 | async-start | bytes 278528 | tf_op jit(solution)/shard_map/all_to_all | solution.py:325
  102.0 10.7 %all-to-all-start.2 = ((f32[8,1,2176]{2,1,0:T(1,128)}), f32[8,1,2176]{2,1,0:T(1,128)S(1)}, u32[]{:S(2)}, u32[]{:S(2)}) async-start(f32[8,1,2176]{2,1,0:T(1,128)} %broadcast_in_dim.72), calls=%async_computation.2 | async-start | bytes 139264 | tf_op jit(solution)/shard_map/all_to_all | solution.py:328

commit v12 on v11

--- a/solution.py
+++ b/solution.py
@@ -210,7 +210,7 @@
             acc_ref[1, 1, s] += gr * ts - gi * tc
         return carry
 
-    lax.fori_loop(0, lc_ref.shape[1] // 8, body, 0, unroll=2)
+    lax.fori_loop(0, lc_ref.shape[1] // 8, body, 0, unroll=4)
     for a in range(2):
         for b in range(2):
             out_ref[a, b] = jnp.sum(acc_ref[a, b], axis=1)

time: 116 us -> 116 us (level)
  no operation moved by 1% of the time
where the time goes in v12:
time: 116 us; the launch traced here: 115 us
  waiting for transfers between devices  31.2 us (27%)
  other arithmetic  30 us (26%)
  starting transfers between devices  20.2 us (17%)
  local copies, waits for them, and re-layouts  13.5 us (12%)
  matrix products  9.32 us (8%)
  Pallas kernels  8.33 us (7%)
  between operations  2.88 us (2%)
    all_to_all x1, waiting for transfers between devices, local(): lax.all_to_all(blocks, ('scan', 'det'), split_axis=0, concat_axis=0, tile...  23.2 us
    mul x1, other arithmetic, local(): turn_sin * weights[None, :, None] * keep[None, None, :]  16.5 us
    all_to_all x1, starting transfers between devices, local(): lax.all_to_all(blocks, ('scan', 'det'), split_axis=0, concat_axis=0, tile...  11.7 us
    pallas_call x1, Pallas kernels, spectrum(): pl.pallas_call(spectrum_kernel, grid=(steps,), in_specs=[pl.BlockSpec(mem...  8.33 us
    dot_general x1, matrix products, local(): jnp.einsum('abrcp,acq->brpq', images, table.reshape(scan_size, tile, tabl...  7.44 us
    unnamed x7, local copies, waits for them, and re-layouts  6.41 us
    cos x1, other arithmetic, local(): jnp.cos(col_angles)  5.25 us
    all_to_all x1, waiting for transfers between devices, local(): gathered = lax.all_to_all(spread, 'scan', 0, 0, tiled=True)  4.97 us
  transfers between devices with their start and end apart: 3, of which 3 were waited for; matrix products, arithmetic and copies ran while one was open for 29% of the time, Pallas kernels for 0%

profile of v12, /device:TPU:0, one launch (start us, length us, event | category | flops | bytes accessed | tf_op | source)
XLA Modules:
  0.0 115.4 jit_solution(2903924039473483187)
XLA Ops:
  0.0 6.4 %copy.22 = bf16[1,128,16384]{1,2,0:T(8,128)(2,1)} copy(bf16[1,128,16384]{2,1,0:T(8,128)(2,1)} %param.4) | data formatting | bytes 8388608 | tf_op args[0]
  6.4 11.7 %all-to-all-start = ((bf16[128,128,128]{1,2,0:T(8,128)(2,1)}), bf16[128,128,128]{1,2,0:T(8,128)(2,1)}, u32[]{:S(2)}, u32[]{:S(2)}) async-start(bf16[128,128,128]{1,2,0:T(8,128)(2,1)} %bitcast.61), calls=%async_computation | async-start | bytes 8388608 | tf_op jit(solution)/shard_map/all_to_all | solution.py:252
  18.3 0.6 fusion.112
  20.9 0.5 fusion.44
  21.4 16.5 %fusion.12 = (f32[16,128,1025]{2,1,0:T(8,128)}, f32[16,128,1025]{2,1,0:T(8,128)}) fusion(f32[1025]{0:T(1024)S(1)} %fusion.86, f32[128]{0:T(128)S(1)} %convert_element_type.142, f32[128,1025]{1,0:T(8,128)S(1)} %get-tuple-element.24, f32[16,128]{1,0:T(8,128)S(1)} %get-tuple-element.32, f32[]{:T(128)} %bitcast.10, f32[128,1025]{1,0:T(8,128)S(1)} %get-tuple-element.23, ...), kind=kLoop, calls=%fused_computation.21 | loop fusion | flops 100761600 | bytes 17864200 | tf_op jit(solution)/shard_map/mul | solution.py:286
  37.9 0.6 convert_reduce_fusion
  38.7 1.6 %slice_reduce_fusion.1 = f32[16,128]{1,0:T(8,128)S(1)} fusion(f32[16,128,1025]{2,1,0:T(8,128)} %get-tuple-element.8.ls_ref.us_ref), kind=kLoop, calls=%fused_computation.90 | loop fusion | bytes 16384 | tf_op jit(solution)/shard_map/slice | solution.py:294
  40.2 1.6 %slice_reduce_fusion.2 = f32[16,128]{1,0:T(8,128)S(1)} fusion(f32[16,128,1025]{2,1,0:T(8,128)} %get-tuple-element.7.lc_ref.uc_ref), kind=kLoop, calls=%fused_computation.91 | loop fusion | bytes 16384 | tf_op jit(solution)/shard_map/slice | solution.py:293
  41.9 4.6 %fusion.33 = (bf16[8,128,512]{1,2,0:T(8,128)(2,1)S(1)}, bf16[8,128,512]{1,2,0:T(8,128)(2,1)S(1)}) fusion(s32[512]{0:T(512)S(1)} %slice.150, s32[8,128]{1,0:T(8,128)S(1)} %multiply_add_fusion), kind=kLoop, calls=%fused_computation.68 | loop fusion | flops 34078720 | bytes 2103296 | tf_op jit(solution)/shard_map/convert
  46.6 23.2 %all-to-all-done = bf16[128,128,128]{1,2,0:T(8,128)(2,1)} async-done(((bf16[128,128,128]{1,2,0:T(8,128)(2,1)}), bf16[128,128,128]{1,2,0:T(8,128)(2,1)}, u32[]{:S(2)}, u32[]{:S(2)}) %all-to-all-start) | async-done | bytes 4194336 | tf_op jit(solution)/shard_map/all_to_all | solution.py:252
  69.8 7.4 %convolution_bitcast_fusion.y_ref = f32[16,128,1152]{2,1,0:T(8,128)S(1)} fusion(bf16[8,16,128,128]{2,3,1,0:T(8,128)(2,1)} %bitcast.5, bf16[8,128,128]{1,2,0:T(8,128)(2,1)S(1)} %select_convert_fusion, bf16[8,128,512]{1,2,0:T(8,128)(2,1)S(1)} %get-tuple-element.26, bf16[8,128,512]{1,2,0:T(8,128)(2,1)S(1)} %get-tuple-element.25), kind=kOutput, calls=%fused_computation.31 | convolution fusion | flops 4838916096 | bytes 15990784 | tf_op jit(solution)/shard_map/abrcp,acq->brpq/dot_general | solution.py:262
  77.5 8.3 %shard_map.46 = f32[2,2,16,512]{3,2,1,0:T(8,128)S(1)} custom-call(f32[16,128,1152]{2,1,0:T(8,128)S(1)} %convolution_bitcast_fusion.y_ref, f32[16,128,1025]{2,1,0:T(8,128)} %get-tuple-element.7.lc_ref.uc_ref, f32[16,128,1025]{2,1,0:T(8,128)} %get-tuple-element.8.ls_ref.us_ref, f32[16,128,1025]{2,1,0:T(8,128)} %get-tuple-element.7.lc_ref.uc_ref, ...), custom_call_target="tpu_custom_call" | custom-call | tf_op jit(solution)/shard_map/pallas_call | solution.py:226
  87.1 0.6 broadcast_in_dim.44
  87.8 0.8 copy.28
  88.6 4.1 %all-to-all-start.1 = ((f32[16,1,2176]{2,1,0:T(1,128)}), f32[16,1,2176]{2,1,0:T(1,128)S(1)}, u32[]{:S(2)}, u32[]{:S(2)}) async-start(f32[16,1,2176]{2,1,0:T(1,128)} %copy.28), calls=%async_computation.1 | async-start | bytes 278528 | tf_op jit(solution)/shard_map/all_to_all | solution.py:325
  92.8 5.2 %fusion.46 = (f32[1025,160]{1,0:T(8,128)S(1)}, f32[1025,160]{1,0:T(8,128)}) fusion(s32[160]{0:T(256)S(1)} %and_select_fusion, s32[1025]{0:T(1024)S(1)} %pad_add_fusion), kind=kLoop, calls=%fused_computation.100 | loop fusion | flops 2460000 | bytes 1316740 | tf_op jit(solution)/shard_map/cos | solution.py:323
  98.0 3.0 %all-to-all-done.1 = f32[16,1,2176]{2,1,0:T(1,128)S(1)} async-done(((f32[16,1,2176]{2,1,0:T(1,128)}), f32[16,1,2176]{2,1,0:T(1,128)S(1)}, u32[]{:S(2)}, u32[]{:S(2)}) %all-to-all-start.1) | async-done | bytes 139296 | tf_op jit(solution)/shard_map/all_to_all | solution.py:325
  101.1 0.7 broadcast_in_dim.72
  101.8 4.4 %all-to-all-start.2 = ((f32[8,1,2176]{2,1,0:T(1,128)}), f32[8,1,2176]{2,1,0:T(1,128)S(1)}, u32[]{:S(2)}, u32[]{:S(2)}) async-start(f32[8,1,2176]{2,1,0:T(1,128)} %broadcast_in_dim.72), calls=%async_computation.2 | async-start | bytes 139264 | tf_op jit(solution)/shard_map/all_to_all | solution.py:328
  106.2 1.4 %pad_maximum_fusion = f32[2050,160]{1,0:T(8,128)S(1)} fusion(f32[1025,160]{1,0:T(8,128)} %get-tuple-element.20, f32[1025,160]{1,0:T(8,128)S(1)} %get-tuple-element.19), kind=kLoop, calls=%fused_computation.57 | loop fusion | flops 328000 | bytes 2624000 | tf_op jit(solution)/shard_map/concatenate | solution.py:323
  107.6 5.0 %all-to-all-done.2 = f32[8,1,2176]{2,1,0:T(1,128)S(1)} async-done(((f32[8,1,2176]{2,1,0:T(1,128)}), f32[8,1,2176]{2,1,0:T(1,128)S(1)}, u32[]{:S(2)}, u32[]{:S(2)}) %all-to-all-start.2) | async-done | bytes 69664 | tf_op jit(solution)/shard_map/all_to_all | solution.py:328
  112.6 0.6 slice.223
  113.8 0.9 fusion.52
  114.8 0.6 divide_multiply_fusion
  (41 shorter events, 2.2 us)
Async XLA Ops:
  6.4 11.8 %copy-start.2 = (s32[128]{0:T(128)S(1)}, s32[128]{0:T(128)}, u32[]{:S(2)}) copy-start(s32[128]{0:T(128)} %param.6) | copy-start | bytes 1540
  6.4 11.8 %copy-start.1 = (s32[128,2]{0,1:T(2,128)S(1)}, s32[128,2]{0,1:T(2,128)}, u32[]{:S(2)}) copy-start(s32[128,2]{0,1:T(2,128)} %param.5) | copy-start | bytes 3076
  6.4 11.9 %copy-start = (f32[2]{0:T(128)S(1)}, f32[2]{0:T(128)}, u32[]{:S(2)}) copy-start(f32[2]{0:T(128)} %param.7) | copy-start | bytes 28
  6.4 63.4 %all-to-all-start = ((bf16[128,128,128]{1,2,0:T(8,128)(2,1)}), bf16[128,128,128]{1,2,0:T(8,128)(2,1)}, u32[]{:S(2)}, u32[]{:S(2)}) async-start(bf16[128,128,128]{1,2,0:T(8,128)(2,1)} %bitcast.61), calls=%async_computation | async-start | bytes 8388608 | tf_op jit(solution)/shard_map/all_to_all | solution.py:252
  88.6 12.4 %all-to-all-start.1 = ((f32[16,1,2176]{2,1,0:T(1,128)}), f32[16,1,2176]{2,1,0:T(1,128)S(1)}, u32[]{:S(2)}, u32[]{:S(2)}) async-start(f32[16,1,2176]{2,1,0:T(1,128)} %copy.28), calls=%async_computation.1 | async-start | bytes 278528 | tf_op jit(solution)/shard_map/all_to_all | solution.py:325
  101.8 10.8 %all-to-all-start.2 = ((f32[8,1,2176]{2,1,0:T(1,128)}), f32[8,1,2176]{2,1,0:T(1,128)S(1)}, u32[]{:S(2)}, u32[]{:S(2)}) async-start(f32[8,1,2176]{2,1,0:T(1,128)} %broadcast_in_dim.72), calls=%async_computation.2 | async-start | bytes 139264 | tf_op jit(solution)/shard_map/all_to_all | solution.py:328

commit v13 on v11

--- a/solution.py
+++ b/solution.py
@@ -174,6 +174,12 @@
                 twisted[b, s1] = (gr, gi)
             elif k == 4:
                 twisted[b, s1] = (gi, -gr)
+            elif k == 2:
+                half_root = math.sqrt(0.5)
+                twisted[b, s1] = ((gr + gi) * half_root, (gi - gr) * half_root)
+            elif k == 6:
+                half_root = math.sqrt(0.5)
+                twisted[b, s1] = ((gi - gr) * half_root, -(gi + gr) * half_root)
             else:
                 c = math.cos(TWO_PI * k / 16)
                 d = math.sin(TWO_PI * k / 16)

time: 116 us -> 116 us (level)
  no operation moved by 1% of the time
where the time goes in v13:
time: 116 us
  waiting for transfers between devices  31.2 us (27%)
  other arithmetic  30 us (26%)
  starting transfers between devices  20.2 us (17%)
  local copies, waits for them, and re-layouts  13.5 us (12%)
  matrix products  9.32 us (8%)
  Pallas kernels  8.49 us (7%)
  between operations  2.88 us (2%)
    all_to_all x1, waiting for transfers between devices, local(): lax.all_to_all(blocks, ('scan', 'det'), split_axis=0, concat_axis=0, tile...  23.2 us
    mul x1, other arithmetic, local(): turn_sin * weights[None, :, None] * keep[None, None, :]  16.5 us
    all_to_all x1, starting transfers between devices, local(): lax.all_to_all(blocks, ('scan', 'det'), split_axis=0, concat_axis=0, tile...  11.7 us
    pallas_call x1, Pallas kernels, spectrum(): pl.pallas_call(spectrum_kernel, grid=(steps,), in_specs=[pl.BlockSpec(mem...  8.49 us
    dot_general x1, matrix products, local(): jnp.einsum('abrcp,acq->brpq', images, table.reshape(scan_size, tile, tabl...  7.44 us
    unnamed x7, local copies, waits for them, and re-layouts  6.41 us
    cos x1, other arithmetic, local(): jnp.cos(col_angles)  5.25 us
    all_to_all x1, waiting for transfers between devices, local(): gathered = lax.all_to_all(spread, 'scan', 0, 0, tiled=True)  4.97 us
  transfers between devices with their start and end apart: 3, of which 3 were waited for; matrix products, arithmetic and copies ran while one was open for 29% of the time, Pallas kernels for 0%

profile of v13, /device:TPU:0, one launch (start us, length us, event | category | flops | bytes accessed | tf_op | source)
XLA Modules:
  0.0 115.6 jit_solution(14105668229894960314)
XLA Ops:
  0.0 6.4 %copy.22 = bf16[1,128,16384]{1,2,0:T(8,128)(2,1)} copy(bf16[1,128,16384]{2,1,0:T(8,128)(2,1)} %param.4) | data formatting | bytes 8388608 | tf_op args[0]
  6.4 11.7 %all-to-all-start = ((bf16[128,128,128]{1,2,0:T(8,128)(2,1)}), bf16[128,128,128]{1,2,0:T(8,128)(2,1)}, u32[]{:S(2)}, u32[]{:S(2)}) async-start(bf16[128,128,128]{1,2,0:T(8,128)(2,1)} %bitcast.61), calls=%async_computation | async-start | bytes 8388608 | tf_op jit(solution)/shard_map/all_to_all | solution.py:258
  18.3 0.6 fusion.112
  20.9 0.5 fusion.44
  21.4 16.5 %fusion.12 = (f32[16,128,1025]{2,1,0:T(8,128)}, f32[16,128,1025]{2,1,0:T(8,128)}) fusion(f32[1025]{0:T(1024)S(1)} %fusion.86, f32[128]{0:T(128)S(1)} %convert_element_type.142, f32[128,1025]{1,0:T(8,128)S(1)} %get-tuple-element.24, f32[16,128]{1,0:T(8,128)S(1)} %get-tuple-element.32, f32[]{:T(128)} %bitcast.10, f32[128,1025]{1,0:T(8,128)S(1)} %get-tuple-element.23, ...), kind=kLoop, calls=%fused_computation.21 | loop fusion | flops 100761600 | bytes 17864200 | tf_op jit(solution)/shard_map/mul | solution.py:292
  37.9 0.6 convert_reduce_fusion
  38.7 1.6 %slice_reduce_fusion.1 = f32[16,128]{1,0:T(8,128)S(1)} fusion(f32[16,128,1025]{2,1,0:T(8,128)} %get-tuple-element.8.ls_ref.us_ref), kind=kLoop, calls=%fused_computation.90 | loop fusion | bytes 16384 | tf_op jit(solution)/shard_map/slice | solution.py:300
  40.2 1.6 %slice_reduce_fusion.2 = f32[16,128]{1,0:T(8,128)S(1)} fusion(f32[16,128,1025]{2,1,0:T(8,128)} %get-tuple-element.7.lc_ref.uc_ref), kind=kLoop, calls=%fused_computation.91 | loop fusion | bytes 16384 | tf_op jit(solution)/shard_map/slice | solution.py:299
  41.9 4.6 %fusion.33 = (bf16[8,128,512]{1,2,0:T(8,128)(2,1)S(1)}, bf16[8,128,512]{1,2,0:T(8,128)(2,1)S(1)}) fusion(s32[512]{0:T(512)S(1)} %slice.150, s32[8,128]{1,0:T(8,128)S(1)} %multiply_add_fusion), kind=kLoop, calls=%fused_computation.68 | loop fusion | flops 34078720 | bytes 2103296 | tf_op jit(solution)/shard_map/convert
  46.6 23.2 %all-to-all-done = bf16[128,128,128]{1,2,0:T(8,128)(2,1)} async-done(((bf16[128,128,128]{1,2,0:T(8,128)(2,1)}), bf16[128,128,128]{1,2,0:T(8,128)(2,1)}, u32[]{:S(2)}, u32[]{:S(2)}) %all-to-all-start) | async-done | bytes 4194336 | tf_op jit(solution)/shard_map/all_to_all | solution.py:258
  69.8 7.4 %convolution_bitcast_fusion.y_ref = f32[16,128,1152]{2,1,0:T(8,128)S(1)} fusion(bf16[8,16,128,128]{2,3,1,0:T(8,128)(2,1)} %bitcast.5, bf16[8,128,128]{1,2,0:T(8,128)(2,1)S(1)} %select_convert_fusion, bf16[8,128,512]{1,2,0:T(8,128)(2,1)S(1)} %get-tuple-element.26, bf16[8,128,512]{1,2,0:T(8,128)(2,1)S(1)} %get-tuple-element.25), kind=kOutput, calls=%fused_computation.31 | convolution fusion | flops 4838916096 | bytes 15990784 | tf_op jit(solution)/shard_map/abrcp,acq->brpq/dot_general | solution.py:268
  77.5 8.5 %shard_map.46 = f32[2,2,16,512]{3,2,1,0:T(8,128)S(1)} custom-call(f32[16,128,1152]{2,1,0:T(8,128)S(1)} %convolution_bitcast_fusion.y_ref, f32[16,128,1025]{2,1,0:T(8,128)} %get-tuple-element.7.lc_ref.uc_ref, f32[16,128,1025]{2,1,0:T(8,128)} %get-tuple-element.8.ls_ref.us_ref, f32[16,128,1025]{2,1,0:T(8,128)} %get-tuple-element.7.lc_ref.uc_ref, ...), custom_call_target="tpu_custom_call" | custom-call | tf_op jit(solution)/shard_map/pallas_call | solution.py:232
  87.2 0.6 broadcast_in_dim.44
  88.0 0.8 copy.28
  88.8 4.1 %all-to-all-start.1 = ((f32[16,1,2176]{2,1,0:T(1,128)}), f32[16,1,2176]{2,1,0:T(1,128)S(1)}, u32[]{:S(2)}, u32[]{:S(2)}) async-start(f32[16,1,2176]{2,1,0:T(1,128)} %copy.28), calls=%async_computation.1 | async-start | bytes 278528 | tf_op jit(solution)/shard_map/all_to_all | solution.py:331
  92.9 5.2 %fusion.46 = (f32[1025,160]{1,0:T(8,128)S(1)}, f32[1025,160]{1,0:T(8,128)}) fusion(s32[160]{0:T(256)S(1)} %and_select_fusion, s32[1025]{0:T(1024)S(1)} %pad_add_fusion), kind=kLoop, calls=%fused_computation.100 | loop fusion | flops 2460000 | bytes 1316740 | tf_op jit(solution)/shard_map/cos | solution.py:329
  98.2 3.0 %all-to-all-done.1 = f32[16,1,2176]{2,1,0:T(1,128)S(1)} async-done(((f32[16,1,2176]{2,1,0:T(1,128)}), f32[16,1,2176]{2,1,0:T(1,128)S(1)}, u32[]{:S(2)}, u32[]{:S(2)}) %all-to-all-start.1) | async-done | bytes 139296 | tf_op jit(solution)/shard_map/all_to_all | solution.py:331
  101.3 0.7 broadcast_in_dim.72
  101.9 4.4 %all-to-all-start.2 = ((f32[8,1,2176]{2,1,0:T(1,128)}), f32[8,1,2176]{2,1,0:T(1,128)S(1)}, u32[]{:S(2)}, u32[]{:S(2)}) async-start(f32[8,1,2176]{2,1,0:T(1,128)} %broadcast_in_dim.72), calls=%async_computation.2 | async-start | bytes 139264 | tf_op jit(solution)/shard_map/all_to_all | solution.py:334
  106.3 1.4 %pad_maximum_fusion = f32[2050,160]{1,0:T(8,128)S(1)} fusion(f32[1025,160]{1,0:T(8,128)} %get-tuple-element.20, f32[1025,160]{1,0:T(8,128)S(1)} %get-tuple-element.19), kind=kLoop, calls=%fused_computation.57 | loop fusion | flops 328000 | bytes 2624000 | tf_op jit(solution)/shard_map/concatenate | solution.py:329
  107.7 5.0 %all-to-all-done.2 = f32[8,1,2176]{2,1,0:T(1,128)S(1)} async-done(((f32[8,1,2176]{2,1,0:T(1,128)}), f32[8,1,2176]{2,1,0:T(1,128)S(1)}, u32[]{:S(2)}, u32[]{:S(2)}) %all-to-all-start.2) | async-done | bytes 69664 | tf_op jit(solution)/shard_map/all_to_all | solution.py:334
  112.7 0.6 slice.223
  114.0 0.9 fusion.52
  114.9 0.6 divide_multiply_fusion
  (41 shorter events, 2.2 us)
Async XLA Ops:
  6.4 11.8 %copy-start.2 = (s32[128]{0:T(128)S(1)}, s32[128]{0:T(128)}, u32[]{:S(2)}) copy-start(s32[128]{0:T(128)} %param.6) | copy-start | bytes 1540
  6.4 11.8 %copy-start.1 = (s32[128,2]{0,1:T(2,128)S(1)}, s32[128,2]{0,1:T(2,128)}, u32[]{:S(2)}) copy-start(s32[128,2]{0,1:T(2,128)} %param.5) | copy-start | bytes 3076
  6.4 11.9 %copy-start = (f32[2]{0:T(128)S(1)}, f32[2]{0:T(128)}, u32[]{:S(2)}) copy-start(f32[2]{0:T(128)} %param.7) | copy-start | bytes 28
  6.4 63.4 %all-to-all-start = ((bf16[128,128,128]{1,2,0:T(8,128)(2,1)}), bf16[128,128,128]{1,2,0:T(8,128)(2,1)}, u32[]{:S(2)}, u32[]{:S(2)}) async-start(bf16[128,128,128]{1,2,0:T(8,128)(2,1)} %bitcast.61), calls=%async_computation | async-start | bytes 8388608 | tf_op jit(solution)/shard_map/all_to_all | solution.py:258
  88.8 12.4 %all-to-all-start.1 = ((f32[16,1,2176]{2,1,0:T(1,128)}), f32[16,1,2176]{2,1,0:T(1,128)S(1)}, u32[]{:S(2)}, u32[]{:S(2)}) async-start(f32[16,1,2176]{2,1,0:T(1,128)} %copy.28), calls=%async_computation.1 | async-start | bytes 278528 | tf_op jit(solution)/shard_map/all_to_all | solution.py:331
  101.9 10.7 %all-to-all-start.2 = ((f32[8,1,2176]{2,1,0:T(1,128)}), f32[8,1,2176]{2,1,0:T(1,128)S(1)}, u32[]{:S(2)}, u32[]{:S(2)}) async-start(f32[8,1,2176]{2,1,0:T(1,128)} %broadcast_in_dim.72), calls=%async_computation.2 | async-start | bytes 139264 | tf_op jit(solution)/shard_map/all_to_all | solution.py:334

commit v14 on v12

--- a/solution.py
+++ b/solution.py
@@ -210,7 +210,7 @@
             acc_ref[1, 1, s] += gr * ts - gi * tc
         return carry
 
-    lax.fori_loop(0, lc_ref.shape[1] // 8, body, 0, unroll=4)
+    lax.fori_loop(0, lc_ref.shape[1] // 8, body, 0, unroll=8)
     for a in range(2):
         for b in range(2):
             out_ref[a, b] = jnp.sum(acc_ref[a, b], axis=1)

time: 116 us -> 116 us (level)
  no operation moved by 1% of the time
where the time goes in v14:
time: 116 us; the launch traced here: 115 us
  waiting for transfers between devices  31.2 us (27%)
  other arithmetic  30 us (26%)
  starting transfers between devices  20.2 us (17%)
  local copies, waits for them, and re-layouts  13.5 us (12%)
  matrix products  9.33 us (8%)
  Pallas kernels  8.31 us (7%)
  between operations  2.88 us (2%)
    all_to_all x1, waiting for transfers between devices, local(): lax.all_to_all(blocks, ('scan', 'det'), split_axis=0, concat_axis=0, tile...  23.2 us
    mul x1, other arithmetic, local(): turn_sin * weights[None, :, None] * keep[None, None, :]  16.5 us
    all_to_all x1, starting transfers between devices, local(): lax.all_to_all(blocks, ('scan', 'det'), split_axis=0, concat_axis=0, tile...  11.7 us
    pallas_call x1, Pallas kernels, spectrum(): pl.pallas_call(spectrum_kernel, grid=(steps,), in_specs=[pl.BlockSpec(mem...  8.31 us
    dot_general x1, matrix products, local(): jnp.einsum('abrcp,acq->brpq', images, table.reshape(scan_size, tile, tabl...  7.45 us
    unnamed x7, local copies, waits for them, and re-layouts  6.41 us
    cos x1, other arithmetic, local(): jnp.cos(col_angles)  5.25 us
    all_to_all x1, waiting for transfers between devices, local(): gathered = lax.all_to_all(spread, 'scan', 0, 0, tiled=True)  4.97 us
  transfers between devices with their start and end apart: 3, of which 3 were waited for; matrix products, arithmetic and copies ran while one was open for 29% of the time, Pallas kernels for 0%

profile of v14, /device:TPU:0, one launch (start us, length us, event | category | flops | bytes accessed | tf_op | source)
XLA Modules:
  0.0 115.4 jit_solution(5232542587890585075)
XLA Ops:
  0.0 6.4 %copy.22 = bf16[1,128,16384]{1,2,0:T(8,128)(2,1)} copy(bf16[1,128,16384]{2,1,0:T(8,128)(2,1)} %param.4) | data formatting | bytes 8388608 | tf_op args[0]
  6.4 11.7 %all-to-all-start = ((bf16[128,128,128]{1,2,0:T(8,128)(2,1)}), bf16[128,128,128]{1,2,0:T(8,128)(2,1)}, u32[]{:S(2)}, u32[]{:S(2)}) async-start(bf16[128,128,128]{1,2,0:T(8,128)(2,1)} %bitcast.61), calls=%async_computation | async-start | bytes 8388608 | tf_op jit(solution)/shard_map/all_to_all | solution.py:252
  18.3 0.6 fusion.112
  20.9 0.5 fusion.44
  21.4 16.5 %fusion.12 = (f32[16,128,1025]{2,1,0:T(8,128)}, f32[16,128,1025]{2,1,0:T(8,128)}) fusion(f32[1025]{0:T(1024)S(1)} %fusion.86, f32[128]{0:T(128)S(1)} %convert_element_type.142, f32[128,1025]{1,0:T(8,128)S(1)} %get-tuple-element.24, f32[16,128]{1,0:T(8,128)S(1)} %get-tuple-element.32, f32[]{:T(128)} %bitcast.10, f32[128,1025]{1,0:T(8,128)S(1)} %get-tuple-element.23, ...), kind=kLoop, calls=%fused_computation.21 | loop fusion | flops 100761600 | bytes 17864200 | tf_op jit(solution)/shard_map/mul | solution.py:286
  37.9 0.6 convert_reduce_fusion
  38.7 1.6 %slice_reduce_fusion.1 = f32[16,128]{1,0:T(8,128)S(1)} fusion(f32[16,128,1025]{2,1,0:T(8,128)} %get-tuple-element.8.ls_ref.us_ref), kind=kLoop, calls=%fused_computation.90 | loop fusion | bytes 16384 | tf_op jit(solution)/shard_map/slice | solution.py:294
  40.2 1.6 %slice_reduce_fusion.2 = f32[16,128]{1,0:T(8,128)S(1)} fusion(f32[16,128,1025]{2,1,0:T(8,128)} %get-tuple-element.7.lc_ref.uc_ref), kind=kLoop, calls=%fused_computation.91 | loop fusion | bytes 16384 | tf_op jit(solution)/shard_map/slice | solution.py:293
  41.9 4.6 %fusion.33 = (bf16[8,128,512]{1,2,0:T(8,128)(2,1)S(1)}, bf16[8,128,512]{1,2,0:T(8,128)(2,1)S(1)}) fusion(s32[512]{0:T(512)S(1)} %slice.150, s32[8,128]{1,0:T(8,128)S(1)} %multiply_add_fusion), kind=kLoop, calls=%fused_computation.68 | loop fusion | flops 34078720 | bytes 2103296 | tf_op jit(solution)/shard_map/convert
  46.6 23.2 %all-to-all-done = bf16[128,128,128]{1,2,0:T(8,128)(2,1)} async-done(((bf16[128,128,128]{1,2,0:T(8,128)(2,1)}), bf16[128,128,128]{1,2,0:T(8,128)(2,1)}, u32[]{:S(2)}, u32[]{:S(2)}) %all-to-all-start) | async-done | bytes 4194336 | tf_op jit(solution)/shard_map/all_to_all | solution.py:252
  69.8 7.4 %convolution_bitcast_fusion.y_ref = f32[16,128,1152]{2,1,0:T(8,128)S(1)} fusion(bf16[8,16,128,128]{2,3,1,0:T(8,128)(2,1)} %bitcast.5, bf16[8,128,128]{1,2,0:T(8,128)(2,1)S(1)} %select_convert_fusion, bf16[8,128,512]{1,2,0:T(8,128)(2,1)S(1)} %get-tuple-element.26, bf16[8,128,512]{1,2,0:T(8,128)(2,1)S(1)} %get-tuple-element.25), kind=kOutput, calls=%fused_computation.31 | convolution fusion | flops 4838916096 | bytes 15990784 | tf_op jit(solution)/shard_map/abrcp,acq->brpq/dot_general | solution.py:262
  77.6 8.3 %shard_map.46 = f32[2,2,16,512]{3,2,1,0:T(8,128)S(1)} custom-call(f32[16,128,1152]{2,1,0:T(8,128)S(1)} %convolution_bitcast_fusion.y_ref, f32[16,128,1025]{2,1,0:T(8,128)} %get-tuple-element.7.lc_ref.uc_ref, f32[16,128,1025]{2,1,0:T(8,128)} %get-tuple-element.8.ls_ref.us_ref, f32[16,128,1025]{2,1,0:T(8,128)} %get-tuple-element.7.lc_ref.uc_ref, ...), custom_call_target="tpu_custom_call" | custom-call | tf_op jit(solution)/shard_map/pallas_call | solution.py:226
  87.1 0.6 broadcast_in_dim.44
  87.8 0.8 copy.28
  88.6 4.1 %all-to-all-start.1 = ((f32[16,1,2176]{2,1,0:T(1,128)}), f32[16,1,2176]{2,1,0:T(1,128)S(1)}, u32[]{:S(2)}, u32[]{:S(2)}) async-start(f32[16,1,2176]{2,1,0:T(1,128)} %copy.28), calls=%async_computation.1 | async-start | bytes 278528 | tf_op jit(solution)/shard_map/all_to_all | solution.py:325
  92.8 5.2 %fusion.46 = (f32[1025,160]{1,0:T(8,128)S(1)}, f32[1025,160]{1,0:T(8,128)}) fusion(s32[160]{0:T(256)S(1)} %and_select_fusion, s32[1025]{0:T(1024)S(1)} %pad_add_fusion), kind=kLoop, calls=%fused_computation.100 | loop fusion | flops 2460000 | bytes 1316740 | tf_op jit(solution)/shard_map/cos | solution.py:323
  98.0 3.0 %all-to-all-done.1 = f32[16,1,2176]{2,1,0:T(1,128)S(1)} async-done(((f32[16,1,2176]{2,1,0:T(1,128)}), f32[16,1,2176]{2,1,0:T(1,128)S(1)}, u32[]{:S(2)}, u32[]{:S(2)}) %all-to-all-start.1) | async-done | bytes 139296 | tf_op jit(solution)/shard_map/all_to_all | solution.py:325
  101.1 0.7 broadcast_in_dim.72
  101.8 4.4 %all-to-all-start.2 = ((f32[8,1,2176]{2,1,0:T(1,128)}), f32[8,1,2176]{2,1,0:T(1,128)S(1)}, u32[]{:S(2)}, u32[]{:S(2)}) async-start(f32[8,1,2176]{2,1,0:T(1,128)} %broadcast_in_dim.72), calls=%async_computation.2 | async-start | bytes 139264 | tf_op jit(solution)/shard_map/all_to_all | solution.py:328
  106.2 1.4 %pad_maximum_fusion = f32[2050,160]{1,0:T(8,128)S(1)} fusion(f32[1025,160]{1,0:T(8,128)} %get-tuple-element.20, f32[1025,160]{1,0:T(8,128)S(1)} %get-tuple-element.19), kind=kLoop, calls=%fused_computation.57 | loop fusion | flops 328000 | bytes 2624000 | tf_op jit(solution)/shard_map/concatenate | solution.py:323
  107.5 5.0 %all-to-all-done.2 = f32[8,1,2176]{2,1,0:T(1,128)S(1)} async-done(((f32[8,1,2176]{2,1,0:T(1,128)}), f32[8,1,2176]{2,1,0:T(1,128)S(1)}, u32[]{:S(2)}, u32[]{:S(2)}) %all-to-all-start.2) | async-done | bytes 69664 | tf_op jit(solution)/shard_map/all_to_all | solution.py:328
  112.6 0.6 slice.223
  113.8 0.9 fusion.52
  114.8 0.6 divide_multiply_fusion
  (41 shorter events, 2.2 us)
Async XLA Ops:
  6.4 11.8 %copy-start.2 = (s32[128]{0:T(128)S(1)}, s32[128]{0:T(128)}, u32[]{:S(2)}) copy-start(s32[128]{0:T(128)} %param.6) | copy-start | bytes 1540
  6.4 11.8 %copy-start.1 = (s32[128,2]{0,1:T(2,128)S(1)}, s32[128,2]{0,1:T(2,128)}, u32[]{:S(2)}) copy-start(s32[128,2]{0,1:T(2,128)} %param.5) | copy-start | bytes 3076
  6.4 11.9 %copy-start = (f32[2]{0:T(128)S(1)}, f32[2]{0:T(128)}, u32[]{:S(2)}) copy-start(f32[2]{0:T(128)} %param.7) | copy-start | bytes 28
  6.4 63.4 %all-to-all-start = ((bf16[128,128,128]{1,2,0:T(8,128)(2,1)}), bf16[128,128,128]{1,2,0:T(8,128)(2,1)}, u32[]{:S(2)}, u32[]{:S(2)}) async-start(bf16[128,128,128]{1,2,0:T(8,128)(2,1)} %bitcast.61), calls=%async_computation | async-start | bytes 8388608 | tf_op jit(solution)/shard_map/all_to_all | solution.py:252
  88.6 12.4 %all-to-all-start.1 = ((f32[16,1,2176]{2,1,0:T(1,128)}), f32[16,1,2176]{2,1,0:T(1,128)S(1)}, u32[]{:S(2)}, u32[]{:S(2)}) async-start(f32[16,1,2176]{2,1,0:T(1,128)} %copy.28), calls=%async_computation.1 | async-start | bytes 278528 | tf_op jit(solution)/shard_map/all_to_all | solution.py:325
  101.8 10.8 %all-to-all-start.2 = ((f32[8,1,2176]{2,1,0:T(1,128)}), f32[8,1,2176]{2,1,0:T(1,128)S(1)}, u32[]{:S(2)}, u32[]{:S(2)}) async-start(f32[8,1,2176]{2,1,0:T(1,128)} %broadcast_in_dim.72), calls=%async_computation.2 | async-start | bytes 139264 | tf_op jit(solution)/shard_map/all_to_all | solution.py:328
